TPU v7x, 32 devices: a whole 2x2x4 slice. The times are simulated.
32 devices in a mesh: groups: 2 (over x), section: 16 (over z, y, core).
Axes of the slice: x: 2, y: 2, z: 4, core: 2. Of those that a mesh axis runs over, the one named last changes fastest.
Arguments:
- section_input: bfloat16 [32, 128, 4096], P(('groups', 'section')), parts along dimension 0, may hold values from -6 to 6
- stash: bfloat16 [32, 128, 4096], P(('groups', 'section')), parts along dimension 0, may hold values from -6 to 6
- cotangent: bfloat16 [32, 128, 4096], P(('groups', 'section')), parts along dimension 0, may hold values from -6 to 6
- norm_gain: float32 [16, 4096], P('section'), may hold values from 0.1 to 1.9
- w_query: bfloat16 [16, 4096, 256], P('section'), may hold values from -0.09375 to 0.09375
- w_kv: bfloat16 [16, 4096, 256], P('section'), may hold values from -0.09375 to 0.09375
- w_out: bfloat16 [16, 256, 4096], P('section'), may hold values from -0.375 to 0.375
- doc_ids: int32 [32, 2, 128], P(('groups', 'section')), parts along dimension 0, may hold values from 0 to 7, never falling along the last dimension, each value on 1 to 64 neighbouring positions
Outputs:
- forwarded: bfloat16 [32, 128, 4096], P(('groups', 'section')), parts along dimension 0
- returned: bfloat16 [32, 128, 4096], P(('groups', 'section')), parts along dimension 0
There are 2 independent parts, one for each index of `groups`. A program takes and returns all parts, laid end to end along the dimension named above; an argument that names none is the same for every part. Nothing has to cross between parts.
Inputs may be any that keep to these rules, and one draw needn't show every extreme that they name: `doc_ids`: ids never fall along a row; each document holds 1 to 64 tokens and one holds exactly that many.
All inputs are finite; a program needn't handle non-finite values.
Results may differ from a plain program's by a relative error of at most 0.01.
Values may be sent and summed in bfloat16 or wider, within the bound.
No kernel may reach another device: no remote copies, remote signals or barrier semaphores. Data moves between devices by JAX's collectives and lax.ppermute only.
A program may use at most 64 MiB of HBM per device.

v0:
```python
import math

import jax
import jax.numpy as jnp
from jax import lax
from jax.sharding import PartitionSpec as P


def shifted(value, axis, steps):
    count = lax.axis_size(axis)
    leading, last = (max(0, -steps), min(count, count - steps))
    return lax.ppermute(value, axis, [(source, source + steps) for source in range(leading, last)])


def rotary_tables(segment, head_dim):
    index = jnp.arange(segment.shape[0], dtype=jnp.int32)
    first = jnp.concatenate([jnp.ones((1,), dtype=bool), segment[1:] != segment[:-1]])
    starts = jnp.where(first, index, jnp.zeros_like(index))
    places = (index - lax.cummax(starts, axis=0)).astype(jnp.float32)
    half = head_dim // 2
    freqs = 500000.0 ** (-(jnp.arange(half, dtype=jnp.float32) * 2.0 / head_dim))
    angles = places[:, None] * freqs[None, :]
    cosine = jnp.concatenate([jnp.cos(angles), jnp.cos(angles)], -1)
    sine_part = jnp.concatenate([jnp.sin(angles), jnp.sin(angles)], -1)
    return (cosine, sine_part)


def rotary(block, cosine, sine_part):
    half = block.shape[-1] // 2
    turned = jnp.concatenate([-block[..., half:], block[..., :half]], -1)
    return block * cosine + turned * sine_part


def section_layer(acts, gain, w_query, w_kv, w_out, segment):
    rows = acts.shape[0]
    head_dim = w_kv.shape[1] // 2
    heads = w_query.shape[1] // head_dim
    values32 = acts.astype(jnp.float32)
    scale = lax.rsqrt(jnp.mean(values32 * values32, axis=-1, keepdims=True) + 1e-05)
    normed = (values32 * scale * gain).astype(jnp.bfloat16)
    query = jnp.dot(normed, w_query, preferred_element_type=jnp.float32).reshape(
        rows, heads, head_dim
    )
    keyval = jnp.dot(normed, w_kv, preferred_element_type=jnp.float32)
    cosine, sine_part = rotary_tables(segment, head_dim)
    query = rotary(query, cosine[:, None, :], sine_part[:, None, :]).astype(jnp.bfloat16)
    keys = rotary(keyval[:, :head_dim], cosine, sine_part).astype(jnp.bfloat16)
    values = keyval[:, head_dim:].astype(jnp.bfloat16)
    scores = jnp.einsum("qhd,kd->hqk", query, keys, preferred_element_type=jnp.float32) / math.sqrt(
        head_dim
    )
    index = jnp.arange(rows, dtype=jnp.int32)
    allowed = (segment[:, None] == segment[None, :]) & (index[None, :] <= index[:, None])
    expd = jnp.where(allowed[None], jnp.exp(scores), jnp.zeros_like(scores))
    probs = (expd / jnp.sum(expd, axis=-1, keepdims=True)).astype(jnp.bfloat16)
    mixed = jnp.einsum("hqk,kd->qhd", probs, values, preferred_element_type=jnp.float32)
    mixed = mixed.astype(jnp.bfloat16).reshape(rows, heads * head_dim)
    return (values32 + jnp.dot(mixed, w_out, preferred_element_type=jnp.float32)).astype(
        jnp.bfloat16
    )


def shards(section_input, stash, cotangent, norm_gain, w_query, w_kv, w_out, doc_ids):
    rows = stash.shape[1]
    width = stash.shape[2]
    pieces = lax.axis_size("section")
    local = stash[0].reshape(pieces, rows // pieces, width)
    spread = lax.all_to_all(local, "section", split_axis=0, concat_axis=0, tiled=True)
    spread = spread[::-1]
    collected = lax.all_to_all(spread, "section", split_axis=0, concat_axis=0, tiled=True)
    fetched = collected.reshape(rows, width)
    outward = section_layer(
        section_input[0], norm_gain[0], w_query[0], w_kv[0], w_out[0], doc_ids[0, 0]
    )

    def replay(acts):
        return section_layer(acts, norm_gain[0], w_query[0], w_kv[0], w_out[0], doc_ids[0, 1])

    unused, pullback = jax.vjp(replay, fetched)
    gradient = pullback(cotangent[0])[0]
    forwarded = shifted(outward[None], "section", 1)
    returned = shifted(gradient[None], "section", -1)
    return (forwarded, returned)


def solution(mesh):
    return jax.shard_map(
        shards,
        mesh=mesh,
        in_specs=(
            P(("groups", "section"), None, None),
            P(("groups", "section"), None, None),
            P(("groups", "section"), None, None),
            P("section", None),
            P("section", None, None),
            P("section", None, None),
            P("section", None, None),
            P(("groups", "section"), None, None),
        ),
        out_specs=(P(("groups", "section"), None, None), P(("groups", "section"), None, None)),
        check_vma=False,
    )
```

profile of v0, /device:TPU:9, one launch (start us, length us, event | category | flops | bytes accessed | tf_op | source)
XLA Modules:
  0.0 98.4 jit_solution(2156212359162217488)
XLA Ops:
  0.7 6.8 %all-to-all-start = ((bf16[16,8,4096]{2,1,0:T(8,128)(2,1)}), bf16[16,8,4096]{2,1,0:T(8,128)(2,1)S(1)}, u32[]{:S(2)}, u32[]{:S(2)}) async-start(bf16[16,8,4096]{2,1,0:T(8,128)(2,1)} %bitcast.152), calls=%async_computation | async-start | bytes 2097152 | tf_op jit(solution)/shard_map/all_to_all | solution.py:68
  7.4 0.6 slice_bitcast_fusion
  8.1 0.1 copy.27
  8.4 0.1 copy.28
  8.5 0.1 copy.36
  8.6 0.2 reduce-window.16
  8.8 0.2 reduce-window.17
  9.0 0.1 reduce.2
  9.2 0.9 multiply_cosine_fusion
  10.4 0.7 copy.30
  11.1 4.1 %copy.54 = bf16[256,4096]{1,0:T(8,128)(2,1)} copy(bf16[256,4096]{0,1:T(8,128)(2,1)} %bitcast.149) | data formatting | bytes 4194304 | tf_op jit(solution)/shard_map/dot_general | solution.py:41
  15.2 1.5 %fusion.8 = f32[128]{0:T(128)S(1)} fusion(bf16[1,128,4096]{2,1,0:T(8,128)(2,1)} %param.8), kind=kLoop, calls=%fused_computation.17 | loop fusion | flops 1572736 | bytes 1049088 | tf_op jit(solution)/shard_map/reduce_sum | solution.py:39
  16.8 0.6 copy-done.14
  17.4 1.7 %fusion.23 = f32[128,256]{1,0:T(8,128)S(1)} fusion(bf16[1,4096,256]{2,1,0:T(8,128)(2,1)S(1)} %copy-done, bf16[1,128,4096]{2,1,0:T(8,128)(2,1)} %param.8, f32[4096]{0:T(1024)} %bitcast.157, f32[128]{0:T(128)S(1)} %add_rsqrt_fusion), kind=kOutput, calls=%fused_computation.32 | convolution fusion | flops 270532608 | bytes 3293696 | tf_op jit(solution)/shard_map/dot_general | solution.py:44
  19.1 13.2 %all-to-all-done = bf16[16,8,4096]{2,1,0:T(8,128)(2,1)S(1)} async-done(((bf16[16,8,4096]{2,1,0:T(8,128)(2,1)}), bf16[16,8,4096]{2,1,0:T(8,128)(2,1)S(1)}, u32[]{:S(2)}, u32[]{:S(2)}) %all-to-all-start) | async-done | bytes 1048608 | tf_op jit(solution)/shard_map/all_to_all | solution.py:68
  32.3 1.0 %rev.3 = bf16[16,8,4096]{2,1,0:T(8,128)(2,1)} reverse(bf16[16,8,4096]{2,1,0:T(8,128)(2,1)S(1)} %all-to-all-done), dimensions={0} | reverse | bytes 2097152 | tf_op jit(solution)/shard_map/rev | solution.py:69
  33.3 5.0 %all-to-all-start.1 = ((bf16[16,8,4096]{2,1,0:T(8,128)(2,1)}), bf16[16,8,4096]{2,1,0:T(8,128)(2,1)S(1)}, u32[]{:S(2)}, u32[]{:S(2)}) async-start(bf16[16,8,4096]{2,1,0:T(8,128)(2,1)} %rev.3), calls=%async_computation.1 | async-start | bytes 2097152 | tf_op jit(solution)/shard_map/all_to_all | solution.py:70
  38.4 2.7 %fusion.42 = f32[128,2,128]{0,2,1:T(8,128)S(1)} fusion(bf16[2,128,4096]{2,1,0:T(8,128)(2,1)} %bitcast.150, bf16[1,128,4096]{2,1,0:T(8,128)(2,1)} %param.8, f32[4096]{0:T(1024)} %bitcast.158, f32[128]{0:T(128)} %copy-done.14), kind=kOutput, calls=%fused_computation.56 | convolution fusion | flops 270532608 | bytes 3293696 | tf_op jit(solution)/shard_map/dot_general | solution.py:41
  41.1 0.9 fusion.28
  42.1 1.2 %convolution_convert_fusion.3 = bf16[128,2,128]{2,0,1:T(8,128)(2,1)S(1)} fusion(f32[2,128,128]{1,2,0:T(8,128)} %fusion.28, f32[128,256]{1,0:T(8,128)S(1)} %fusion.23), kind=kOutput, calls=%fused_computation.43 | convolution fusion | flops 8487295 | bytes 360448 | tf_op jit(solution)/shard_map/hqk,kd->qhd/dot_general | solution.py:56
  43.2 3.3 %fusion.4 = bf16[1,128,4096]{2,1,0:T(8,128)(2,1)} fusion(bf16[128,256]{0,1:T(8,128)(2,1)S(1)} %bitcast.156, bf16[1,128,4096]{2,1,0:T(8,128)(2,1)} %param.8, bf16[1,256,4096]{2,1,0:T(8,128)(2,1)} %param.14), kind=kOutput, calls=%fused_computation.7 | convolution fusion | flops 270008320 | bytes 4259840 | tf_op jit(solution)/shard_map/dot_general | solution.py:58
  46.5 3.3 %collective-permute-start = (bf16[1,128,4096]{2,1,0:T(8,128)(2,1)}, bf16[1,128,4096]{2,1,0:T(8,128)(2,1)}, u32[]{:S(2)}, u32[]{:S(2)}) collective-permute-start(bf16[1,128,4096]{2,1,0:T(8,128)(2,1)} %fusion.4), channel_id=1, source_target_pairs={{0,1},{1,2},{2,3},{3,4},{4,5},{5,6},{6,7},{7,8},{8,9},{9,10},{10,1... | collective-permute-start | bytes 3145736 | tf_op jit(solution)/shard_map/ppermute | solution.py:12
  49.9 0.7 fusion.73
  50.6 0.1 copy.35
  50.7 2.8 %fusion.29 = bf16[128,256]{1,0:T(8,128)(2,1)S(1)} fusion(bf16[1,256,4096]{2,1,0:T(8,128)(2,1)} %param.14, bf16[1,128,4096]{2,1,0:T(8,128)(2,1)} %param.10), kind=kOutput, calls=%fused_computation.40 | convolution fusion | flops 268468224 | bytes 3211264 | tf_op jit(solution)/shard_map/transpose(jvp())/dot_general | solution.py:58
  53.5 0.1 copy.51
  53.6 10.5 %all-to-all-done.1 = bf16[16,8,4096]{2,1,0:T(8,128)(2,1)S(1)} async-done(((bf16[16,8,4096]{2,1,0:T(8,128)(2,1)}), bf16[16,8,4096]{2,1,0:T(8,128)(2,1)S(1)}, u32[]{:S(2)}, u32[]{:S(2)}) %all-to-all-start.1) | async-done | bytes 1048608 | tf_op jit(solution)/shard_map/all_to_all | solution.py:70
  64.1 0.3 fusion.12
  64.4 0.6 multiply_add_fusion
  65.0 0.5 fusion.21
  65.6 0.8 pad_maximum_fusion.2
  66.4 0.9 copy.39
  67.4 2.4 %fusion.38 = f32[128,2,128]{0,2,1:T(8,128)S(1)} fusion(bf16[2,128,4096]{2,1,0:T(8,128)(2,1)} %bitcast.151, bf16[16,8,4096]{2,1,0:T(8,128)(2,1)S(1)} %all-to-all-done.1, f32[4096]{0:T(1024)} %bitcast.159, f32[16,8]{1,0:T(8,128)} %copy-done.12), kind=kOutput, calls=%fused_computation.52 | convolution fusion | flops 270532608 | bytes 3293696 | tf_op jit(solution)/shard_map/jvp()/dot_general | solution.py:41
  69.9 0.2 fusion.60
  70.1 0.8 fusion.34
  70.9 0.2 multiply_reduce_fusion
  71.1 0.8 fusion.90
  71.9 0.9 broadcast_multiply_fusion
  72.8 0.8 add.56
  73.6 0.9 fusion.93
  74.6 2.4 %convolution_convert_fusion = bf16[128,4096]{1,0:T(8,128)(2,1)S(1)} fusion(bf16[128,256]{0,1:T(8,128)(2,1)S(1)} %bitcast.155, bf16[1,4096,256]{2,1,0:T(8,128)(2,1)} %param.12), kind=kOutput, calls=%fused_computation.2 | convolution fusion | flops 268435456 | bytes 3211264 | tf_op jit(solution)/shard_map/transpose(jvp())/dot_general | solution.py:41
  77.2 1.0 %fusion.11 = (f32[128]{0:T(128)S(1)}, f32[128,4096]{1,0:T(8,128)S(1)}) fusion(bf16[16,8,4096]{2,1,0:T(8,128)(2,1)S(1)} %all-to-all-done.1, f32[4096]{0:T(1024)S(1)} %bitcast.161, bf16[128,4096]{1,0:T(8,128)(2,1)S(1)} %convolution_convert_fusion, bf16[1,4096,256]{2,1,0:T(8,128)(2,1)S(1)} %copy-done, f32[128,128]{1,0:T(8,128)S(1)} %pad_add_fusion.1, ...), kind=kOutput, calls=%fused_computation.20 | convolution fusion | flops 272170880 | bytes 6406656 | tf_op jit(solution)/shard_map/transpose(jvp())/dot_general | solution.py:44
  78.2 0.2 copy-done.1
  78.4 0.6 fusion.37
  79.1 1.9 %collective-permute-start.1 = (bf16[1,128,4096]{2,1,0:T(8,128)(2,1)S(1)}, bf16[1,128,4096]{2,1,0:T(8,128)(2,1)S(1)}, u32[]{:S(2)}, u32[]{:S(2)}) collective-permute-start(bf16[1,128,4096]{2,1,0:T(8,128)(2,1)S(1)} %fusion.37), channel_id=1, source_target_pairs={{1,0},{2,1},{3,2},{4,3},{5,4},{6,5},{7,6},{8,7},{9,8},{10,9},{11,1... | collective-permute-start | bytes 3145736 | tf_op jit(solution)/shard_map/ppermute | solution.py:12
  81.0 14.2 %collective-permute-done.1 = bf16[1,128,4096]{2,1,0:T(8,128)(2,1)S(1)} collective-permute-done((bf16[1,128,4096]{2,1,0:T(8,128)(2,1)S(1)}, bf16[1,128,4096]{2,1,0:T(8,128)(2,1)S(1)}, u32[]{:S(2)}, u32[]{:S(2)}) %collective-permute-start.1) | collective-permute-done | bytes 1048608 | tf_op jit(solution)/shard_map/ppermute | solution.py:12
  95.2 2.3 %copy.57 = bf16[1,128,4096]{2,1,0:T(8,128)(2,1)} copy(bf16[1,128,4096]{2,1,0:T(8,128)(2,1)} %collective-permute-done) | data formatting | bytes 2097152
  97.5 1.0 copy.58
  (52 shorter events, 1.2 us)
Async XLA Ops:
  0.6 16.7 %copy-start = (bf16[1,4096,256]{2,1,0:T(8,128)(2,1)S(1)}, bf16[1,4096,256]{2,1,0:T(8,128)(2,1)}, u32[]{:S(2)}) copy-start(bf16[1,4096,256]{2,1,0:T(8,128)(2,1)} %param.13) | copy-start | bytes 6291460
  0.6 6.8 %copy-start.11 = (s32[1,2,128]{2,1,0:T(2,128)S(1)}, s32[1,2,128]{2,1,0:T(2,128)}, u32[]{:S(2)}) copy-start(s32[1,2,128]{2,1,0:T(2,128)} %param.15) | copy-start | bytes 3076
  0.7 31.6 %all-to-all-start = ((bf16[16,8,4096]{2,1,0:T(8,128)(2,1)}), bf16[16,8,4096]{2,1,0:T(8,128)(2,1)S(1)}, u32[]{:S(2)}, u32[]{:S(2)}) async-start(bf16[16,8,4096]{2,1,0:T(8,128)(2,1)} %bitcast.152), calls=%async_computation | async-start | bytes 2097152 | tf_op jit(solution)/shard_map/all_to_all | solution.py:68
  16.8 0.6 copy-start.14
  33.3 30.8 %all-to-all-start.1 = ((bf16[16,8,4096]{2,1,0:T(8,128)(2,1)}), bf16[16,8,4096]{2,1,0:T(8,128)(2,1)S(1)}, u32[]{:S(2)}, u32[]{:S(2)}) async-start(bf16[16,8,4096]{2,1,0:T(8,128)(2,1)} %rev.3), calls=%async_computation.1 | async-start | bytes 2097152 | tf_op jit(solution)/shard_map/all_to_all | solution.py:70
  38.4 2.8 %copy-start.4 = (f32[128,128]{0,1:T(8,128)S(1)}, f32[128,128]{0,1:T(8,128)}, u32[]{:S(2)}) copy-start(f32[128,128]{0,1:T(8,128)} %copy.30) | copy-start | bytes 196612
  43.2 6.7 %copy-start.13 = (s32[128]{0:T(128)S(1)}, s32[128]{0:T(128)}, u32[]{:S(2)}) copy-start(s32[128]{0:T(128)} %get-tuple-element.19) | copy-start | bytes 1540
  46.5 34.5 %collective-permute-start = (bf16[1,128,4096]{2,1,0:T(8,128)(2,1)}, bf16[1,128,4096]{2,1,0:T(8,128)(2,1)}, u32[]{:S(2)}, u32[]{:S(2)}) collective-permute-start(bf16[1,128,4096]{2,1,0:T(8,128)(2,1)} %fusion.4), channel_id=1, source_target_pairs={{0,1},{1,2},{2,3},{3,4},{4,5},{5,6},{6,7},{7,8},{8,9},{9,10},{10,1... | collective-permute-start | bytes 3145736 | tf_op jit(solution)/shard_map/ppermute | solution.py:12
  50.7 14.3 %copy-start.8 = (f32[1,4096]{1,0:T(1,128)S(1)}, f32[1,4096]{1,0:T(1,128)}, u32[]{:S(2)}) copy-start(f32[1,4096]{1,0:T(1,128)} %param.11) | copy-start | bytes 49156
  64.4 1.2 %copy-start.2 = (f32[128,64]{1,0:T(8,128)S(1)}, f32[128,64]{1,0:T(8,128)}, u32[]{:S(2)}) copy-start(f32[128,64]{1,0:T(8,128)} %get-tuple-element.22) | copy-start | bytes 98308
  65.0 0.6 copy-start.12
  67.4 2.5 %copy-start.5 = (bf16[128,128,1]{1,0,2:T(8,128)(2,1)S(1)}, bf16[128,128,1]{1,0,2:T(8,128)(2,1)}, u32[]{:S(2)}) copy-start(bf16[128,128,1]{1,0,2:T(8,128)(2,1)} %get-tuple-element.15) | copy-start | bytes 98308
  67.4 3.7 %copy-start.3 = (f32[128,64]{1,0:T(8,128)S(1)}, f32[128,64]{1,0:T(8,128)}, u32[]{:S(2)}) copy-start(f32[128,64]{1,0:T(8,128)} %get-tuple-element.22) | copy-start | bytes 98308
  67.4 3.7 %copy-start.10 = (pred[128,128]{1,0:T(8,128)(4,1)S(1)}, pred[128,128]{1,0:T(8,128)(4,1)}, u32[]{:S(2)}) copy-start(pred[128,128]{1,0:T(8,128)(4,1)} %get-tuple-element.29) | copy-start | bytes 49156
  72.8 4.3 %copy-start.6 = (f32[128,128]{1,0:T(8,128)S(1)}, f32[128,128]{1,0:T(8,128)}, u32[]{:S(2)}) copy-start(f32[128,128]{1,0:T(8,128)} %get-tuple-element.40) | copy-start | bytes 196612
  74.5 2.7 %copy-start.7 = (bf16[128,128]{1,0:T(8,128)(2,1)S(1)}, bf16[128,128]{1,0:T(8,128)(2,1)}, u32[]{:S(2)}) copy-start(bf16[128,128]{1,0:T(8,128)(2,1)} %fusion.34) | copy-start | bytes 98308
  74.5 2.7 %copy-start.9 = (f32[1,4096]{1,0:T(1,128)S(1)}, f32[1,4096]{1,0:T(1,128)}, u32[]{:S(2)}) copy-start(f32[1,4096]{1,0:T(1,128)} %param.11) | copy-start | bytes 49156
  77.2 1.2 %copy-start.1 = (bf16[1,128,4096]{2,1,0:T(8,128)(2,1)S(1)}, bf16[1,128,4096]{2,1,0:T(8,128)(2,1)}, u32[]{:S(2)}) copy-start(bf16[1,128,4096]{2,1,0:T(8,128)(2,1)} %param.10) | copy-start | bytes 3145732
  79.1 16.1 %collective-permute-start.1 = (bf16[1,128,4096]{2,1,0:T(8,128)(2,1)S(1)}, bf16[1,128,4096]{2,1,0:T(8,128)(2,1)S(1)}, u32[]{:S(2)}, u32[]{:S(2)}) collective-permute-start(bf16[1,128,4096]{2,1,0:T(8,128)(2,1)S(1)} %fusion.37), channel_id=1, source_target_pairs={{1,0},{2,1},{3,2},{4,3},{5,4},{6,5},{7,6},{8,7},{9,8},{10,9},{11,1... | collective-permute-start | bytes 3145736 | tf_op jit(solution)/shard_map/ppermute | solution.py:12
where the time goes:
time: 99.5 us; the launch traced here: 98.4 us
  waiting for transfers between devices  37.8 us (38%)
  matrix products  21.8 us (22%)
  starting transfers between devices  17 us (17%)
  local copies, waits for them, and re-layouts  13 us (13%)
  other arithmetic  7.76 us (8%)
  between operations  1.06 us (1%)
    ppermute x2, waiting for transfers between devices, shifted(): lax.ppermute(value, axis, [(source, source + steps) for source in range(l...  14.2 us
    all_to_all x1, waiting for transfers between devices, shards(): lax.all_to_all(local, 'section', split_axis=0, concat_axis=0, tiled=True)  13.2 us
    all_to_all x1, waiting for transfers between devices, shards(): lax.all_to_all(spread, 'section', split_axis=0, concat_axis=0, tiled=True)  10.5 us
    dot_general x3, matrix products, section_layer(): jnp.dot(normed, w_query, preferred_element_type=jnp.float32)  7.59 us
    all_to_all x1, starting transfers between devices, shards(): lax.all_to_all(local, 'section', split_axis=0, concat_axis=0, tiled=True)  6.75 us
    dot_general x2, matrix products, section_layer(): jnp.dot(mixed, w_out, preferred_element_type=jnp.float32)  6.06 us
    ppermute x2, starting transfers between devices, shifted(): lax.ppermute(value, axis, [(source, source + steps) for source in range(l...  5.25 us
    all_to_all x1, starting transfers between devices, shards(): lax.all_to_all(spread, 'section', split_axis=0, concat_axis=0, tiled=True)  4.97 us
  transfers between devices with their start and end apart: 4, of which 3 were waited for; matrix products, arithmetic and copies ran while one was open for 38% of the time, Pallas kernels for 0%

commit v1 on v0

--- a/solution.py
+++ b/solution.py
@@ -61,14 +61,9 @@
 
 
 def shards(section_input, stash, cotangent, norm_gain, w_query, w_kv, w_out, doc_ids):
-    rows = stash.shape[1]
-    width = stash.shape[2]
     pieces = lax.axis_size("section")
-    local = stash[0].reshape(pieces, rows // pieces, width)
-    spread = lax.all_to_all(local, "section", split_axis=0, concat_axis=0, tiled=True)
-    spread = spread[::-1]
-    collected = lax.all_to_all(spread, "section", split_axis=0, concat_axis=0, tiled=True)
-    fetched = collected.reshape(rows, width)
+    mirror = [(source, pieces - 1 - source) for source in range(pieces)]
+    fetched = lax.ppermute(stash[0], "section", mirror)
     outward = section_layer(
         section_input[0], norm_gain[0], w_query[0], w_kv[0], w_out[0], doc_ids[0, 0]
     )

time: 99.5 us -> 90.8 us (0.913)
  starting transfers between devices: 17 us -> 7.14 us
  waiting for transfers between devices: 37.8 us -> 43.4 us
  matrix products: 21.8 us -> 18.3 us
    ppermute x0 -> x1, waiting for transfers between devices: none -> 29.6 us  [shards(): fetched = lax.ppermute(stash[0], 'section', mirror)]
    all_to_all x2 -> x0, waiting for transfers between devices: 23.6 us -> none  [the longest x1 13.2 us: shards(): lax.all_to_all(local, 'section', split_axis=0, concat_axis=0, tiled=True)]
    all_to_all x2 -> x0, starting transfers between devices: 11.7 us -> none  [the longest x1 6.75 us: shards(): lax.all_to_all(local, 'section', split_axis=0, concat_axis=0, tiled=True)]
    ppermute x0 -> x1, starting transfers between devices: none -> 2.88 us  [shards(): fetched = lax.ppermute(stash[0], 'section', mirror)]
    dot_general x3, matrix products: 7.59 us -> 5.99 us  [section_layer(): jnp.dot(normed, w_query, preferred_element_type=jnp.float32)]
    dot_general x4, matrix products: 2.77 us -> 1.49 us  [section_layer(): jnp.einsum('qhd,kd->hqk', query, keys, preferred_element_type=jnp.float32)]
    rev x1 -> x0, local copies, waits for them, and re-layouts: 1.04 us -> none  [shards(): spread = spread[::-1]]
    unnamed x32 -> x42, local copies, waits for them, and re-layouts: 4.08 us -> 4.13 us
  transfers between devices with their start and end apart: 4 -> 3, of which waited for: 3 -> 2; matrix products, arithmetic and copies ran while one was open for 38% -> 38% of each run, Pallas kernels for 0% -> 0%
where the time goes in v1:
time: 90.8 us; the launch traced here: 90.3 us
  waiting for transfers between devices  43.4 us (48%)
  matrix products  18.3 us (20%)
  local copies, waits for them, and re-layouts  12.6 us (14%)
  other arithmetic  7.75 us (9%)
  starting transfers between devices  7.14 us (8%)
  between operations  1.14 us (1%)
    ppermute x1, waiting for transfers between devices, shards(): fetched = lax.ppermute(stash[0], 'section', mirror)  29.6 us
    ppermute x2, waiting for transfers between devices, shifted(): lax.ppermute(value, axis, [(source, source + steps) for source in range(l...  13.7 us
    dot_general x2, matrix products, section_layer(): jnp.dot(mixed, w_out, preferred_element_type=jnp.float32)  6.06 us
    dot_general x3, matrix products, section_layer(): jnp.dot(normed, w_query, preferred_element_type=jnp.float32)  5.99 us
    ppermute x2, starting transfers between devices, shifted(): lax.ppermute(value, axis, [(source, source + steps) for source in range(l...  4.26 us
    unnamed x42, local copies, waits for them, and re-layouts  4.13 us
    dot_general x1, local copies, waits for them, and re-layouts, section_layer(): jnp.dot(normed, w_query, preferred_element_type=jnp.float32)  4.13 us
    dot_general x3, matrix products, section_layer(): keyval = jnp.dot(normed, w_kv, preferred_element_type=jnp.float32)  3.23 us
  transfers between devices with their start and end apart: 3, of which 2 were waited for; matrix products, arithmetic and copies ran while one was open for 38% of the time, Pallas kernels for 0%

profile of v1, /device:TPU:9, one launch (start us, length us, event | category | flops | bytes accessed | tf_op | source)
XLA Modules:
  0.0 90.3 jit_solution(4729354883986155468)
XLA Ops:
  0.6 2.9 %collective-permute-start.1 = (bf16[128,4096]{1,0:T(8,128)(2,1)}, bf16[128,4096]{1,0:T(8,128)(2,1)S(1)}, u32[]{:S(2)}, u32[]{:S(2)}) collective-permute-start(bf16[128,4096]{1,0:T(8,128)(2,1)} %bitcast.145), channel_id=1, source_target_pairs={{0,15},{1,14},{2,13},{3,12},{4,11},{5,10},{6,9},{7,8},{8,7},{9,6},... | collective-permute-start | bytes 3145736 | tf_op jit(solution)/shard_map/ppermute | solution.py:66
  3.5 0.9 %compare_bitcast_fusion = (pred[127,1]{0,1:T(4,128)(4,1)S(1)}, pred[127,1]{0,1:T(4,128)(4,1)S(1)}) fusion(s32[1,2,128]{2,1,0:T(2,128)} %param.15), kind=kLoop, calls=%fused_computation.121 | loop fusion | flops 254 | bytes 2286 | tf_op jit(solution)/shard_map/jvp()/concatenate | solution.py:17
  4.4 1.3 %slice_bitcast_fusion = (s32[128]{0:T(128)}, s32[128]{0:T(128)S(1)}) fusion(s32[1,2,128]{2,1,0:T(2,128)} %param.15), kind=kLoop, calls=%fused_computation.128 | loop fusion | bytes 2048 | tf_op jit(solution)/shard_map/jvp()/eq | solution.py:53
  5.7 1.5 %fusion.6 = f32[128]{0:T(128)S(1)} fusion(bf16[1,128,4096]{2,1,0:T(8,128)(2,1)} %param.8), kind=kLoop, calls=%fused_computation.16 | loop fusion | flops 1572736 | bytes 1049088 | tf_op jit(solution)/shard_map/reduce_sum | solution.py:39
  7.3 0.1 copy.27
  7.5 0.1 copy.28
  7.6 0.2 reduce-window.16
  7.8 0.1 reduce
  7.9 0.1 copy.36
  8.0 0.2 reduce-window.17
  8.2 0.1 reduce.1
  8.4 1.7 %fusion.21 = f32[128,256]{1,0:T(8,128)S(1)} fusion(bf16[1,4096,256]{2,1,0:T(8,128)(2,1)S(1)} %copy-done, bf16[1,128,4096]{2,1,0:T(8,128)(2,1)} %param.8, f32[4096]{0:T(1024)} %bitcast.138, f32[128]{0:T(128)S(1)} %add_rsqrt_fusion), kind=kOutput, calls=%fused_computation.31 | convolution fusion | flops 270532608 | bytes 3293696 | tf_op jit(solution)/shard_map/dot_general | solution.py:44
  10.1 0.7 slice_negate_fusion.5
  10.8 0.9 %multiply_cosine_fusion = (f32[128,64]{1,0:T(8,128)S(1)}, f32[128,64]{1,0:T(8,128)}, f32[128,64]{1,0:T(8,128)S(1)}, f32[128,64]{1,0:T(8,128)S(1)}) fusion(f32[128]{0:T(128)S(1)} %subtract_convert_fusion, f32[64]{0:T(128)S(1)} %negate_power_fusion, f32[128]{0:T(128)S(1)} %subtract_convert_fusion.1), kind=kLoop, calls=%fused_computation.78 | loop fusion | flops 16384 | bytes 132352 | tf_op jit(solution)/shard_map/jvp()/cos | solution.py:23
  11.9 0.7 copy.31
  12.7 0.7 copy.30
  13.4 4.1 %copy.54 = bf16[256,4096]{1,0:T(8,128)(2,1)} copy(bf16[256,4096]{0,1:T(8,128)(2,1)} %bitcast.131) | data formatting | bytes 4194304 | tf_op jit(solution)/shard_map/dot_general | solution.py:41
  17.6 2.7 %fusion.39 = f32[128,2,128]{0,2,1:T(8,128)S(1)} fusion(bf16[2,128,4096]{2,1,0:T(8,128)(2,1)} %bitcast.132, bf16[1,128,4096]{2,1,0:T(8,128)(2,1)} %param.8, f32[4096]{0:T(1024)S(1)} %bitcast.140, f32[128]{0:T(128)S(1)} %copy-done.19), kind=kOutput, calls=%fused_computation.54 | convolution fusion | flops 270532608 | bytes 3293696 | tf_op jit(solution)/shard_map/dot_general | solution.py:41
  20.4 0.9 %fusion.26 = f32[2,128,128]{1,2,0:T(8,128)} fusion(f32[128,2,64]{0,2,1:T(8,128)S(1)} %get-tuple-element.11, f32[128,2,64]{0,2,1:T(8,128)S(1)} %get-tuple-element.10, f32[128,2,128]{0,2,1:T(8,128)S(1)} %fusion.39, f32[128,128]{0,1:T(8,128)S(1)} %copy-done.5, f32[128,128]{0,1:T(8,128)S(1)} %copy-done.6, pred[128,128]{0,1:T(8,128)(4,1)S(1)} %copy.27, ...), kind=kOutput, calls=%fused_computation.38 | convolution fusion | flops 8732672 | bytes 868352 | tf_op jit(solution)/shard_map/qhd,kd->hqk/dot_general | solution.py:49
  21.3 1.2 %convolution_convert_fusion.3 = bf16[128,2,128]{2,0,1:T(8,128)(2,1)S(1)} fusion(f32[2,128,128]{1,2,0:T(8,128)} %fusion.26, f32[128,256]{1,0:T(8,128)S(1)} %fusion.21), kind=kOutput, calls=%fused_computation.42 | convolution fusion | flops 8487295 | bytes 360448 | tf_op jit(solution)/shard_map/hqk,kd->qhd/dot_general | solution.py:56
  22.5 3.3 %fusion.4 = bf16[1,128,4096]{2,1,0:T(8,128)(2,1)} fusion(bf16[128,256]{0,1:T(8,128)(2,1)S(1)} %bitcast.137, bf16[1,128,4096]{2,1,0:T(8,128)(2,1)} %param.8, bf16[1,256,4096]{2,1,0:T(8,128)(2,1)} %param.14), kind=kOutput, calls=%fused_computation.7 | convolution fusion | flops 270008320 | bytes 4259840 | tf_op jit(solution)/shard_map/dot_general | solution.py:58
  25.8 1.9 %collective-permute-start = (bf16[1,128,4096]{2,1,0:T(8,128)(2,1)}, bf16[1,128,4096]{2,1,0:T(8,128)(2,1)}, u32[]{:S(2)}, u32[]{:S(2)}) collective-permute-start(bf16[1,128,4096]{2,1,0:T(8,128)(2,1)} %fusion.4), channel_id=1, source_target_pairs={{0,1},{1,2},{2,3},{3,4},{4,5},{5,6},{6,7},{7,8},{8,9},{9,10},{10,1... | collective-permute-start | bytes 3145736 | tf_op jit(solution)/shard_map/ppermute | solution.py:12
  27.7 0.7 fusion.70
  28.4 0.1 copy.35
  28.5 2.8 %fusion.27 = bf16[128,256]{1,0:T(8,128)(2,1)S(1)} fusion(bf16[1,256,4096]{2,1,0:T(8,128)(2,1)} %param.14, bf16[1,128,4096]{2,1,0:T(8,128)(2,1)} %param.10), kind=kOutput, calls=%fused_computation.39 | convolution fusion | flops 268468224 | bytes 3211264 | tf_op jit(solution)/shard_map/transpose(jvp())/dot_general | solution.py:58
  31.3 0.1 copy.51
  31.4 29.6 %collective-permute-done.1 = bf16[128,4096]{1,0:T(8,128)(2,1)S(1)} collective-permute-done((bf16[128,4096]{1,0:T(8,128)(2,1)}, bf16[128,4096]{1,0:T(8,128)(2,1)S(1)}, u32[]{:S(2)}, u32[]{:S(2)}) %collective-permute-start.1) | collective-permute-done | bytes 1048608 | tf_op jit(solution)/shard_map/ppermute | solution.py:66
  61.0 0.3 fusion.10
  61.3 0.5 fusion.19
  61.9 0.2 copy-done.3
  62.2 0.8 pad_maximum_fusion.2
  63.0 0.9 %copy.39 = f32[128,128]{0,1:T(8,128)S(1)} copy(f32[128,128]{1,0:T(8,128)} %get-tuple-element.16) | data formatting | bytes 131072 | tf_op jit(solution)/shard_map/jvp()/concatenate | solution.py:24
  64.0 2.4 %fusion.36 = f32[128,2,128]{0,2,1:T(8,128)S(1)} fusion(bf16[2,128,4096]{2,1,0:T(8,128)(2,1)} %bitcast.133, bf16[128,4096]{1,0:T(8,128)(2,1)S(1)} %collective-permute-done.1, f32[4096]{0:T(1024)} %bitcast.139, f32[128]{0:T(128)} %copy-done.14), kind=kOutput, calls=%fused_computation.51 | convolution fusion | flops 270532608 | bytes 3293696 | tf_op jit(solution)/shard_map/jvp()/dot_general | solution.py:41
  66.5 0.2 fusion.57
  66.7 0.2 fusion.32
  66.9 0.2 multiply_reduce_fusion
  67.1 0.2 fusion.87
  67.2 0.2 broadcast_multiply_fusion
  67.6 0.4 copy-done.1
  68.0 0.8 convolution_convert_fusion
  68.9 0.1 pad_add_fusion.1
  69.0 1.0 %fusion.13 = (f32[128]{0:T(128)S(1)}, f32[128,4096]{1,0:T(8,128)S(1)}) fusion(bf16[128,4096]{1,0:T(8,128)(2,1)S(1)} %collective-permute-done.1, f32[4096]{0:T(1024)S(1)} %bitcast.142, bf16[128,4096]{1,0:T(8,128)(2,1)S(1)} %convolution_convert_fusion, bf16[1,4096,256]{2,1,0:T(8,128)(2,1)S(1)} %copy-done, f32[128,128]{1,0:T(8,128)S(1)} %pad_add_fusion.1, ...), kind=kOutput, calls=%fused_computation.23 | convolution fusion | flops 272170880 | bytes 6406656 | tf_op jit(solution)/shard_map/transpose(jvp())/dot_general | solution.py:44
  70.1 0.2 copy-done.2
  70.2 0.6 fusion.35
  70.9 2.4 %collective-permute-start.2 = (bf16[1,128,4096]{2,1,0:T(8,128)(2,1)S(1)}, bf16[1,128,4096]{2,1,0:T(8,128)(2,1)S(1)}, u32[]{:S(2)}, u32[]{:S(2)}) collective-permute-start(bf16[1,128,4096]{2,1,0:T(8,128)(2,1)S(1)} %fusion.35), channel_id=1, source_target_pairs={{1,0},{2,1},{3,2},{4,3},{5,4},{6,5},{7,6},{8,7},{9,8},{10,9},{11,1... | collective-permute-start | bytes 3145736 | tf_op jit(solution)/shard_map/ppermute | solution.py:12
  73.2 13.7 %collective-permute-done.2 = bf16[1,128,4096]{2,1,0:T(8,128)(2,1)S(1)} collective-permute-done((bf16[1,128,4096]{2,1,0:T(8,128)(2,1)S(1)}, bf16[1,128,4096]{2,1,0:T(8,128)(2,1)S(1)}, u32[]{:S(2)}, u32[]{:S(2)}) %collective-permute-start.2) | collective-permute-done | bytes 1048608 | tf_op jit(solution)/shard_map/ppermute | solution.py:12
  87.0 2.3 %copy.57 = bf16[1,128,4096]{2,1,0:T(8,128)(2,1)} copy(bf16[1,128,4096]{2,1,0:T(8,128)(2,1)} %collective-permute-done) | data formatting | bytes 2097152
  89.3 1.0 %copy.58 = bf16[1,128,4096]{2,1,0:T(8,128)(2,1)} copy(bf16[1,128,4096]{2,1,0:T(8,128)(2,1)S(1)} %collective-permute-done.2) | data formatting | bytes 2097152
  (58 shorter events, 0.8 us)
Async XLA Ops:
  0.6 7.7 %copy-start = (bf16[1,4096,256]{2,1,0:T(8,128)(2,1)S(1)}, bf16[1,4096,256]{2,1,0:T(8,128)(2,1)}, u32[]{:S(2)}) copy-start(bf16[1,4096,256]{2,1,0:T(8,128)(2,1)} %param.13) | copy-start | bytes 6291460
  0.6 60.4 %collective-permute-start.1 = (bf16[128,4096]{1,0:T(8,128)(2,1)}, bf16[128,4096]{1,0:T(8,128)(2,1)S(1)}, u32[]{:S(2)}, u32[]{:S(2)}) collective-permute-start(bf16[128,4096]{1,0:T(8,128)(2,1)} %bitcast.145), channel_id=1, source_target_pairs={{0,15},{1,14},{2,13},{3,12},{4,11},{5,10},{6,9},{7,8},{8,7},{9,6},... | collective-permute-start | bytes 3145736 | tf_op jit(solution)/shard_map/ppermute | solution.py:66
  7.2 2.9 %copy-start.18 = (f32[128]{0:T(128)}, f32[128]{0:T(128)S(1)}, u32[]{:S(2)}) copy-start(f32[128]{0:T(128)S(1)} %add_rsqrt_fusion) | copy-start | bytes 1540
  13.4 4.1 %copy-start.10 = (f32[1,4096]{1,0:T(1,128)S(1)}, f32[1,4096]{1,0:T(1,128)}, u32[]{:S(2)}) copy-start(f32[1,4096]{1,0:T(1,128)} %param.11) | copy-start | bytes 49156
  13.4 4.1 %copy-start.19 = (f32[128]{0:T(128)S(1)}, f32[128]{0:T(128)}, u32[]{:S(2)}) copy-start(f32[128]{0:T(128)} %copy-done.18) | copy-start | bytes 1540
  17.5 2.8 %copy-start.5 = (f32[128,128]{0,1:T(8,128)S(1)}, f32[128,128]{0,1:T(8,128)}, u32[]{:S(2)}) copy-start(f32[128,128]{0,1:T(8,128)} %copy.31) | copy-start | bytes 196612
  17.5 2.8 %copy-start.6 = (f32[128,128]{0,1:T(8,128)S(1)}, f32[128,128]{0,1:T(8,128)}, u32[]{:S(2)}) copy-start(f32[128,128]{0,1:T(8,128)} %copy.30) | copy-start | bytes 196612
  17.6 2.8 %copy-start.7 = (f32[128,64]{1,0:T(8,128)S(1)}, f32[128,64]{1,0:T(8,128)}, u32[]{:S(2)}) copy-start(f32[128,64]{1,0:T(8,128)} %get-tuple-element.8) | copy-start | bytes 98308
  17.6 2.8 %copy-start.8 = (f32[128,64]{1,0:T(8,128)S(1)}, f32[128,64]{1,0:T(8,128)}, u32[]{:S(2)}) copy-start(f32[128,64]{1,0:T(8,128)} %get-tuple-element.9) | copy-start | bytes 98308
  22.5 5.2 %copy-start.13 = (s32[128]{0:T(128)S(1)}, s32[128]{0:T(128)}, u32[]{:S(2)}) copy-start(s32[128]{0:T(128)} %get-tuple-element.17) | copy-start | bytes 1540
  25.8 47.5 %collective-permute-start = (bf16[1,128,4096]{2,1,0:T(8,128)(2,1)}, bf16[1,128,4096]{2,1,0:T(8,128)(2,1)}, u32[]{:S(2)}, u32[]{:S(2)}) collective-permute-start(bf16[1,128,4096]{2,1,0:T(8,128)(2,1)} %fusion.4), channel_id=1, source_target_pairs={{0,1},{1,2},{2,3},{3,4},{4,5},{5,6},{6,7},{7,8},{8,9},{9,10},{10,1... | collective-permute-start | bytes 3145736 | tf_op jit(solution)/shard_map/ppermute | solution.py:12
  61.3 0.6 copy-start.16
  61.3 0.8 copy-start.3
  61.3 0.6 copy-start.14
  64.0 2.5 %copy-start.9 = (bf16[128,128,1]{1,0,2:T(8,128)(2,1)S(1)}, bf16[128,128,1]{1,0,2:T(8,128)(2,1)}, u32[]{:S(2)}) copy-start(bf16[128,128,1]{1,0,2:T(8,128)(2,1)} %get-tuple-element.15) | copy-start | bytes 98308
  64.0 3.1 %copy-start.4 = (f32[128,64]{1,0:T(8,128)S(1)}, f32[128,64]{1,0:T(8,128)}, u32[]{:S(2)}) copy-start(f32[128,64]{1,0:T(8,128)} %get-tuple-element.20) | copy-start | bytes 98308
  64.0 3.1 %copy-start.12 = (pred[128,128]{1,0:T(8,128)(4,1)S(1)}, pred[128,128]{1,0:T(8,128)(4,1)}, u32[]{:S(2)}) copy-start(pred[128,128]{1,0:T(8,128)(4,1)} %get-tuple-element.25) | copy-start | bytes 49156
  66.4 1.6 %copy-start.1 = (bf16[1,4096,256]{2,1,0:T(8,128)(2,1)S(1)}, bf16[1,4096,256]{2,1,0:T(8,128)(2,1)}, u32[]{:S(2)}) copy-start(bf16[1,4096,256]{2,1,0:T(8,128)(2,1)} %param.12) | copy-start | bytes 6291460
  67.5 1.5 %copy-start.11 = (f32[1,4096]{1,0:T(1,128)S(1)}, f32[1,4096]{1,0:T(1,128)}, u32[]{:S(2)}) copy-start(f32[1,4096]{1,0:T(1,128)} %param.11) | copy-start | bytes 49156
  69.0 1.1 %copy-start.17 = (f32[128]{0:T(128)S(1)}, f32[128]{0:T(128)}, u32[]{:S(2)}) copy-start(f32[128]{0:T(128)} %copy-done.16) | copy-start | bytes 1540
  69.0 1.2 %copy-start.2 = (bf16[1,128,4096]{2,1,0:T(8,128)(2,1)S(1)}, bf16[1,128,4096]{2,1,0:T(8,128)(2,1)}, u32[]{:S(2)}) copy-start(bf16[1,128,4096]{2,1,0:T(8,128)(2,1)} %param.10) | copy-start | bytes 3145732
  69.0 1.2 %copy-start.15 = (f32[128]{0:T(128)S(1)}, f32[128]{0:T(128)}, u32[]{:S(2)}) copy-start(f32[128]{0:T(128)} %copy-done.14) | copy-start | bytes 1540
  70.9 16.1 %collective-permute-start.2 = (bf16[1,128,4096]{2,1,0:T(8,128)(2,1)S(1)}, bf16[1,128,4096]{2,1,0:T(8,128)(2,1)S(1)}, u32[]{:S(2)}, u32[]{:S(2)}) collective-permute-start(bf16[1,128,4096]{2,1,0:T(8,128)(2,1)S(1)} %fusion.35), channel_id=1, source_target_pairs={{1,0},{2,1},{3,2},{4,3},{5,4},{6,5},{7,6},{8,7},{9,8},{10,9},{11,1... | collective-permute-start | bytes 3145736 | tf_op jit(solution)/shard_map/ppermute | solution.py:12

commit v2 on v1

--- a/solution.py
+++ b/solution.py
@@ -63,7 +63,16 @@
 def shards(section_input, stash, cotangent, norm_gain, w_query, w_kv, w_out, doc_ids):
     pieces = lax.axis_size("section")
     mirror = [(source, pieces - 1 - source) for source in range(pieces)]
-    fetched = lax.ppermute(stash[0], "section", mirror)
+    rows = stash.shape[1]
+    chunks = 4 if rows % 32 == 0 else 1
+    step = rows // chunks
+    fetched = jnp.concatenate(
+        [
+            lax.ppermute(stash[0, start : start + step], "section", mirror)
+            for start in range(0, rows, step)
+        ],
+        0,
+    )
     outward = section_layer(
         section_input[0], norm_gain[0], w_query[0], w_kv[0], w_out[0], doc_ids[0, 0]
     )

time: 90.8 us -> 98.6 us (1.086)
  waiting for transfers between devices: 43.4 us -> 35.1 us
  local copies, waits for them, and re-layouts: 12.6 us -> 18.9 us
  other arithmetic: 7.75 us -> 12.5 us
  starting transfers between devices: 7.14 us -> 11.2 us
    ppermute x1 -> x4, waiting for transfers between devices: 29.6 us -> 21.2 us  [shards(): lax.ppermute(stash[0, start:start + step], 'section', mirror)]
    ppermute x1 -> x4, starting transfers between devices: 2.88 us -> 5.5 us  [shards(): lax.ppermute(stash[0, start:start + step], 'section', mirror)]
    squeeze x0 -> x1, local copies, waits for them, and re-layouts: none -> 2.34 us  [shards(): stash[0, start:start + step]]
    dot_general x3, matrix products: 3.23 us -> 4.99 us  [section_layer(): keyval = jnp.dot(normed, w_kv, preferred_element_type=jnp.float32)]
    concatenate x2, local copies, waits for them, and re-layouts: 0.81 us -> 2.49 us  [rotary_tables(): cosine = jnp.concatenate([jnp.cos(angles), jnp.cos(angles)], -1)]
    concatenate x2, other arithmetic: 0.84 us -> 2.44 us  [rotary_tables(): cosine = jnp.concatenate([jnp.cos(angles), jnp.cos(angles)], -1)]
    concatenate x2, local copies, waits for them, and re-layouts: 1.66 us -> 3.13 us  [rotary_tables(): sine_part = jnp.concatenate([jnp.sin(angles), jnp.sin(angles)], -1)]
    ppermute x2, starting transfers between devices: 4.26 us -> 5.71 us  [shifted(): lax.ppermute(value, axis, [(source, source + steps) for source in range(l...]
  transfers between devices with their start and end apart: 3 -> 6, of which waited for: 2 -> 3; matrix products, arithmetic and copies ran while one was open for 38% -> 45% of each run, Pallas kernels for 0% -> 0%
where the time goes in v2:
time: 98.6 us; the launch traced here: 97.8 us
  waiting for transfers between devices  35.1 us (36%)
  local copies, waits for them, and re-layouts  18.9 us (19%)
  matrix products  18.9 us (19%)
  other arithmetic  12.5 us (13%)
  starting transfers between devices  11.2 us (11%)
  between operations  1.21 us (1%)
    ppermute x4, waiting for transfers between devices, shards(): lax.ppermute(stash[0, start:start + step], 'section', mirror)  21.2 us
    ppermute x2, waiting for transfers between devices, shifted(): lax.ppermute(value, axis, [(source, source + steps) for source in range(l...  13.9 us
    dot_general x3, matrix products, section_layer(): jnp.dot(normed, w_query, preferred_element_type=jnp.float32)  5.95 us
    dot_general x2, matrix products, section_layer(): jnp.dot(mixed, w_out, preferred_element_type=jnp.float32)  5.81 us
    ppermute x2, starting transfers between devices, shifted(): lax.ppermute(value, axis, [(source, source + steps) for source in range(l...  5.71 us
    ppermute x4, starting transfers between devices, shards(): lax.ppermute(stash[0, start:start + step], 'section', mirror)  5.5 us
    dot_general x3, matrix products, section_layer(): keyval = jnp.dot(normed, w_kv, preferred_element_type=jnp.float32)  4.99 us
    unnamed x58, local copies, waits for them, and re-layouts  4.44 us
  transfers between devices with their start and end apart: 6, of which 3 were waited for; matrix products, arithmetic and copies ran while one was open for 45% of the time, Pallas kernels for 0%

profile of v2, /device:TPU:9, one launch (start us, length us, event | category | flops | bytes accessed | tf_op | source)
XLA Modules:
  0.0 97.8 jit_solution(17513681899129420530)
XLA Ops:
  0.7 2.3 %slice_bitcast_fusion.3 = (bf16[32,4096]{1,0:T(8,128)(2,1)}, bf16[32,4096]{1,0:T(8,128)(2,1)}, bf16[32,4096]{1,0:T(8,128)(2,1)}, bf16[32,4096]{1,0:T(8,128)(2,1)}) fusion(bf16[1,128,4096]{2,1,0:T(8,128)(2,1)} %param.9), kind=kLoop, calls=%fused_computation.61 | loop fusion | bytes 2097152 | tf_op jit(solution)/shard_map/squeeze | solution.py:71
  3.0 2.8 %collective-permute-start.1 = (bf16[32,4096]{1,0:T(8,128)(2,1)}, bf16[32,4096]{1,0:T(8,128)(2,1)S(1)}, u32[]{:S(2)}, u32[]{:S(2)}) collective-permute-start(bf16[32,4096]{1,0:T(8,128)(2,1)} %get-tuple-element.2), channel_id=1, source_target_pairs={{0,15},{1,14},{2,13},{3,12},{4,11},{5,10},{6,9},{7,8},{8,7},{9,6},... | collective-permute-start | bytes 786440 | tf_op jit(solution)/shard_map/ppermute | solution.py:71
  5.9 2.6 %collective-permute-start.4 = (bf16[32,4096]{1,0:T(8,128)(2,1)}, bf16[32,4096]{1,0:T(8,128)(2,1)}, u32[]{:S(2)}, u32[]{:S(2)}) collective-permute-start(bf16[32,4096]{1,0:T(8,128)(2,1)} %get-tuple-element.4), channel_id=1, source_target_pairs={{0,15},{1,14},{2,13},{3,12},{4,11},{5,10},{6,9},{7,8},{8,7},{9,6},... | collective-permute-start | bytes 786440 | tf_op jit(solution)/shard_map/ppermute | solution.py:71
  8.5 0.5 negate_power_fusion
  9.1 0.5 slice_bitcast_fusion.4
  9.7 0.3 fusion.6
  10.0 0.5 add_rsqrt_fusion
  10.7 0.6 fusion.79
  11.4 0.2 reduce-window.16
  11.7 0.6 subtract_convert_fusion.1
  12.3 0.8 copy.36
  13.0 0.2 reduce-window.17
  13.3 1.2 %fusion.21 = f32[128,256]{1,0:T(8,128)S(1)} fusion(bf16[1,4096,256]{2,1,0:T(8,128)(2,1)S(1)} %copy-done, bf16[1,128,4096]{2,1,0:T(8,128)(2,1)S(1)} %copy-done.3, f32[4096]{0:T(1024)} %bitcast.147, f32[128]{0:T(128)} %add_rsqrt_fusion), kind=kOutput, calls=%fused_computation.31 | convolution fusion | flops 270532608 | bytes 3293696 | tf_op jit(solution)/shard_map/dot_general | solution.py:44
  14.6 0.6 copy-done.7
  15.2 0.7 slice_negate_fusion.5
  15.9 1.2 %multiply_cosine_fusion = (f32[128,64]{1,0:T(8,128)S(1)}, f32[128,64]{1,0:T(8,128)}, f32[128,64]{1,0:T(8,128)S(1)}, f32[128,64]{1,0:T(8,128)}) fusion(f32[128]{0:T(128)S(1)} %subtract_convert_fusion, f32[64]{0:T(128)S(1)} %copy-done.25, f32[128]{0:T(128)S(1)} %copy-done.26), kind=kLoop, calls=%fused_computation.83 | loop fusion | flops 16384 | bytes 132352 | tf_op jit(solution)/shard_map/jvp()/cos | solution.py:23
  17.1 0.7 pad_maximum_fusion.2
  17.8 1.6 %copy.31 = f32[128,128]{0,1:T(8,128)} copy(f32[128,128]{1,0:T(8,128)} %pad_maximum_fusion.2) | data formatting | bytes 131072 | tf_op jit(solution)/shard_map/concatenate | solution.py:24
  19.4 1.6 %pad_maximum_fusion.1 = f32[128,128]{1,0:T(8,128)} fusion(f32[128,64]{1,0:T(8,128)} %get-tuple-element.32), kind=kLoop, calls=%fused_computation.100 | loop fusion | flops 16384 | bytes 98304 | tf_op jit(solution)/shard_map/concatenate | solution.py:23
  21.0 1.6 %copy.30 = f32[128,128]{0,1:T(8,128)} copy(f32[128,128]{1,0:T(8,128)} %pad_maximum_fusion.1) | data formatting | bytes 131072 | tf_op jit(solution)/shard_map/concatenate | solution.py:23
  22.6 4.1 %copy.54 = bf16[256,4096]{1,0:T(8,128)(2,1)} copy(bf16[256,4096]{0,1:T(8,128)(2,1)} %bitcast.138) | data formatting | bytes 4194304 | tf_op jit(solution)/shard_map/dot_general | solution.py:41
  26.7 2.5 %fusion.39 = f32[128,2,128]{0,2,1:T(8,128)S(1)} fusion(bf16[2,128,4096]{2,1,0:T(8,128)(2,1)} %bitcast.139, bf16[1,128,4096]{2,1,0:T(8,128)(2,1)S(1)} %copy-done.3, f32[4096]{0:T(1024)} %bitcast.148, f32[128]{0:T(128)} %add_rsqrt_fusion), kind=kOutput, calls=%fused_computation.55 | convolution fusion | flops 270532608 | bytes 3293696 | tf_op jit(solution)/shard_map/dot_general | solution.py:41
  29.3 0.3 fusion.26
  29.5 1.0 %convolution_convert_fusion.3 = bf16[128,2,128]{2,0,1:T(8,128)(2,1)S(1)} fusion(f32[2,128,128]{1,2,0:T(8,128)S(1)} %fusion.26, f32[128,256]{1,0:T(8,128)} %copy-done.7), kind=kOutput, calls=%fused_computation.42 | convolution fusion | flops 8487295 | bytes 360448 | tf_op jit(solution)/shard_map/hqk,kd->qhd/dot_general | solution.py:56
  30.6 3.4 %fusion.4 = bf16[1,128,4096]{2,1,0:T(8,128)(2,1)} fusion(bf16[128,256]{0,1:T(8,128)(2,1)S(1)} %bitcast.144, bf16[1,128,4096]{2,1,0:T(8,128)(2,1)} %param.8, bf16[1,256,4096]{2,1,0:T(8,128)(2,1)} %param.14), kind=kOutput, calls=%fused_computation.7 | convolution fusion | flops 270008320 | bytes 4259840 | tf_op jit(solution)/shard_map/dot_general | solution.py:58
  34.0 3.5 %collective-permute-start = (bf16[1,128,4096]{2,1,0:T(8,128)(2,1)}, bf16[1,128,4096]{2,1,0:T(8,128)(2,1)}, u32[]{:S(2)}, u32[]{:S(2)}) collective-permute-start(bf16[1,128,4096]{2,1,0:T(8,128)(2,1)} %fusion.4), channel_id=1, source_target_pairs={{0,1},{1,2},{2,3},{3,4},{4,5},{5,6},{6,7},{7,8},{8,9},{9,10},{10,1... | collective-permute-start | bytes 3145736 | tf_op jit(solution)/shard_map/ppermute | solution.py:12
  37.5 0.7 fusion.70
  38.3 2.4 %fusion.27 = bf16[128,256]{1,0:T(8,128)(2,1)S(1)} fusion(bf16[1,256,4096]{2,1,0:T(8,128)(2,1)} %param.14, bf16[1,128,4096]{2,1,0:T(8,128)(2,1)S(1)} %copy-done.2), kind=kOutput, calls=%fused_computation.39 | convolution fusion | flops 268468224 | bytes 3211264 | tf_op jit(solution)/shard_map/transpose(jvp())/dot_general | solution.py:58
  40.7 0.7 copy.51
  41.5 10.3 %collective-permute-done.4 = bf16[32,4096]{1,0:T(8,128)(2,1)} collective-permute-done((bf16[32,4096]{1,0:T(8,128)(2,1)}, bf16[32,4096]{1,0:T(8,128)(2,1)}, u32[]{:S(2)}, u32[]{:S(2)}) %collective-permute-start.4) | collective-permute-done | bytes 262176 | tf_op jit(solution)/shard_map/ppermute | solution.py:71
  51.8 10.9 %collective-permute-done.3 = bf16[32,4096]{1,0:T(8,128)(2,1)} collective-permute-done((bf16[32,4096]{1,0:T(8,128)(2,1)}, bf16[32,4096]{1,0:T(8,128)(2,1)}, u32[]{:S(2)}, u32[]{:S(2)}) %collective-permute-start.3) | collective-permute-done | bytes 262176 | tf_op jit(solution)/shard_map/ppermute | solution.py:71
  62.7 1.4 %fusion.10 = f32[128]{0:T(128)S(1)} fusion(bf16[32,4096]{1,0:T(8,128)(2,1)} %collective-permute-done.4, bf16[32,4096]{1,0:T(8,128)(2,1)} %collective-permute-done.3, bf16[32,4096]{1,0:T(8,128)(2,1)} %collective-permute-done.2, bf16[32,4096]{1,0:T(8,128)(2,1)S(1)} %collective-permute-done.1), kind=kLoop, calls=%fused_computation.20 | loop fusion | flops 5242752 | bytes 1049088 | tf_op jit(solution)/shard_map/jvp()/reduce_sum | solution.py:39
  64.1 1.6 %fusion.19 = f32[128,256]{1,0:T(8,128)S(1)} fusion(bf16[1,4096,256]{2,1,0:T(8,128)(2,1)S(1)} %copy-done, f32[4096]{0:T(1024)} %bitcast.149, f32[128]{0:T(128)S(1)} %fusion.81, bf16[32,4096]{1,0:T(8,128)(2,1)} %collective-permute-done.4, bf16[32,4096]{1,0:T(8,128)(2,1)} %collective-permute-done.3, bf16[32,4096]{1,0:T(8,128)(2,1)} %collective-permute-done.2, ...), kind=kOutput, calls=%fused_computation.29 | convolution fusion | flops 274202624 | bytes 3293696 | tf_op jit(solution)/shard_map/jvp()/dot_general | solution.py:44
  65.9 0.8 pad_maximum_fusion.3
  66.7 0.9 copy.38
  67.6 1.6 %copy.39 = f32[128,128]{0,1:T(8,128)} copy(f32[128,128]{1,0:T(8,128)} %get-tuple-element.20) | data formatting | bytes 131072 | tf_op jit(solution)/shard_map/jvp()/concatenate | solution.py:24
  69.2 2.7 %fusion.36 = f32[128,2,128]{0,2,1:T(8,128)S(1)} fusion(bf16[2,128,4096]{2,1,0:T(8,128)(2,1)} %bitcast.140, f32[4096]{0:T(1024)} %bitcast.150, f32[128]{0:T(128)} %copy-done.21, bf16[32,4096]{1,0:T(8,128)(2,1)} %collective-permute-done.4, bf16[32,4096]{1,0:T(8,128)(2,1)} %collective-permute-done.3, bf16[32,4096]{1,0:T(8,128)(2,1)} %collective-permute-done.2, ...), kind=kOutput, calls=%fused_computation.52 | convolution fusion | flops 274202624 | bytes 3293696 | tf_op jit(solution)/shard_map/jvp()/dot_general | solution.py:41
  72.0 0.2 fusion.57
  72.4 0.2 multiply_reduce_fusion
  72.7 0.2 broadcast_multiply_fusion
  73.1 0.4 copy-done.1
  73.5 0.8 convolution_convert_fusion
  74.5 2.1 %fusion.13 = (f32[128]{0:T(128)S(1)}, f32[128,4096]{1,0:T(8,128)S(1)}) fusion(bf16[32,4096]{1,0:T(8,128)(2,1)} %collective-permute-done.4, bf16[32,4096]{1,0:T(8,128)(2,1)} %collective-permute-done.3, bf16[32,4096]{1,0:T(8,128)(2,1)} %collective-permute-done.2, bf16[32,4096]{1,0:T(8,128)(2,1)S(1)} %collective-permute-done.1, f32[4096]{0:T(1024)S(1)} %bitcast.151, ...), kind=kOutput, calls=%fused_computation.23 | convolution fusion | flops 276889472 | bytes 6406656 | tf_op jit(solution)/shard_map/transpose(jvp())/dot_general | solution.py:44
  76.7 1.8 %fusion.35 = bf16[1,128,4096]{2,1,0:T(8,128)(2,1)S(1)} fusion(f32[128,4096]{1,0:T(8,128)S(1)} %get-tuple-element.42, bf16[1,128,4096]{2,1,0:T(8,128)(2,1)S(1)} %copy-done.2, f32[128]{0:T(128)S(1)} %multiply_multiply_fusion, f32[128]{0:T(128)S(1)} %copy-done.22, bf16[32,4096]{1,0:T(8,128)(2,1)} %collective-permute-done.4, ...), kind=kLoop, calls=%fused_computation.50 | loop fusion | flops 7864320 | bytes 5243904 | tf_op jit(solution)/shard_map/broadcast_in_dim | solution.py:86
  78.4 2.2 %collective-permute-start.5 = (bf16[1,128,4096]{2,1,0:T(8,128)(2,1)S(1)}, bf16[1,128,4096]{2,1,0:T(8,128)(2,1)S(1)}, u32[]{:S(2)}, u32[]{:S(2)}) collective-permute-start(bf16[1,128,4096]{2,1,0:T(8,128)(2,1)S(1)} %fusion.35), channel_id=1, source_target_pairs={{1,0},{2,1},{3,2},{4,3},{5,4},{6,5},{7,6},{8,7},{9,8},{10,9},{11,1... | collective-permute-start | bytes 3145736 | tf_op jit(solution)/shard_map/ppermute | solution.py:12
  80.7 13.9 %collective-permute-done.5 = bf16[1,128,4096]{2,1,0:T(8,128)(2,1)S(1)} collective-permute-done((bf16[1,128,4096]{2,1,0:T(8,128)(2,1)S(1)}, bf16[1,128,4096]{2,1,0:T(8,128)(2,1)S(1)}, u32[]{:S(2)}, u32[]{:S(2)}) %collective-permute-start.5) | collective-permute-done | bytes 1048608 | tf_op jit(solution)/shard_map/ppermute | solution.py:12
  94.5 2.3 %copy.57 = bf16[1,128,4096]{2,1,0:T(8,128)(2,1)} copy(bf16[1,128,4096]{2,1,0:T(8,128)(2,1)} %collective-permute-done) | data formatting | bytes 2097152
  96.8 1.0 copy.58
  (81 shorter events, 1.6 us)
Async XLA Ops:
  0.6 12.7 %copy-start = (bf16[1,4096,256]{2,1,0:T(8,128)(2,1)S(1)}, bf16[1,4096,256]{2,1,0:T(8,128)(2,1)}, u32[]{:S(2)}) copy-start(bf16[1,4096,256]{2,1,0:T(8,128)(2,1)} %param.13) | copy-start | bytes 6291460
  0.6 8.4 %copy-start.19 = (s32[1,2,128]{2,1,0:T(2,128)S(1)}, s32[1,2,128]{2,1,0:T(2,128)}, u32[]{:S(2)}) copy-start(s32[1,2,128]{2,1,0:T(2,128)} %param.15) | copy-start | bytes 3076
  0.7 9.0 %copy-start.3 = (bf16[1,128,4096]{2,1,0:T(8,128)(2,1)S(1)}, bf16[1,128,4096]{2,1,0:T(8,128)(2,1)}, u32[]{:S(2)}) copy-start(bf16[1,128,4096]{2,1,0:T(8,128)(2,1)} %param.8) | copy-start | bytes 3145732
  3.0 38.4 %collective-permute-start.1 = (bf16[32,4096]{1,0:T(8,128)(2,1)}, bf16[32,4096]{1,0:T(8,128)(2,1)S(1)}, u32[]{:S(2)}, u32[]{:S(2)}) collective-permute-start(bf16[32,4096]{1,0:T(8,128)(2,1)} %get-tuple-element.2), channel_id=1, source_target_pairs={{0,15},{1,14},{2,13},{3,12},{4,11},{5,10},{6,9},{7,8},{8,7},{9,6},... | collective-permute-start | bytes 786440 | tf_op jit(solution)/shard_map/ppermute | solution.py:71
  5.8 35.6 %collective-permute-start.2 = (bf16[32,4096]{1,0:T(8,128)(2,1)}, bf16[32,4096]{1,0:T(8,128)(2,1)}, u32[]{:S(2)}, u32[]{:S(2)}) collective-permute-start(bf16[32,4096]{1,0:T(8,128)(2,1)} %get-tuple-element.3), channel_id=1, source_target_pairs={{0,15},{1,14},{2,13},{3,12},{4,11},{5,10},{6,9},{7,8},{8,7},{9,6},... | collective-permute-start | bytes 786440 | tf_op jit(solution)/shard_map/ppermute | solution.py:71
  5.9 45.9 %collective-permute-start.4 = (bf16[32,4096]{1,0:T(8,128)(2,1)}, bf16[32,4096]{1,0:T(8,128)(2,1)}, u32[]{:S(2)}, u32[]{:S(2)}) collective-permute-start(bf16[32,4096]{1,0:T(8,128)(2,1)} %get-tuple-element.4), channel_id=1, source_target_pairs={{0,15},{1,14},{2,13},{3,12},{4,11},{5,10},{6,9},{7,8},{8,7},{9,6},... | collective-permute-start | bytes 786440 | tf_op jit(solution)/shard_map/ppermute | solution.py:71
  8.5 54.2 %collective-permute-start.3 = (bf16[32,4096]{1,0:T(8,128)(2,1)}, bf16[32,4096]{1,0:T(8,128)(2,1)}, u32[]{:S(2)}, u32[]{:S(2)}) collective-permute-start(bf16[32,4096]{1,0:T(8,128)(2,1)} %get-tuple-element.5), channel_id=1, source_target_pairs={{0,15},{1,14},{2,13},{3,12},{4,11},{5,10},{6,9},{7,8},{8,7},{9,6},... | collective-permute-start | bytes 786440 | tf_op jit(solution)/shard_map/ppermute | solution.py:71
  13.3 2.6 %copy-start.25 = (f32[64]{0:T(128)S(1)}, f32[64]{0:T(128)}, u32[]{:S(2)}) copy-start(f32[64]{0:T(128)} %negate_power_fusion) | copy-start | bytes 772
  13.3 2.6 %copy-start.26 = (f32[128]{0:T(128)S(1)}, f32[128]{0:T(128)}, u32[]{:S(2)}) copy-start(f32[128]{0:T(128)} %subtract_convert_fusion.1) | copy-start | bytes 1540
  14.6 0.7 copy-start.7
  26.7 2.5 %copy-start.4 = (f32[128,64]{1,0:T(8,128)S(1)}, f32[128,64]{1,0:T(8,128)}, u32[]{:S(2)}) copy-start(f32[128,64]{1,0:T(8,128)} %get-tuple-element.32) | copy-start | bytes 98308
  26.7 2.5 %copy-start.8 = (f32[128,256]{1,0:T(8,128)S(1)}, f32[128,256]{1,0:T(8,128)}, u32[]{:S(2)}) copy-start(f32[128,256]{1,0:T(8,128)} %copy-done.7) | copy-start | bytes 393220
  26.7 2.5 %copy-start.13 = (f32[128,128]{0,1:T(8,128)S(1)}, f32[128,128]{0,1:T(8,128)}, u32[]{:S(2)}) copy-start(f32[128,128]{0,1:T(8,128)} %copy.31) | copy-start | bytes 196612
  26.7 2.5 %copy-start.14 = (f32[128,128]{0,1:T(8,128)S(1)}, f32[128,128]{0,1:T(8,128)}, u32[]{:S(2)}) copy-start(f32[128,128]{0,1:T(8,128)} %copy.30) | copy-start | bytes 196612
  26.7 2.5 %copy-start.15 = (f32[128,64]{1,0:T(8,128)S(1)}, f32[128,64]{1,0:T(8,128)}, u32[]{:S(2)}) copy-start(f32[128,64]{1,0:T(8,128)} %get-tuple-element.12) | copy-start | bytes 98308
  26.7 2.5 %copy-start.16 = (f32[128,64]{1,0:T(8,128)S(1)}, f32[128,64]{1,0:T(8,128)}, u32[]{:S(2)}) copy-start(f32[128,64]{1,0:T(8,128)} %get-tuple-element.13) | copy-start | bytes 98308
  30.6 6.9 %copy-start.20 = (s32[128]{0:T(128)S(1)}, s32[128]{0:T(128)}, u32[]{:S(2)}) copy-start(s32[128]{0:T(128)} %get-tuple-element.21) | copy-start | bytes 1540
  30.6 7.7 %copy-start.2 = (bf16[1,128,4096]{2,1,0:T(8,128)(2,1)S(1)}, bf16[1,128,4096]{2,1,0:T(8,128)(2,1)}, u32[]{:S(2)}) copy-start(bf16[1,128,4096]{2,1,0:T(8,128)(2,1)} %param.10) | copy-start | bytes 3145732
  34.0 46.7 %collective-permute-start = (bf16[1,128,4096]{2,1,0:T(8,128)(2,1)}, bf16[1,128,4096]{2,1,0:T(8,128)(2,1)}, u32[]{:S(2)}, u32[]{:S(2)}) collective-permute-start(bf16[1,128,4096]{2,1,0:T(8,128)(2,1)} %fusion.4), channel_id=1, source_target_pairs={{0,1},{1,2},{2,3},{3,4},{4,5},{5,6},{6,7},{7,8},{8,9},{9,10},{10,1... | collective-permute-start | bytes 3145736 | tf_op jit(solution)/shard_map/ppermute | solution.py:12
  64.1 1.7 %copy-start.23 = (f32[128]{0:T(128)}, f32[128]{0:T(128)S(1)}, u32[]{:S(2)}) copy-start(f32[128]{0:T(128)S(1)} %fusion.10) | copy-start | bytes 1540
  64.1 1.7 %copy-start.21 = (f32[128]{0:T(128)}, f32[128]{0:T(128)S(1)}, u32[]{:S(2)}) copy-start(f32[128]{0:T(128)S(1)} %fusion.81) | copy-start | bytes 1540
  64.1 1.8 %copy-start.11 = (f32[128,64]{1,0:T(8,128)S(1)}, f32[128,64]{1,0:T(8,128)}, u32[]{:S(2)}) copy-start(f32[128,64]{1,0:T(8,128)} %get-tuple-element.24) | copy-start | bytes 98308
  65.8 0.9 copy-start.5
  69.2 2.8 %copy-start.10 = (f32[128,128]{0,1:T(8,128)S(1)}, f32[128,128]{0,1:T(8,128)}, u32[]{:S(2)}) copy-start(f32[128,128]{0,1:T(8,128)} %copy.39) | copy-start | bytes 196612
  69.2 2.8 %copy-start.17 = (bf16[128,128,1]{1,0,2:T(8,128)(2,1)S(1)}, bf16[128,128,1]{1,0,2:T(8,128)(2,1)}, u32[]{:S(2)}) copy-start(bf16[128,128,1]{1,0,2:T(8,128)(2,1)} %get-tuple-element.19) | copy-start | bytes 98308
  69.2 3.0 %copy-start.9 = (bf16[128,256]{0,1:T(8,128)(2,1)S(1)}, bf16[128,256]{0,1:T(8,128)(2,1)}, u32[]{:S(2)}) copy-start(bf16[128,256]{0,1:T(8,128)(2,1)} %copy.51) | copy-start | bytes 196612
  69.2 3.2 %copy-start.6 = (f32[128,256]{1,0:T(8,128)S(1)}, f32[128,256]{1,0:T(8,128)}, u32[]{:S(2)}) copy-start(f32[128,256]{1,0:T(8,128)} %copy-done.5) | copy-start | bytes 393220
  69.2 3.4 %copy-start.12 = (f32[128,64]{1,0:T(8,128)S(1)}, f32[128,64]{1,0:T(8,128)}, u32[]{:S(2)}) copy-start(f32[128,64]{1,0:T(8,128)} %get-tuple-element.24) | copy-start | bytes 98308
  69.2 3.4 %copy-start.18 = (pred[128,128]{1,0:T(8,128)(4,1)S(1)}, pred[128,128]{1,0:T(8,128)(4,1)}, u32[]{:S(2)}) copy-start(pred[128,128]{1,0:T(8,128)(4,1)} %get-tuple-element.29) | copy-start | bytes 49156
  71.9 1.6 %copy-start.1 = (bf16[1,4096,256]{2,1,0:T(8,128)(2,1)S(1)}, bf16[1,4096,256]{2,1,0:T(8,128)(2,1)}, u32[]{:S(2)}) copy-start(bf16[1,4096,256]{2,1,0:T(8,128)(2,1)} %param.12) | copy-start | bytes 6291460
  73.0 1.5 %copy-start.27 = (f32[1,4096]{1,0:T(1,128)S(1)}, f32[1,4096]{1,0:T(1,128)}, u32[]{:S(2)}) copy-start(f32[1,4096]{1,0:T(1,128)} %param.11) | copy-start | bytes 49156
  74.5 2.2 %copy-start.24 = (f32[128]{0:T(128)S(1)}, f32[128]{0:T(128)}, u32[]{:S(2)}) copy-start(f32[128]{0:T(128)} %copy-done.23) | copy-start | bytes 1540
  74.5 2.2 %copy-start.22 = (f32[128]{0:T(128)S(1)}, f32[128]{0:T(128)}, u32[]{:S(2)}) copy-start(f32[128]{0:T(128)} %copy-done.21) | copy-start | bytes 1540
  78.4 16.1 %collective-permute-start.5 = (bf16[1,128,4096]{2,1,0:T(8,128)(2,1)S(1)}, bf16[1,128,4096]{2,1,0:T(8,128)(2,1)S(1)}, u32[]{:S(2)}, u32[]{:S(2)}) collective-permute-start(bf16[1,128,4096]{2,1,0:T(8,128)(2,1)S(1)} %fusion.35), channel_id=1, source_target_pairs={{1,0},{2,1},{3,2},{4,3},{5,4},{6,5},{7,6},{8,7},{9,8},{10,9},{11,1... | collective-permute-start | bytes 3145736 | tf_op jit(solution)/shard_map/ppermute | solution.py:12

commit v3 on v1

--- a/solution.py
+++ b/solution.py
@@ -38,23 +38,26 @@
     values32 = acts.astype(jnp.float32)
     scale = lax.rsqrt(jnp.mean(values32 * values32, axis=-1, keepdims=True) + 1e-05)
     normed = (values32 * scale * gain).astype(jnp.bfloat16)
-    query = jnp.dot(normed, w_query, preferred_element_type=jnp.float32).reshape(
-        rows, heads, head_dim
-    )
+    query = jnp.dot(normed, w_query, preferred_element_type=jnp.float32)
     keyval = jnp.dot(normed, w_kv, preferred_element_type=jnp.float32)
     cosine, sine_part = rotary_tables(segment, head_dim)
-    query = rotary(query, cosine[:, None, :], sine_part[:, None, :]).astype(jnp.bfloat16)
     keys = rotary(keyval[:, :head_dim], cosine, sine_part).astype(jnp.bfloat16)
     values = keyval[:, head_dim:].astype(jnp.bfloat16)
-    scores = jnp.einsum("qhd,kd->hqk", query, keys, preferred_element_type=jnp.float32) / math.sqrt(
-        head_dim
-    )
     index = jnp.arange(rows, dtype=jnp.int32)
     allowed = (segment[:, None] == segment[None, :]) & (index[None, :] <= index[:, None])
-    expd = jnp.where(allowed[None], jnp.exp(scores), jnp.zeros_like(scores))
-    probs = (expd / jnp.sum(expd, axis=-1, keepdims=True)).astype(jnp.bfloat16)
-    mixed = jnp.einsum("hqk,kd->qhd", probs, values, preferred_element_type=jnp.float32)
-    mixed = mixed.astype(jnp.bfloat16).reshape(rows, heads * head_dim)
+    mixed = []
+    for head in range(heads):
+        part = query[:, head * head_dim : (head + 1) * head_dim]
+        part = rotary(part, cosine, sine_part).astype(jnp.bfloat16)
+        scores = lax.dot_general(
+            part, keys, (((1,), (1,)), ((), ())), preferred_element_type=jnp.float32
+        ) / math.sqrt(head_dim)
+        expd = jnp.where(allowed, jnp.exp(scores), jnp.zeros_like(scores))
+        probs = (expd / jnp.sum(expd, axis=-1, keepdims=True)).astype(jnp.bfloat16)
+        mixed.append(
+            jnp.dot(probs, values, preferred_element_type=jnp.float32).astype(jnp.bfloat16)
+        )
+    mixed = jnp.concatenate(mixed, -1)
     return (values32 + jnp.dot(mixed, w_out, preferred_element_type=jnp.float32)).astype(
         jnp.bfloat16
     )

time: 90.8 us -> 86.1 us (0.948)
  waiting for transfers between devices: 43.4 us -> 59.4 us
  local copies, waits for them, and re-layouts: 12.6 us -> 3.19 us
  matrix products: 18.3 us -> 9.56 us
  other arithmetic: 7.75 us -> 5.61 us
    ppermute x1, waiting for transfers between devices: 29.6 us -> 45.7 us  [shards(): fetched = lax.ppermute(stash[0], 'section', mirror)]
    dot_general x2, matrix products: 6.06 us -> 1.29 us  [section_layer(): jnp.dot(mixed, w_out, preferred_element_type=jnp.float32)]
    dot_general x1 -> x0, local copies, waits for them, and re-layouts: 4.13 us -> none  [section_layer(): jnp.dot(normed, w_query, preferred_element_type=jnp.float32)]
    dot_general x10 -> x17, matrix products: 8.98 us -> 4.93 us  [the longest x8 1.91 us: section_layer(): lax.dot_general(part, keys, (((1,), (1,)), ((), ())), preferred_element_t...]
    concatenate x4 -> x0, local copies, waits for them, and re-layouts: 2.47 us -> none  [the longest x2 1.66 us: rotary_tables(): sine_part = jnp.concatenate([jnp.sin(angles), jnp.sin(angles)], -1)]
    unnamed x42 -> x14, local copies, waits for them, and re-layouts: 4.13 us -> 2.21 us
    concatenate x3 -> x0, other arithmetic: 0.92 us -> none  [the longest x2 0.84 us: rotary_tables(): cosine = jnp.concatenate([jnp.cos(angles), jnp.cos(angles)], -1)]
  transfers between devices with their start and end apart: 3 -> 3, of which waited for: 2 -> 2; matrix products, arithmetic and copies ran while one was open for 38% -> 19% of each run, Pallas kernels for 0% -> 0%
where the time goes in v3:
time: 86.1 us; the launch traced here: 85.9 us
  waiting for transfers between devices  59.4 us (69%)
  matrix products  9.56 us (11%)
  starting transfers between devices  7.15 us (8%)
  other arithmetic  5.61 us (7%)
  local copies, waits for them, and re-layouts  3.19 us (4%)
  between operations  0.96 us (1%)
    ppermute x1, waiting for transfers between devices, shards(): fetched = lax.ppermute(stash[0], 'section', mirror)  45.7 us
    ppermute x2, waiting for transfers between devices, shifted(): lax.ppermute(value, axis, [(source, source + steps) for source in range(l...  13.7 us
    ppermute x2, starting transfers between devices, shifted(): lax.ppermute(value, axis, [(source, source + steps) for source in range(l...  4.28 us
    dot_general x3, matrix products, section_layer(): keyval = jnp.dot(normed, w_kv, preferred_element_type=jnp.float32)  3.35 us
    ppermute x1, starting transfers between devices, shards(): fetched = lax.ppermute(stash[0], 'section', mirror)  2.88 us
    unnamed x14, local copies, waits for them, and re-layouts  2.21 us
    dot_general x8, matrix products, section_layer(): lax.dot_general(part, keys, (((1,), (1,)), ((), ())), preferred_element_t...  1.91 us
    dot_general x3, matrix products, section_layer(): query = jnp.dot(normed, w_query, preferred_element_type=jnp.float32)  1.85 us
  transfers between devices with their start and end apart: 3, of which 2 were waited for; matrix products, arithmetic and copies ran while one was open for 19% of the time, Pallas kernels for 0%

profile of v3, /device:TPU:9, one launch (start us, length us, event | category | flops | bytes accessed | tf_op | source)
XLA Modules:
  0.0 85.9 jit_solution(7591512837775977904)
XLA Ops:
  0.6 2.9 %collective-permute-start.1 = (bf16[128,4096]{1,0:T(8,128)(2,1)}, bf16[128,4096]{1,0:T(8,128)(2,1)S(1)}, u32[]{:S(2)}, u32[]{:S(2)}) collective-permute-start(bf16[128,4096]{1,0:T(8,128)(2,1)} %bitcast.66), channel_id=1, source_target_pairs={{0,15},{1,14},{2,13},{3,12},{4,11},{5,10},{6,9},{7,8},{8,7},{9,6},... | collective-permute-start | bytes 3145736 | tf_op jit(solution)/shard_map/ppermute | solution.py:69
  3.5 0.9 %compare_bitcast_fusion = (pred[127,1]{0,1:T(4,128)(4,1)S(1)}, pred[127,1]{0,1:T(4,128)(4,1)S(1)}) fusion(s32[1,2,128]{2,1,0:T(2,128)} %param.15), kind=kLoop, calls=%fused_computation.154 | loop fusion | flops 254 | bytes 2286 | tf_op jit(solution)/shard_map/jvp()/concatenate | solution.py:17
  4.4 0.8 slice_bitcast_fusion
  5.3 0.1 copy.17
  5.4 0.2 reduce-window.17
  5.6 0.1 reduce.1
  5.7 0.1 copy.16
  5.8 0.2 reduce-window.16
  6.0 0.1 reduce
  6.1 1.5 %fusion.6 = f32[128]{0:T(128)S(1)} fusion(bf16[1,128,4096]{2,1,0:T(8,128)(2,1)} %param.8), kind=kLoop, calls=%fused_computation.16 | loop fusion | flops 1572736 | bytes 1049088 | tf_op jit(solution)/shard_map/reduce_sum | solution.py:39
  7.7 1.9 %fusion.20 = f32[128,256]{1,0:T(8,128)S(1)} fusion(bf16[1,4096,256]{2,1,0:T(8,128)(2,1)S(1)} %copy-done, bf16[1,128,4096]{2,1,0:T(8,128)(2,1)} %param.8, f32[4096]{0:T(1024)} %bitcast.61, f32[128]{0:T(128)S(1)} %add_rsqrt_fusion), kind=kOutput, calls=%fused_computation.30 | convolution fusion | flops 270532608 | bytes 3293696 | tf_op jit(solution)/shard_map/dot_general | solution.py:42
  9.6 0.2 copy-done.4
  9.9 0.5 fusion.25
  10.4 0.1 slice_negate_fusion.8
  10.5 0.5 multiply_cosine_fusion
  11.0 0.3 fusion.108
  11.4 0.2 convolution_convert_fusion.11
  11.6 0.3 fusion.107
  11.9 0.2 convolution_convert_fusion.10
  12.1 0.5 fusion.4
  12.6 1.9 %collective-permute-start = (bf16[1,128,4096]{2,1,0:T(8,128)(2,1)S(1)}, bf16[1,128,4096]{2,1,0:T(8,128)(2,1)S(1)}, u32[]{:S(2)}, u32[]{:S(2)}) collective-permute-start(bf16[1,128,4096]{2,1,0:T(8,128)(2,1)S(1)} %fusion.4), channel_id=1, source_target_pairs={{0,1},{1,2},{2,3},{3,4},{4,5},{5,6},{6,7},{7,8},{8,9},{9,10},{10,1... | collective-permute-start | bytes 3145736 | tf_op jit(solution)/shard_map/ppermute | solution.py:12
  14.5 0.8 fusion.27
  15.3 45.7 %collective-permute-done.1 = bf16[128,4096]{1,0:T(8,128)(2,1)S(1)} collective-permute-done((bf16[128,4096]{1,0:T(8,128)(2,1)}, bf16[128,4096]{1,0:T(8,128)(2,1)S(1)}, u32[]{:S(2)}, u32[]{:S(2)}) %collective-permute-start.1) | collective-permute-done | bytes 1048608 | tf_op jit(solution)/shard_map/ppermute | solution.py:69
  61.0 0.3 fusion.10
  61.3 0.5 fusion.23
  61.9 0.1 slice_negate_fusion.5
  62.0 0.5 fusion.18
  62.6 0.1 fusion.59
  62.7 0.1 fusion.61
  62.8 0.2 fusion.30
  63.0 0.2 fusion.80
  63.2 0.2 multiply_reduce_fusion.1
  63.4 0.2 convolution_convert_fusion.8
  63.6 0.2 multiply_reduce_fusion
  63.8 0.2 convolution_convert_fusion.4
  64.0 0.3 fusion.36
  64.3 0.2 fusion.40
  64.5 0.3 fusion.37
  64.7 0.2 fusion.90
  65.1 0.1 fusion.106
  65.2 0.1 pad_add_fusion.2
  65.4 0.8 convolution_convert_fusion
  66.2 1.0 %fusion.13 = (f32[128]{0:T(128)S(1)}, f32[128,4096]{1,0:T(8,128)S(1)}) fusion(bf16[128,4096]{1,0:T(8,128)(2,1)S(1)} %collective-permute-done.1, f32[4096]{0:T(1024)S(1)} %bitcast.65, bf16[128,4096]{1,0:T(8,128)(2,1)S(1)} %convolution_convert_fusion, bf16[1,4096,256]{2,1,0:T(8,128)(2,1)S(1)} %copy-done, f32[128,128]{1,0:T(8,128)S(1)} %get-tuple-element.18, ...), kind=kOutput, calls=%fused_computation.23 | convolution fusion | flops 272170880 | bytes 6406656 | tf_op jit(solution)/shard_map/transpose(jvp())/dot_general | solution.py:42
  67.2 0.7 fusion.43
  67.8 2.4 %collective-permute-start.2 = (bf16[1,128,4096]{2,1,0:T(8,128)(2,1)S(1)}, bf16[1,128,4096]{2,1,0:T(8,128)(2,1)S(1)}, u32[]{:S(2)}, u32[]{:S(2)}) collective-permute-start(bf16[1,128,4096]{2,1,0:T(8,128)(2,1)S(1)} %fusion.43), channel_id=1, source_target_pairs={{1,0},{2,1},{3,2},{4,3},{5,4},{6,5},{7,6},{8,7},{9,8},{10,9},{11,1... | collective-permute-start | bytes 3145736 | tf_op jit(solution)/shard_map/ppermute | solution.py:12
  70.2 13.7 %collective-permute-done.2 = bf16[1,128,4096]{2,1,0:T(8,128)(2,1)S(1)} collective-permute-done((bf16[1,128,4096]{2,1,0:T(8,128)(2,1)S(1)}, bf16[1,128,4096]{2,1,0:T(8,128)(2,1)S(1)}, u32[]{:S(2)}, u32[]{:S(2)}) %collective-permute-start.2) | collective-permute-done | bytes 1048608 | tf_op jit(solution)/shard_map/ppermute | solution.py:12
  84.0 1.0 %copy.28 = bf16[1,128,4096]{2,1,0:T(8,128)(2,1)} copy(bf16[1,128,4096]{2,1,0:T(8,128)(2,1)S(1)} %collective-permute-done) | data formatting | bytes 2097152
  84.9 1.0 %copy.29 = bf16[1,128,4096]{2,1,0:T(8,128)(2,1)} copy(bf16[1,128,4096]{2,1,0:T(8,128)(2,1)S(1)} %collective-permute-done.2) | data formatting | bytes 2097152
  (27 shorter events, 0.5 us)
Async XLA Ops:
  0.6 7.0 %copy-start = (bf16[1,4096,256]{2,1,0:T(8,128)(2,1)S(1)}, bf16[1,4096,256]{2,1,0:T(8,128)(2,1)}, u32[]{:S(2)}) copy-start(bf16[1,4096,256]{2,1,0:T(8,128)(2,1)} %param.13) | copy-start | bytes 6291460
  0.6 60.4 %collective-permute-start.1 = (bf16[128,4096]{1,0:T(8,128)(2,1)}, bf16[128,4096]{1,0:T(8,128)(2,1)S(1)}, u32[]{:S(2)}, u32[]{:S(2)}) collective-permute-start(bf16[128,4096]{1,0:T(8,128)(2,1)} %bitcast.66), channel_id=1, source_target_pairs={{0,15},{1,14},{2,13},{3,12},{4,11},{5,10},{6,9},{7,8},{8,7},{9,6},... | collective-permute-start | bytes 3145736 | tf_op jit(solution)/shard_map/ppermute | solution.py:69
  7.6 2.0 %copy-start.3 = (bf16[1,128,4096]{2,1,0:T(8,128)(2,1)S(1)}, bf16[1,128,4096]{2,1,0:T(8,128)(2,1)}, u32[]{:S(2)}) copy-start(bf16[1,128,4096]{2,1,0:T(8,128)(2,1)} %param.8) | copy-start | bytes 3145732
  7.6 2.2 %copy-start.4 = (bf16[1,4096,256]{2,1,0:T(8,128)(2,1)S(1)}, bf16[1,4096,256]{2,1,0:T(8,128)(2,1)}, u32[]{:S(2)}) copy-start(bf16[1,4096,256]{2,1,0:T(8,128)(2,1)} %param.12) | copy-start | bytes 6291460
  7.6 2.2 %copy-start.5 = (f32[1,4096]{1,0:T(1,128)S(1)}, f32[1,4096]{1,0:T(1,128)}, u32[]{:S(2)}) copy-start(f32[1,4096]{1,0:T(1,128)} %param.11) | copy-start | bytes 49156
  10.4 1.7 %copy-start.1 = (bf16[1,256,4096]{2,1,0:T(8,128)(2,1)S(1)}, bf16[1,256,4096]{2,1,0:T(8,128)(2,1)}, u32[]{:S(2)}) copy-start(bf16[1,256,4096]{2,1,0:T(8,128)(2,1)} %param.14) | copy-start | bytes 6291460
  12.1 2.4 %copy-start.2 = (bf16[1,128,4096]{2,1,0:T(8,128)(2,1)S(1)}, bf16[1,128,4096]{2,1,0:T(8,128)(2,1)}, u32[]{:S(2)}) copy-start(bf16[1,128,4096]{2,1,0:T(8,128)(2,1)} %param.10) | copy-start | bytes 3145732
  12.6 57.7 %collective-permute-start = (bf16[1,128,4096]{2,1,0:T(8,128)(2,1)S(1)}, bf16[1,128,4096]{2,1,0:T(8,128)(2,1)S(1)}, u32[]{:S(2)}, u32[]{:S(2)}) collective-permute-start(bf16[1,128,4096]{2,1,0:T(8,128)(2,1)S(1)} %fusion.4), channel_id=1, source_target_pairs={{0,1},{1,2},{2,3},{3,4},{4,5},{5,6},{6,7},{7,8},{8,9},{9,10},{10,1... | collective-permute-start | bytes 3145736 | tf_op jit(solution)/shard_map/ppermute | solution.py:12
  67.8 16.1 %collective-permute-start.2 = (bf16[1,128,4096]{2,1,0:T(8,128)(2,1)S(1)}, bf16[1,128,4096]{2,1,0:T(8,128)(2,1)S(1)}, u32[]{:S(2)}, u32[]{:S(2)}) collective-permute-start(bf16[1,128,4096]{2,1,0:T(8,128)(2,1)S(1)} %fusion.43), channel_id=1, source_target_pairs={{1,0},{2,1},{3,2},{4,3},{5,4},{6,5},{7,6},{8,7},{9,8},{10,9},{11,1... | collective-permute-start | bytes 3145736 | tf_op jit(solution)/shard_map/ppermute | solution.py:12

commit v4 on v3

--- a/solution.py
+++ b/solution.py
@@ -77,7 +77,11 @@
     unused, pullback = jax.vjp(replay, fetched)
     gradient = pullback(cotangent[0])[0]
     forwarded = shifted(outward[None], "section", 1)
-    returned = shifted(gradient[None], "section", -1)
+    half = gradient.shape[0] // 2
+    returned = jnp.concatenate(
+        [shifted(gradient[None, :half], "section", -1), shifted(gradient[None, half:], "section", -1)],
+        1,
+    )
     return (forwarded, returned)
 
 

time: 86.1 us -> 86.4 us (level)
  starting transfers between devices: 7.15 us -> 9.07 us
  waiting for transfers between devices: 59.4 us -> 57.5 us
  other arithmetic: 5.61 us -> 6.61 us
    ppermute x2 -> x3, waiting for transfers between devices: 13.7 us -> 11.8 us  [shifted(): lax.ppermute(value, axis, [(source, source + steps) for source in range(l...]
    ppermute x2 -> x3, starting transfers between devices: 4.28 us -> 6.2 us  [shifted(): lax.ppermute(value, axis, [(source, source + steps) for source in range(l...]
    concatenate x0 -> x1, other arithmetic: none -> 1.06 us  [shards(): jnp.concatenate([shifted(gradient[None, :half], 'section', -1), shifted(g...]
    unnamed x14 -> x13, local copies, waits for them, and re-layouts: 2.21 us -> 1.33 us
  transfers between devices with their start and end apart: 3 -> 4, of which waited for: 2 -> 3; matrix products, arithmetic and copies ran while one was open for 19% -> 19% of each run, Pallas kernels for 0% -> 0%
where the time goes in v4:
time: 86.4 us; the launch traced here: 86.1 us
  waiting for transfers between devices  57.5 us (67%)
  matrix products  9.57 us (11%)
  starting transfers between devices  9.07 us (10%)
  other arithmetic  6.61 us (8%)
  local copies, waits for them, and re-layouts  2.39 us (3%)
  between operations  0.97 us (1%)
    ppermute x1, waiting for transfers between devices, shards(): fetched = lax.ppermute(stash[0], 'section', mirror)  45.7 us
    ppermute x3, waiting for transfers between devices, shifted(): lax.ppermute(value, axis, [(source, source + steps) for source in range(l...  11.8 us
    ppermute x3, starting transfers between devices, shifted(): lax.ppermute(value, axis, [(source, source + steps) for source in range(l...  6.2 us
    dot_general x3, matrix products, section_layer(): keyval = jnp.dot(normed, w_kv, preferred_element_type=jnp.float32)  3.36 us
    ppermute x1, starting transfers between devices, shards(): fetched = lax.ppermute(stash[0], 'section', mirror)  2.88 us
    dot_general x8, matrix products, section_layer(): lax.dot_general(part, keys, (((1,), (1,)), ((), ())), preferred_element_t...  1.91 us
    dot_general x3, matrix products, section_layer(): query = jnp.dot(normed, w_query, preferred_element_type=jnp.float32)  1.85 us
    reduce_sum x2, other arithmetic, section_layer(): jnp.mean(values32 * values32, axis=-1, keepdims=True) + 1e-05  1.81 us
  transfers between devices with their start and end apart: 4, of which 3 were waited for; matrix products, arithmetic and copies ran while one was open for 19% of the time, Pallas kernels for 0%

profile of v4, /device:TPU:9, one launch (start us, length us, event | category | flops | bytes accessed | tf_op | source)
XLA Modules:
  0.0 86.1 jit_solution(2592352470203356092)
XLA Ops:
  0.6 2.9 %collective-permute-start.1 = (bf16[128,4096]{1,0:T(8,128)(2,1)}, bf16[128,4096]{1,0:T(8,128)(2,1)S(1)}, u32[]{:S(2)}, u32[]{:S(2)}) collective-permute-start(bf16[128,4096]{1,0:T(8,128)(2,1)} %bitcast.68), channel_id=1, source_target_pairs={{0,15},{1,14},{2,13},{3,12},{4,11},{5,10},{6,9},{7,8},{8,7},{9,6},... | collective-permute-start | bytes 3145736 | tf_op jit(solution)/shard_map/ppermute | solution.py:69
  3.5 0.9 %compare_bitcast_fusion = (pred[127,1]{0,1:T(4,128)(4,1)S(1)}, pred[127,1]{0,1:T(4,128)(4,1)S(1)}) fusion(s32[1,2,128]{2,1,0:T(2,128)} %param.15), kind=kLoop, calls=%fused_computation.156 | loop fusion | flops 254 | bytes 2286 | tf_op jit(solution)/shard_map/jvp()/concatenate | solution.py:17
  4.4 0.8 slice_bitcast_fusion.2
  5.3 0.1 copy.17
  5.4 0.2 reduce-window.17
  5.6 0.1 reduce.1
  5.7 0.1 copy.16
  5.8 0.2 reduce-window.16
  6.0 0.1 reduce
  6.1 1.5 %fusion.6 = f32[128]{0:T(128)S(1)} fusion(bf16[1,128,4096]{2,1,0:T(8,128)(2,1)} %param.8), kind=kLoop, calls=%fused_computation.16 | loop fusion | flops 1572736 | bytes 1049088 | tf_op jit(solution)/shard_map/reduce_sum | solution.py:39
  7.7 1.9 %fusion.20 = f32[128,256]{1,0:T(8,128)S(1)} fusion(bf16[1,4096,256]{2,1,0:T(8,128)(2,1)S(1)} %copy-done, bf16[1,128,4096]{2,1,0:T(8,128)(2,1)} %param.8, f32[4096]{0:T(1024)} %bitcast.63, f32[128]{0:T(128)S(1)} %add_rsqrt_fusion), kind=kOutput, calls=%fused_computation.30 | convolution fusion | flops 270532608 | bytes 3293696 | tf_op jit(solution)/shard_map/dot_general | solution.py:42
  9.5 0.3 copy-done.4
  9.9 0.5 fusion.25
  10.4 0.1 slice_negate_fusion.7
  10.5 0.5 multiply_cosine_fusion
  11.1 0.3 fusion.107
  11.4 0.2 convolution_convert_fusion.11
  11.6 0.3 fusion.106
  11.9 0.2 convolution_convert_fusion.10
  12.1 0.5 fusion.4
  12.6 1.9 %collective-permute-start = (bf16[1,128,4096]{2,1,0:T(8,128)(2,1)S(1)}, bf16[1,128,4096]{2,1,0:T(8,128)(2,1)S(1)}, u32[]{:S(2)}, u32[]{:S(2)}) collective-permute-start(bf16[1,128,4096]{2,1,0:T(8,128)(2,1)S(1)} %fusion.4), channel_id=1, source_target_pairs={{0,1},{1,2},{2,3},{3,4},{4,5},{5,6},{6,7},{7,8},{8,9},{9,10},{10,1... | collective-permute-start | bytes 3145736 | tf_op jit(solution)/shard_map/ppermute | solution.py:12
  14.5 0.8 fusion.27
  15.4 45.7 %collective-permute-done.1 = bf16[128,4096]{1,0:T(8,128)(2,1)S(1)} collective-permute-done((bf16[128,4096]{1,0:T(8,128)(2,1)}, bf16[128,4096]{1,0:T(8,128)(2,1)S(1)}, u32[]{:S(2)}, u32[]{:S(2)}) %collective-permute-start.1) | collective-permute-done | bytes 1048608 | tf_op jit(solution)/shard_map/ppermute | solution.py:69
  61.0 0.3 fusion.10
  61.3 0.5 fusion.23
  62.0 0.5 fusion.18
  62.6 0.1 fusion.58
  62.7 0.1 fusion.60
  62.8 0.2 fusion.30
  63.0 0.2 fusion.79
  63.2 0.2 multiply_reduce_fusion.1
  63.4 0.2 convolution_convert_fusion.8
  63.6 0.2 multiply_reduce_fusion
  63.8 0.2 convolution_convert_fusion.4
  64.0 0.3 fusion.36
  64.3 0.2 fusion.40
  64.5 0.3 fusion.37
  64.7 0.2 fusion.89
  65.2 0.1 pad_add_fusion.2
  65.4 0.8 convolution_convert_fusion
  66.2 1.0 %fusion.13 = (f32[128]{0:T(128)S(1)}, f32[128,4096]{1,0:T(8,128)S(1)}) fusion(bf16[128,4096]{1,0:T(8,128)(2,1)S(1)} %collective-permute-done.1, f32[4096]{0:T(1024)S(1)} %bitcast.67, bf16[128,4096]{1,0:T(8,128)(2,1)S(1)} %convolution_convert_fusion, bf16[1,4096,256]{2,1,0:T(8,128)(2,1)S(1)} %copy-done, f32[128,128]{1,0:T(8,128)S(1)} %get-tuple-element.20, ...), kind=kOutput, calls=%fused_computation.23 | convolution fusion | flops 272170880 | bytes 6406656 | tf_op jit(solution)/shard_map/transpose(jvp())/dot_general | solution.py:42
  67.2 0.7 fusion.9
  67.9 2.4 %collective-permute-start.2 = (bf16[1,64,4096]{2,1,0:T(8,128)(2,1)S(1)}, bf16[1,64,4096]{2,1,0:T(8,128)(2,1)S(1)}, u32[]{:S(2)}, u32[]{:S(2)}) collective-permute-start(bf16[1,64,4096]{2,1,0:T(8,128)(2,1)S(1)} %get-tuple-element.4), channel_id=1, source_target_pairs={{1,0},{2,1},{3,2},{4,3},{5,4},{6,5},{7,6},{8,7},{9,8},{10,9},{11,1... | collective-permute-start | bytes 1572872 | tf_op jit(solution)/shard_map/ppermute | solution.py:12
  70.3 1.9 %collective-permute-start.3 = (bf16[1,64,4096]{2,1,0:T(8,128)(2,1)S(1)}, bf16[1,64,4096]{2,1,0:T(8,128)(2,1)S(1)}, u32[]{:S(2)}, u32[]{:S(2)}) collective-permute-start(bf16[1,64,4096]{2,1,0:T(8,128)(2,1)S(1)} %get-tuple-element.5), channel_id=1, source_target_pairs={{1,0},{2,1},{3,2},{4,3},{5,4},{6,5},{7,6},{8,7},{9,8},{10,9},{11,1... | collective-permute-start | bytes 1572872 | tf_op jit(solution)/shard_map/ppermute | solution.py:12
  72.2 6.2 %collective-permute-done.2 = bf16[1,64,4096]{2,1,0:T(8,128)(2,1)S(1)} collective-permute-done((bf16[1,64,4096]{2,1,0:T(8,128)(2,1)S(1)}, bf16[1,64,4096]{2,1,0:T(8,128)(2,1)S(1)}, u32[]{:S(2)}, u32[]{:S(2)}) %collective-permute-start.2) | collective-permute-done | bytes 524320 | tf_op jit(solution)/shard_map/ppermute | solution.py:12
  78.4 5.6 %collective-permute-done.3 = bf16[1,64,4096]{2,1,0:T(8,128)(2,1)S(1)} collective-permute-done((bf16[1,64,4096]{2,1,0:T(8,128)(2,1)S(1)}, bf16[1,64,4096]{2,1,0:T(8,128)(2,1)S(1)}, u32[]{:S(2)}, u32[]{:S(2)}) %collective-permute-start.3) | collective-permute-done | bytes 524320 | tf_op jit(solution)/shard_map/ppermute | solution.py:12
  84.1 1.1 %pad_maximum_fusion = bf16[1,128,4096]{2,1,0:T(8,128)(2,1)} fusion(bf16[1,64,4096]{2,1,0:T(8,128)(2,1)S(1)} %collective-permute-done.3, bf16[1,64,4096]{2,1,0:T(8,128)(2,1)S(1)} %collective-permute-done.2), kind=kLoop, calls=%fused_computation.66 | loop fusion | flops 2097152 | bytes 2097152 | tf_op jit(solution)/shard_map/concatenate | solution.py:81
  85.1 1.0 %copy.27 = bf16[1,128,4096]{2,1,0:T(8,128)(2,1)} copy(bf16[1,128,4096]{2,1,0:T(8,128)(2,1)S(1)} %collective-permute-done) | data formatting | bytes 2097152
  (29 shorter events, 0.7 us)
Async XLA Ops:
  0.6 7.0 %copy-start = (bf16[1,4096,256]{2,1,0:T(8,128)(2,1)S(1)}, bf16[1,4096,256]{2,1,0:T(8,128)(2,1)}, u32[]{:S(2)}) copy-start(bf16[1,4096,256]{2,1,0:T(8,128)(2,1)} %param.13) | copy-start | bytes 6291460
  0.6 60.4 %collective-permute-start.1 = (bf16[128,4096]{1,0:T(8,128)(2,1)}, bf16[128,4096]{1,0:T(8,128)(2,1)S(1)}, u32[]{:S(2)}, u32[]{:S(2)}) collective-permute-start(bf16[128,4096]{1,0:T(8,128)(2,1)} %bitcast.68), channel_id=1, source_target_pairs={{0,15},{1,14},{2,13},{3,12},{4,11},{5,10},{6,9},{7,8},{8,7},{9,6},... | collective-permute-start | bytes 3145736 | tf_op jit(solution)/shard_map/ppermute | solution.py:69
  7.6 1.9 %copy-start.3 = (bf16[1,128,4096]{2,1,0:T(8,128)(2,1)S(1)}, bf16[1,128,4096]{2,1,0:T(8,128)(2,1)}, u32[]{:S(2)}) copy-start(bf16[1,128,4096]{2,1,0:T(8,128)(2,1)} %param.8) | copy-start | bytes 3145732
  7.6 2.2 %copy-start.4 = (bf16[1,4096,256]{2,1,0:T(8,128)(2,1)S(1)}, bf16[1,4096,256]{2,1,0:T(8,128)(2,1)}, u32[]{:S(2)}) copy-start(bf16[1,4096,256]{2,1,0:T(8,128)(2,1)} %param.12) | copy-start | bytes 6291460
  7.6 2.2 %copy-start.5 = (f32[1,4096]{1,0:T(1,128)S(1)}, f32[1,4096]{1,0:T(1,128)}, u32[]{:S(2)}) copy-start(f32[1,4096]{1,0:T(1,128)} %param.11) | copy-start | bytes 49156
  10.4 1.7 %copy-start.1 = (bf16[1,256,4096]{2,1,0:T(8,128)(2,1)S(1)}, bf16[1,256,4096]{2,1,0:T(8,128)(2,1)}, u32[]{:S(2)}) copy-start(bf16[1,256,4096]{2,1,0:T(8,128)(2,1)} %param.14) | copy-start | bytes 6291460
  12.1 2.4 %copy-start.2 = (bf16[1,128,4096]{2,1,0:T(8,128)(2,1)S(1)}, bf16[1,128,4096]{2,1,0:T(8,128)(2,1)}, u32[]{:S(2)}) copy-start(bf16[1,128,4096]{2,1,0:T(8,128)(2,1)} %param.10) | copy-start | bytes 3145732
  12.6 59.7 %collective-permute-start = (bf16[1,128,4096]{2,1,0:T(8,128)(2,1)S(1)}, bf16[1,128,4096]{2,1,0:T(8,128)(2,1)S(1)}, u32[]{:S(2)}, u32[]{:S(2)}) collective-permute-start(bf16[1,128,4096]{2,1,0:T(8,128)(2,1)S(1)} %fusion.4), channel_id=1, source_target_pairs={{0,1},{1,2},{2,3},{3,4},{4,5},{5,6},{6,7},{7,8},{8,9},{9,10},{10,1... | collective-permute-start | bytes 3145736 | tf_op jit(solution)/shard_map/ppermute | solution.py:12
  67.9 10.5 %collective-permute-start.2 = (bf16[1,64,4096]{2,1,0:T(8,128)(2,1)S(1)}, bf16[1,64,4096]{2,1,0:T(8,128)(2,1)S(1)}, u32[]{:S(2)}, u32[]{:S(2)}) collective-permute-start(bf16[1,64,4096]{2,1,0:T(8,128)(2,1)S(1)} %get-tuple-element.4), channel_id=1, source_target_pairs={{1,0},{2,1},{3,2},{4,3},{5,4},{6,5},{7,6},{8,7},{9,8},{10,9},{11,1... | collective-permute-start | bytes 1572872 | tf_op jit(solution)/shard_map/ppermute | solution.py:12
  70.3 13.8 %collective-permute-start.3 = (bf16[1,64,4096]{2,1,0:T(8,128)(2,1)S(1)}, bf16[1,64,4096]{2,1,0:T(8,128)(2,1)S(1)}, u32[]{:S(2)}, u32[]{:S(2)}) collective-permute-start(bf16[1,64,4096]{2,1,0:T(8,128)(2,1)S(1)} %get-tuple-element.5), channel_id=1, source_target_pairs={{1,0},{2,1},{3,2},{4,3},{5,4},{6,5},{7,6},{8,7},{9,8},{10,9},{11,1... | collective-permute-start | bytes 1572872 | tf_op jit(solution)/shard_map/ppermute | solution.py:12

commit v5 on v3

--- a/solution.py
+++ b/solution.py
@@ -74,6 +74,7 @@
     def replay(acts):
         return section_layer(acts, norm_gain[0], w_query[0], w_kv[0], w_out[0], doc_ids[0, 1])
 
+    outward, fetched = lax.optimization_barrier((outward, fetched))
     unused, pullback = jax.vjp(replay, fetched)
     gradient = pullback(cotangent[0])[0]
     forwarded = shifted(outward[None], "section", 1)

time: 86.1 us -> 87.3 us (1.014)
  starting transfers between devices: 7.15 us -> 8.44 us
    ppermute x1, waiting for transfers between devices: 45.7 us -> 36.4 us  [shards(): fetched = lax.ppermute(stash[0], 'section', mirror)]
    ppermute x2, waiting for transfers between devices: 13.7 us -> 22.2 us  [shifted(): lax.ppermute(value, axis, [(source, source + steps) for source in range(l...]
    ppermute x2, starting transfers between devices: 4.28 us -> 5.56 us  [shifted(): lax.ppermute(value, axis, [(source, source + steps) for source in range(l...]
  transfers between devices with their start and end apart: 3 -> 3, of which waited for: 2 -> 3; matrix products, arithmetic and copies ran while one was open for 19% -> 11% of each run, Pallas kernels for 0% -> 0%
where the time goes in v5:
time: 87.3 us; the launch traced here: 86.4 us
  waiting for transfers between devices  58.6 us (67%)
  matrix products  9.56 us (11%)
  starting transfers between devices  8.44 us (10%)
  other arithmetic  5.55 us (6%)
  local copies, waits for them, and re-layouts  3.29 us (4%)
  between operations  0.94 us (1%)
    ppermute x1, waiting for transfers between devices, shards(): fetched = lax.ppermute(stash[0], 'section', mirror)  36.4 us
    ppermute x2, waiting for transfers between devices, shifted(): lax.ppermute(value, axis, [(source, source + steps) for source in range(l...  22.2 us
    ppermute x2, starting transfers between devices, shifted(): lax.ppermute(value, axis, [(source, source + steps) for source in range(l...  5.56 us
    dot_general x3, matrix products, section_layer(): keyval = jnp.dot(normed, w_kv, preferred_element_type=jnp.float32)  3.37 us
    ppermute x1, starting transfers between devices, shards(): fetched = lax.ppermute(stash[0], 'section', mirror)  2.88 us
    unnamed x14, local copies, waits for them, and re-layouts  2.3 us
    dot_general x8, matrix products, section_layer(): lax.dot_general(part, keys, (((1,), (1,)), ((), ())), preferred_element_t...  1.91 us
    dot_general x3, matrix products, section_layer(): query = jnp.dot(normed, w_query, preferred_element_type=jnp.float32)  1.83 us
  transfers between devices with their start and end apart: 3, of which 3 were waited for; matrix products, arithmetic and copies ran while one was open for 11% of the time, Pallas kernels for 0%

profile of v5, /device:TPU:9, one launch (start us, length us, event | category | flops | bytes accessed | tf_op | source)
XLA Modules:
  0.0 86.4 jit_solution(16293800296189542603)
XLA Ops:
  0.6 2.9 %collective-permute-start = (bf16[128,4096]{1,0:T(8,128)(2,1)}, bf16[128,4096]{1,0:T(8,128)(2,1)S(1)}, u32[]{:S(2)}, u32[]{:S(2)}) collective-permute-start(bf16[128,4096]{1,0:T(8,128)(2,1)} %bitcast.66), channel_id=1, source_target_pairs={{0,15},{1,14},{2,13},{3,12},{4,11},{5,10},{6,9},{7,8},{8,7},{9,6},... | collective-permute-start | bytes 3145736 | tf_op jit(solution)/shard_map/ppermute | solution.py:69
  3.5 0.9 %compare_bitcast_fusion = (pred[127,1]{0,1:T(4,128)(4,1)S(1)}, pred[127,1]{0,1:T(4,128)(4,1)S(1)}) fusion(s32[1,2,128]{2,1,0:T(2,128)} %param.15), kind=kLoop, calls=%fused_computation.153 | loop fusion | flops 254 | bytes 2286 | tf_op jit(solution)/shard_map/jvp()/concatenate | solution.py:17
  4.4 0.8 slice_bitcast_fusion
  5.2 1.5 %fusion.5 = f32[128]{0:T(128)S(1)} fusion(bf16[1,128,4096]{2,1,0:T(8,128)(2,1)} %param.8), kind=kLoop, calls=%fused_computation.15 | loop fusion | flops 1572736 | bytes 1049088 | tf_op jit(solution)/shard_map/reduce_sum | solution.py:39
  6.8 0.1 copy.16
  6.9 0.2 reduce-window.16
  7.1 0.1 reduce
  7.2 0.1 copy.17
  7.3 0.2 reduce-window.17
  7.5 0.1 reduce.1
  7.7 1.9 %fusion.19 = f32[128,256]{1,0:T(8,128)S(1)} fusion(bf16[1,4096,256]{2,1,0:T(8,128)(2,1)S(1)} %copy-done, bf16[1,128,4096]{2,1,0:T(8,128)(2,1)} %param.8, f32[4096]{0:T(1024)} %bitcast.61, f32[128]{0:T(128)S(1)} %add_rsqrt_fusion), kind=kOutput, calls=%fused_computation.29 | convolution fusion | flops 270532608 | bytes 3293696 | tf_op jit(solution)/shard_map/dot_general | solution.py:42
  9.6 0.3 copy-done.4
  9.9 0.5 fusion.24
  10.4 0.1 slice_negate_fusion.7
  10.5 0.5 multiply_cosine_fusion
  11.1 0.3 fusion.107
  11.4 0.3 fusion.106
  11.7 0.2 convolution_convert_fusion.10
  11.9 0.2 convolution_convert_fusion.11
  12.1 0.8 fusion.26
  13.0 0.5 fusion
  13.4 36.4 %collective-permute-done = bf16[128,4096]{1,0:T(8,128)(2,1)S(1)} collective-permute-done((bf16[128,4096]{1,0:T(8,128)(2,1)}, bf16[128,4096]{1,0:T(8,128)(2,1)S(1)}, u32[]{:S(2)}, u32[]{:S(2)}) %collective-permute-start) | collective-permute-done | bytes 1048608 | tf_op jit(solution)/shard_map/ppermute | solution.py:69
  49.8 0.3 fusion.9
  50.1 0.5 fusion.17
  50.6 0.5 fusion.22
  51.3 0.1 slice_negate_fusion.5
  51.4 0.1 fusion.58
  51.5 0.1 fusion.60
  51.6 0.2 fusion.29
  51.8 0.2 fusion.79
  52.0 0.2 multiply_reduce_fusion.1
  52.2 0.2 multiply_reduce_fusion
  52.4 0.2 convolution_convert_fusion.4
  52.6 0.3 fusion.35
  52.9 0.2 convolution_convert_fusion.8
  53.1 0.2 fusion.39
  53.3 0.3 fusion.36
  53.6 0.2 fusion.89
  54.0 0.1 pad_add_fusion.2
  54.2 0.8 convolution_convert_fusion
  55.0 1.0 %fusion.12 = (f32[128]{0:T(128)S(1)}, f32[128,4096]{1,0:T(8,128)S(1)}) fusion(bf16[128,4096]{1,0:T(8,128)(2,1)S(1)} %collective-permute-done, f32[4096]{0:T(1024)S(1)} %bitcast.65, bf16[128,4096]{1,0:T(8,128)(2,1)S(1)} %convolution_convert_fusion, bf16[1,4096,256]{2,1,0:T(8,128)(2,1)S(1)} %copy-done, f32[128,128]{1,0:T(8,128)S(1)} %get-tuple-element.22, ...), kind=kOutput, calls=%fused_computation.22 | convolution fusion | flops 272170880 | bytes 6406656 | tf_op jit(solution)/shard_map/transpose(jvp())/dot_general | solution.py:42
  56.0 0.7 fusion.42
  56.7 2.3 %collective-permute-start.2 = (bf16[1,128,4096]{2,1,0:T(8,128)(2,1)S(1)}, bf16[1,128,4096]{2,1,0:T(8,128)(2,1)S(1)}, u32[]{:S(2)}, u32[]{:S(2)}) collective-permute-start(bf16[1,128,4096]{2,1,0:T(8,128)(2,1)S(1)} %fusion.42), channel_id=1, source_target_pairs={{1,0},{2,1},{3,2},{4,3},{5,4},{6,5},{7,6},{8,7},{9,8},{10,9},{11,1... | collective-permute-start | bytes 3145736 | tf_op jit(solution)/shard_map/ppermute | solution.py:12
  59.0 3.3 %collective-permute-start.1 = (bf16[1,128,4096]{2,1,0:T(8,128)(2,1)S(1)}, bf16[1,128,4096]{2,1,0:T(8,128)(2,1)S(1)}, u32[]{:S(2)}, u32[]{:S(2)}) collective-permute-start(bf16[1,128,4096]{2,1,0:T(8,128)(2,1)S(1)} %bitcast.60), channel_id=1, source_target_pairs={{0,1},{1,2},{2,3},{3,4},{4,5},{5,6},{6,7},{7,8},{8,9},{9,10},{10,1... | collective-permute-start | bytes 3145736 | tf_op jit(solution)/shard_map/ppermute | solution.py:12
  62.3 21.8 %collective-permute-done.2 = bf16[1,128,4096]{2,1,0:T(8,128)(2,1)S(1)} collective-permute-done((bf16[1,128,4096]{2,1,0:T(8,128)(2,1)S(1)}, bf16[1,128,4096]{2,1,0:T(8,128)(2,1)S(1)}, u32[]{:S(2)}, u32[]{:S(2)}) %collective-permute-start.2) | collective-permute-done | bytes 1048608 | tf_op jit(solution)/shard_map/ppermute | solution.py:12
  84.0 0.4 collective-permute-done.1
  84.4 1.0 %copy.28 = bf16[1,128,4096]{2,1,0:T(8,128)(2,1)} copy(bf16[1,128,4096]{2,1,0:T(8,128)(2,1)S(1)} %collective-permute-done.1) | data formatting | bytes 2097152
  85.4 1.0 %copy.29 = bf16[1,128,4096]{2,1,0:T(8,128)(2,1)} copy(bf16[1,128,4096]{2,1,0:T(8,128)(2,1)S(1)} %collective-permute-done.2) | data formatting | bytes 2097152
  (26 shorter events, 0.5 us)
Async XLA Ops:
  0.6 7.0 %copy-start = (bf16[1,4096,256]{2,1,0:T(8,128)(2,1)S(1)}, bf16[1,4096,256]{2,1,0:T(8,128)(2,1)}, u32[]{:S(2)}) copy-start(bf16[1,4096,256]{2,1,0:T(8,128)(2,1)} %param.13) | copy-start | bytes 6291460
  0.6 49.2 %collective-permute-start = (bf16[128,4096]{1,0:T(8,128)(2,1)}, bf16[128,4096]{1,0:T(8,128)(2,1)S(1)}, u32[]{:S(2)}, u32[]{:S(2)}) collective-permute-start(bf16[128,4096]{1,0:T(8,128)(2,1)} %bitcast.66), channel_id=1, source_target_pairs={{0,15},{1,14},{2,13},{3,12},{4,11},{5,10},{6,9},{7,8},{8,7},{9,6},... | collective-permute-start | bytes 3145736 | tf_op jit(solution)/shard_map/ppermute | solution.py:69
  6.9 2.6 %copy-start.5 = (f32[1,4096]{1,0:T(1,128)S(1)}, f32[1,4096]{1,0:T(1,128)}, u32[]{:S(2)}) copy-start(f32[1,4096]{1,0:T(1,128)} %param.11) | copy-start | bytes 49156
  7.6 1.9 %copy-start.3 = (bf16[1,128,4096]{2,1,0:T(8,128)(2,1)S(1)}, bf16[1,128,4096]{2,1,0:T(8,128)(2,1)}, u32[]{:S(2)}) copy-start(bf16[1,128,4096]{2,1,0:T(8,128)(2,1)} %param.8) | copy-start | bytes 3145732
  7.6 2.2 %copy-start.4 = (bf16[1,4096,256]{2,1,0:T(8,128)(2,1)S(1)}, bf16[1,4096,256]{2,1,0:T(8,128)(2,1)}, u32[]{:S(2)}) copy-start(bf16[1,4096,256]{2,1,0:T(8,128)(2,1)} %param.12) | copy-start | bytes 6291460
  9.9 2.2 %copy-start.2 = (bf16[1,128,4096]{2,1,0:T(8,128)(2,1)S(1)}, bf16[1,128,4096]{2,1,0:T(8,128)(2,1)}, u32[]{:S(2)}) copy-start(bf16[1,128,4096]{2,1,0:T(8,128)(2,1)} %param.10) | copy-start | bytes 3145732
  10.4 1.7 %copy-start.1 = (bf16[1,256,4096]{2,1,0:T(8,128)(2,1)S(1)}, bf16[1,256,4096]{2,1,0:T(8,128)(2,1)}, u32[]{:S(2)}) copy-start(bf16[1,256,4096]{2,1,0:T(8,128)(2,1)} %param.14) | copy-start | bytes 6291460
  56.7 27.4 %collective-permute-start.2 = (bf16[1,128,4096]{2,1,0:T(8,128)(2,1)S(1)}, bf16[1,128,4096]{2,1,0:T(8,128)(2,1)S(1)}, u32[]{:S(2)}, u32[]{:S(2)}) collective-permute-start(bf16[1,128,4096]{2,1,0:T(8,128)(2,1)S(1)} %fusion.42), channel_id=1, source_target_pairs={{1,0},{2,1},{3,2},{4,3},{5,4},{6,5},{7,6},{8,7},{9,8},{10,9},{11,1... | collective-permute-start | bytes 3145736 | tf_op jit(solution)/shard_map/ppermute | solution.py:12
  59.0 25.4 %collective-permute-start.1 = (bf16[1,128,4096]{2,1,0:T(8,128)(2,1)S(1)}, bf16[1,128,4096]{2,1,0:T(8,128)(2,1)S(1)}, u32[]{:S(2)}, u32[]{:S(2)}) collective-permute-start(bf16[1,128,4096]{2,1,0:T(8,128)(2,1)S(1)} %bitcast.60), channel_id=1, source_target_pairs={{0,1},{1,2},{2,3},{3,4},{4,5},{5,6},{6,7},{7,8},{8,9},{9,10},{10,1... | collective-permute-start | bytes 3145736 | tf_op jit(solution)/shard_map/ppermute | solution.py:12

commit v6 on v5

--- a/solution.py
+++ b/solution.py
@@ -74,10 +74,15 @@
     def replay(acts):
         return section_layer(acts, norm_gain[0], w_query[0], w_kv[0], w_out[0], doc_ids[0, 1])
 
+    cut = pieces // 2 - 1
+    early = lax.ppermute(
+        outward[None], "section", [(source, source + 1) for source in range(pieces - 1) if source != cut]
+    )
     outward, fetched = lax.optimization_barrier((outward, fetched))
+    late = lax.ppermute(outward[None], "section", [(cut, cut + 1)])
+    forwarded = jnp.where(lax.axis_index("section") == cut + 1, late, early)
     unused, pullback = jax.vjp(replay, fetched)
     gradient = pullback(cotangent[0])[0]
-    forwarded = shifted(outward[None], "section", 1)
     returned = shifted(gradient[None], "section", -1)
     return (forwarded, returned)
 

time: 87.3 us -> 93.8 us (1.074)
  the two profiles are of different devices: /device:TPU:9 before, /device:TPU:19 now
where the time goes in v6:
time: 93.8 us; the launch traced here: 93.4 us
  waiting for transfers between devices  59.2 us (63%)
  matrix products  11.9 us (13%)
  other arithmetic  10.1 us (11%)
  starting transfers between devices  7.89 us (8%)
  local copies, waits for them, and re-layouts  3.39 us (4%)
  between operations  0.95 us (1%)
    ppermute x1, waiting for transfers between devices, shards(): fetched = lax.ppermute(stash[0], 'section', mirror)  31.9 us
    ppermute x1, waiting for transfers between devices, shifted(): lax.ppermute(value, axis, [(source, source + steps) for source in range(l...  27.3 us
    dot_general x2, matrix products, section_layer(): jnp.dot(mixed, w_out, preferred_element_type=jnp.float32)  3.6 us
    dot_general x3, matrix products, section_layer(): keyval = jnp.dot(normed, w_kv, preferred_element_type=jnp.float32)  3.36 us
    unnamed x17, local copies, waits for them, and re-layouts  2.4 us
    select_n x1, other arithmetic, shards(): forwarded = jnp.where(lax.axis_index('section') == cut + 1, late, early)  2.31 us
    ppermute x1, starting transfers between devices, shifted(): lax.ppermute(value, axis, [(source, source + steps) for source in range(l...  2.29 us
    ppermute x1, starting transfers between devices, shards(): lax.ppermute(outward[None], 'section', [(source, source + 1) for source i...  2.19 us
  transfers between devices with their start and end apart: 4, of which 2 were waited for; matrix products, arithmetic and copies ran while one was open for 22% of the time, Pallas kernels for 0%

profile of v6, /device:TPU:19, one launch (start us, length us, event | category | flops | bytes accessed | tf_op | source)
XLA Modules:
  0.0 93.4 jit_solution(5277677560123218585)
XLA Ops:
  0.6 1.8 %collective-permute-start = (bf16[128,4096]{1,0:T(8,128)(2,1)}, bf16[128,4096]{1,0:T(8,128)(2,1)S(1)}, u32[]{:S(2)}, u32[]{:S(2)}) collective-permute-start(bf16[128,4096]{1,0:T(8,128)(2,1)} %bitcast.66), channel_id=1, source_target_pairs={{0,15},{1,14},{2,13},{3,12},{4,11},{5,10},{6,9},{7,8},{8,7},{9,6},... | collective-permute-start | bytes 3145736 | tf_op jit(solution)/shard_map/ppermute | solution.py:69
  2.4 0.9 compare_bitcast_fusion
  3.3 0.8 slice_bitcast_fusion
  4.1 1.5 %fusion.5 = f32[128]{0:T(128)S(1)} fusion(bf16[1,128,4096]{2,1,0:T(8,128)(2,1)} %param.8), kind=kLoop, calls=%fused_computation.15 | loop fusion | flops 1572736 | bytes 1049088 | tf_op jit(solution)/shard_map/reduce_sum | solution.py:39
  5.6 1.9 %fusion.19 = f32[128,256]{1,0:T(8,128)S(1)} fusion(bf16[1,4096,256]{2,1,0:T(8,128)(2,1)S(1)} %copy-done, bf16[1,128,4096]{2,1,0:T(8,128)(2,1)} %param.8, f32[4096]{0:T(1024)} %bitcast.61, f32[128]{0:T(128)S(1)} %add_rsqrt_fusion), kind=kOutput, calls=%fused_computation.29 | convolution fusion | flops 270532608 | bytes 3293696 | tf_op jit(solution)/shard_map/dot_general | solution.py:42
  7.5 0.3 copy-done.4
  7.8 0.5 fusion.24
  8.4 0.1 copy.17
  8.5 0.2 reduce-window.17
  8.7 0.1 reduce.1
  8.8 0.5 subtract_convert_fusion
  9.3 0.1 copy.16
  9.5 0.2 reduce-window.16
  9.8 0.1 slice_negate_fusion.7
  9.9 1.3 %multiply_cosine_fusion = (f32[128,64]{1,0:T(8,128)S(1)}, f32[128,64]{1,0:T(8,128)S(1)}, f32[128,64]{1,0:T(8,128)S(1)}, f32[128,64]{1,0:T(8,128)S(1)}) fusion(f32[128]{0:T(128)} %subtract_convert_fusion, f32[64]{0:T(128)S(1)} %negate_power_fusion, f32[128]{0:T(128)S(1)} %subtract_convert_fusion.1), kind=kLoop, calls=%fused_computation.75 | loop fusion | flops 16384 | bytes 132352 | tf_op jit(solution)/shard_map/jvp()/cos | solution.py:23
  11.2 0.3 fusion.106
  11.5 0.3 fusion.107
  11.8 0.2 convolution_convert_fusion.10
  12.0 0.2 convolution_convert_fusion.11
  12.3 2.8 %fusion = bf16[128,4096]{1,0:T(8,128)(2,1)} fusion(bf16[1,128,4096]{2,1,0:T(8,128)(2,1)} %param.8, bf16[1,256,4096]{2,1,0:T(8,128)(2,1)S(1)} %copy-done.1, bf16[128,128]{1,0:T(8,128)(2,1)S(1)} %convolution_convert_fusion.10, bf16[128,128]{1,0:T(8,128)(2,1)S(1)} %convolution_convert_fusion.11), kind=kOutput, calls=%fused_computation.1 | convolution fusion | flops 270139392 | bytes 4259840 | tf_op jit(solution)/shard_map/dot_general | solution.py:61
  15.0 2.2 %collective-permute-start.2 = (bf16[1,128,4096]{2,1,0:T(8,128)(2,1)}, bf16[1,128,4096]{2,1,0:T(8,128)(2,1)}, u32[]{:S(2)}, u32[]{:S(2)}) collective-permute-start(bf16[1,128,4096]{2,1,0:T(8,128)(2,1)} %bitcast.10), channel_id=1, source_target_pairs={{0,1},{1,2},{2,3},{3,4},{4,5},{5,6},{6,7},{8,9},{9,10},{10,11},{11... | collective-permute-start | bytes 3145736 | tf_op jit(solution)/shard_map/ppermute | solution.py:78
  17.2 0.8 fusion.26
  18.1 31.9 %collective-permute-done = bf16[128,4096]{1,0:T(8,128)(2,1)S(1)} collective-permute-done((bf16[128,4096]{1,0:T(8,128)(2,1)}, bf16[128,4096]{1,0:T(8,128)(2,1)S(1)}, u32[]{:S(2)}, u32[]{:S(2)}) %collective-permute-start) | collective-permute-done | bytes 1048608 | tf_op jit(solution)/shard_map/ppermute | solution.py:69
  50.0 0.3 fusion.9
  50.3 0.5 fusion.17
  50.8 1.1 %copy-done.5 = bf16[1,4096,256]{2,1,0:T(8,128)(2,1)S(1)} copy-done((bf16[1,4096,256]{2,1,0:T(8,128)(2,1)S(1)}, bf16[1,4096,256]{2,1,0:T(8,128)(2,1)}, u32[]{:S(2)}) %copy-start.5) | copy-done | bytes 2097176
  51.9 0.5 fusion.22
  52.6 0.1 fusion.58
  52.8 0.1 fusion.60
  52.9 0.2 fusion.79
  53.1 0.2 fusion.29
  53.3 0.2 multiply_reduce_fusion.1
  53.5 0.2 multiply_reduce_fusion
  53.6 0.3 fusion.35
  53.9 0.2 convolution_convert_fusion.4
  54.1 0.2 convolution_convert_fusion.8
  54.3 0.3 fusion.36
  54.6 0.2 fusion.89
  55.1 0.2 fusion.39
  55.3 0.1 pad_add_fusion.2
  55.4 0.8 convolution_convert_fusion
  56.2 1.0 %fusion.12 = (f32[128]{0:T(128)S(1)}, f32[128,4096]{1,0:T(8,128)S(1)}) fusion(bf16[128,4096]{1,0:T(8,128)(2,1)S(1)} %collective-permute-done, f32[4096]{0:T(1024)S(1)} %bitcast.65, bf16[128,4096]{1,0:T(8,128)(2,1)S(1)} %convolution_convert_fusion, bf16[1,4096,256]{2,1,0:T(8,128)(2,1)S(1)} %copy-done, f32[128,128]{1,0:T(8,128)S(1)} %get-tuple-element.22, ...), kind=kOutput, calls=%fused_computation.22 | convolution fusion | flops 272170880 | bytes 6406656 | tf_op jit(solution)/shard_map/transpose(jvp())/dot_general | solution.py:42
  57.3 1.6 %fusion.42 = bf16[1,128,4096]{2,1,0:T(8,128)(2,1)} fusion(bf16[128,4096]{1,0:T(8,128)(2,1)S(1)} %collective-permute-done, f32[128,4096]{1,0:T(8,128)S(1)} %get-tuple-element.55, bf16[1,128,4096]{2,1,0:T(8,128)(2,1)S(1)} %copy-done.2, f32[128]{0:T(128)S(1)} %multiply_multiply_fusion.2, f32[128]{0:T(128)S(1)} %fusion.92), kind=kLoop, calls=%fused_computation.64 | loop fusion | flops 4194304 | bytes 5243904 | tf_op jit(solution)/shard_map/broadcast_in_dim | solution.py:86
  58.9 2.3 %collective-permute-start.3 = (bf16[1,128,4096]{2,1,0:T(8,128)(2,1)}, bf16[1,128,4096]{2,1,0:T(8,128)(2,1)S(1)}, u32[]{:S(2)}, u32[]{:S(2)}) collective-permute-start(bf16[1,128,4096]{2,1,0:T(8,128)(2,1)} %fusion.42), channel_id=1, source_target_pairs={{1,0},{2,1},{3,2},{4,3},{5,4},{6,5},{7,6},{8,7},{9,8},{10,9},{11,1... | collective-permute-start | bytes 3145736 | tf_op jit(solution)/shard_map/ppermute | solution.py:12
  61.2 1.7 %collective-permute-start.1 = (bf16[1,128,4096]{2,1,0:T(8,128)(2,1)}, bf16[1,128,4096]{2,1,0:T(8,128)(2,1)}, u32[]{:S(2)}, u32[]{:S(2)}) collective-permute-start(bf16[1,128,4096]{2,1,0:T(8,128)(2,1)} %bitcast.9), channel_id=1, source_target_pairs={{7,8},{23,24}} | collective-permute-start | bytes 3145736 | tf_op jit(solution)/shard_map/ppermute | solution.py:82
  62.9 27.3 %collective-permute-done.3 = bf16[1,128,4096]{2,1,0:T(8,128)(2,1)S(1)} collective-permute-done((bf16[1,128,4096]{2,1,0:T(8,128)(2,1)}, bf16[1,128,4096]{2,1,0:T(8,128)(2,1)S(1)}, u32[]{:S(2)}, u32[]{:S(2)}) %collective-permute-start.3) | collective-permute-done | bytes 1048608 | tf_op jit(solution)/shard_map/ppermute | solution.py:12
  90.1 2.3 %broadcast_select_fusion = bf16[1,128,4096]{2,1,0:T(8,128)(2,1)} fusion(bf16[1,128,4096]{2,1,0:T(8,128)(2,1)} %collective-permute-done.1, bf16[1,128,4096]{2,1,0:T(8,128)(2,1)} %collective-permute-done.2, pred[]{:T(512)S(6)} %eq.33), kind=kLoop, calls=%fused_computation.67 | loop fusion | flops 524288 | bytes 3145729 | tf_op jit(solution)/shard_map/jit(_where)/select_n | solution.py:83
  92.5 1.0 %copy.27 = bf16[1,128,4096]{2,1,0:T(8,128)(2,1)} copy(bf16[1,128,4096]{2,1,0:T(8,128)(2,1)S(1)} %collective-permute-done.3) | data formatting | bytes 2097152
  (32 shorter events, 0.7 us)
Async XLA Ops:
  0.6 5.0 %copy-start = (bf16[1,4096,256]{2,1,0:T(8,128)(2,1)S(1)}, bf16[1,4096,256]{2,1,0:T(8,128)(2,1)}, u32[]{:S(2)}) copy-start(bf16[1,4096,256]{2,1,0:T(8,128)(2,1)} %param.13) | copy-start | bytes 6291460
  0.6 49.4 %collective-permute-start = (bf16[128,4096]{1,0:T(8,128)(2,1)}, bf16[128,4096]{1,0:T(8,128)(2,1)S(1)}, u32[]{:S(2)}, u32[]{:S(2)}) collective-permute-start(bf16[128,4096]{1,0:T(8,128)(2,1)} %bitcast.66), channel_id=1, source_target_pairs={{0,15},{1,14},{2,13},{3,12},{4,11},{5,10},{6,9},{7,8},{8,7},{9,6},... | collective-permute-start | bytes 3145736 | tf_op jit(solution)/shard_map/ppermute | solution.py:69
  5.6 1.9 %copy-start.3 = (bf16[1,128,4096]{2,1,0:T(8,128)(2,1)S(1)}, bf16[1,128,4096]{2,1,0:T(8,128)(2,1)}, u32[]{:S(2)}) copy-start(bf16[1,128,4096]{2,1,0:T(8,128)(2,1)} %param.8) | copy-start | bytes 3145732
  5.6 2.2 %copy-start.4 = (bf16[1,4096,256]{2,1,0:T(8,128)(2,1)S(1)}, bf16[1,4096,256]{2,1,0:T(8,128)(2,1)}, u32[]{:S(2)}) copy-start(bf16[1,4096,256]{2,1,0:T(8,128)(2,1)} %param.12) | copy-start | bytes 6291460
  5.6 2.2 %copy-start.6 = (f32[1,4096]{1,0:T(1,128)S(1)}, f32[1,4096]{1,0:T(1,128)}, u32[]{:S(2)}) copy-start(f32[1,4096]{1,0:T(1,128)} %param.11) | copy-start | bytes 49156
  9.7 2.5 %copy-start.1 = (bf16[1,256,4096]{2,1,0:T(8,128)(2,1)S(1)}, bf16[1,256,4096]{2,1,0:T(8,128)(2,1)}, u32[]{:S(2)}) copy-start(bf16[1,256,4096]{2,1,0:T(8,128)(2,1)} %param.14) | copy-start | bytes 6291460
  12.2 5.0 %copy-start.2 = (bf16[1,128,4096]{2,1,0:T(8,128)(2,1)S(1)}, bf16[1,128,4096]{2,1,0:T(8,128)(2,1)}, u32[]{:S(2)}) copy-start(bf16[1,128,4096]{2,1,0:T(8,128)(2,1)} %param.10) | copy-start | bytes 3145732
  15.0 35.3 %copy-start.7 = (f32[1,4096]{1,0:T(1,128)S(1)}, f32[1,4096]{1,0:T(1,128)}, u32[]{:S(2)}) copy-start(f32[1,4096]{1,0:T(1,128)} %param.11) | copy-start | bytes 49156
  15.0 75.1 %collective-permute-start.2 = (bf16[1,128,4096]{2,1,0:T(8,128)(2,1)}, bf16[1,128,4096]{2,1,0:T(8,128)(2,1)}, u32[]{:S(2)}, u32[]{:S(2)}) collective-permute-start(bf16[1,128,4096]{2,1,0:T(8,128)(2,1)} %bitcast.10), channel_id=1, source_target_pairs={{0,1},{1,2},{2,3},{3,4},{4,5},{5,6},{6,7},{8,9},{9,10},{10,11},{11... | collective-permute-start | bytes 3145736 | tf_op jit(solution)/shard_map/ppermute | solution.py:78
  50.3 1.6 %copy-start.5 = (bf16[1,4096,256]{2,1,0:T(8,128)(2,1)S(1)}, bf16[1,4096,256]{2,1,0:T(8,128)(2,1)}, u32[]{:S(2)}) copy-start(bf16[1,4096,256]{2,1,0:T(8,128)(2,1)} %param.12) | copy-start | bytes 6291460
  58.9 31.2 %collective-permute-start.3 = (bf16[1,128,4096]{2,1,0:T(8,128)(2,1)}, bf16[1,128,4096]{2,1,0:T(8,128)(2,1)S(1)}, u32[]{:S(2)}, u32[]{:S(2)}) collective-permute-start(bf16[1,128,4096]{2,1,0:T(8,128)(2,1)} %fusion.42), channel_id=1, source_target_pairs={{1,0},{2,1},{3,2},{4,3},{5,4},{6,5},{7,6},{8,7},{9,8},{10,9},{11,1... | collective-permute-start | bytes 3145736 | tf_op jit(solution)/shard_map/ppermute | solution.py:12
  61.2 29.0 %collective-permute-start.1 = (bf16[1,128,4096]{2,1,0:T(8,128)(2,1)}, bf16[1,128,4096]{2,1,0:T(8,128)(2,1)}, u32[]{:S(2)}, u32[]{:S(2)}) collective-permute-start(bf16[1,128,4096]{2,1,0:T(8,128)(2,1)} %bitcast.9), channel_id=1, source_target_pairs={{7,8},{23,24}} | collective-permute-start | bytes 3145736 | tf_op jit(solution)/shard_map/ppermute | solution.py:82

commit v7 on v1

--- a/solution.py
+++ b/solution.py
@@ -38,23 +38,28 @@
     values32 = acts.astype(jnp.float32)
     scale = lax.rsqrt(jnp.mean(values32 * values32, axis=-1, keepdims=True) + 1e-05)
     normed = (values32 * scale * gain).astype(jnp.bfloat16)
-    query = jnp.dot(normed, w_query, preferred_element_type=jnp.float32).reshape(
-        rows, heads, head_dim
-    )
+    query = jnp.dot(normed, w_query, preferred_element_type=jnp.float32)
     keyval = jnp.dot(normed, w_kv, preferred_element_type=jnp.float32)
     cosine, sine_part = rotary_tables(segment, head_dim)
-    query = rotary(query, cosine[:, None, :], sine_part[:, None, :]).astype(jnp.bfloat16)
     keys = rotary(keyval[:, :head_dim], cosine, sine_part).astype(jnp.bfloat16)
     values = keyval[:, head_dim:].astype(jnp.bfloat16)
-    scores = jnp.einsum("qhd,kd->hqk", query, keys, preferred_element_type=jnp.float32) / math.sqrt(
-        head_dim
-    )
     index = jnp.arange(rows, dtype=jnp.int32)
     allowed = (segment[:, None] == segment[None, :]) & (index[None, :] <= index[:, None])
-    expd = jnp.where(allowed[None], jnp.exp(scores), jnp.zeros_like(scores))
+    stacked = jnp.concatenate(
+        [query[:, head * head_dim : (head + 1) * head_dim] for head in range(heads)], 0
+    )
+    stacked = rotary(
+        stacked, jnp.tile(cosine, (heads, 1)), jnp.tile(sine_part, (heads, 1))
+    ).astype(jnp.bfloat16)
+    scores = lax.dot_general(
+        stacked, keys, (((1,), (1,)), ((), ())), preferred_element_type=jnp.float32
+    ) / math.sqrt(head_dim)
+    expd = jnp.where(jnp.tile(allowed, (heads, 1)), jnp.exp(scores), jnp.zeros_like(scores))
     probs = (expd / jnp.sum(expd, axis=-1, keepdims=True)).astype(jnp.bfloat16)
-    mixed = jnp.einsum("hqk,kd->qhd", probs, values, preferred_element_type=jnp.float32)
-    mixed = mixed.astype(jnp.bfloat16).reshape(rows, heads * head_dim)
+    mixed = jnp.dot(probs, values, preferred_element_type=jnp.float32).astype(jnp.bfloat16)
+    mixed = jnp.concatenate(
+        [mixed[head * rows : (head + 1) * rows] for head in range(heads)], -1
+    )
     return (values32 + jnp.dot(mixed, w_out, preferred_element_type=jnp.float32)).astype(
         jnp.bfloat16
     )

time: 90.8 us -> 86 us (0.947)
  waiting for transfers between devices: 43.4 us -> 58.3 us
  matrix products: 18.3 us -> 8.56 us
  local copies, waits for them, and re-layouts: 12.6 us -> 4.76 us
  other arithmetic: 7.75 us -> 5.93 us
    ppermute x1, waiting for transfers between devices: 29.6 us -> 44.6 us  [shards(): fetched = lax.ppermute(stash[0], 'section', mirror)]
    dot_general x2, matrix products: 6.06 us -> 1.31 us  [section_layer(): jnp.dot(mixed, w_out, preferred_element_type=jnp.float32)]
    dot_general x1 -> x0, local copies, waits for them, and re-layouts: 4.13 us -> none  [section_layer(): jnp.dot(normed, w_query, preferred_element_type=jnp.float32)]
    dot_general x10, matrix products: 8.98 us -> 5.24 us  [the longest x3 3.83 us: section_layer(): query = jnp.dot(normed, w_query, preferred_element_type=jnp.float32)]
    concatenate x4 -> x0, local copies, waits for them, and re-layouts: 2.47 us -> none  [the longest x2 1.66 us: rotary_tables(): sine_part = jnp.concatenate([jnp.sin(angles), jnp.sin(angles)], -1)]
    dot_general x3, matrix products: 3.23 us -> 2.01 us  [section_layer(): keyval = jnp.dot(normed, w_kv, preferred_element_type=jnp.float32)]
    unnamed x42 -> x14, local copies, waits for them, and re-layouts: 4.13 us -> 3.49 us
  transfers between devices with their start and end apart: 3 -> 3, of which waited for: 2 -> 2; matrix products, arithmetic and copies ran while one was open for 38% -> 18% of each run, Pallas kernels for 0% -> 0%
where the time goes in v7:
time: 86 us; the launch traced here: 85.7 us
  waiting for transfers between devices  58.3 us (68%)
  matrix products  8.56 us (10%)
  starting transfers between devices  7.16 us (8%)
  other arithmetic  5.93 us (7%)
  local copies, waits for them, and re-layouts  4.76 us (6%)
  between operations  1.03 us (1%)
    ppermute x1, waiting for transfers between devices, shards(): fetched = lax.ppermute(stash[0], 'section', mirror)  44.6 us
    ppermute x2, waiting for transfers between devices, shifted(): lax.ppermute(value, axis, [(source, source + steps) for source in range(l...  13.7 us
    ppermute x2, starting transfers between devices, shifted(): lax.ppermute(value, axis, [(source, source + steps) for source in range(l...  4.28 us
    dot_general x3, matrix products, section_layer(): query = jnp.dot(normed, w_query, preferred_element_type=jnp.float32)  3.83 us
    unnamed x14, local copies, waits for them, and re-layouts  3.49 us
    ppermute x1, starting transfers between devices, shards(): fetched = lax.ppermute(stash[0], 'section', mirror)  2.88 us
    dot_general x3, matrix products, section_layer(): keyval = jnp.dot(normed, w_kv, preferred_element_type=jnp.float32)  2.01 us
    reduce_sum x2, other arithmetic, section_layer(): jnp.mean(values32 * values32, axis=-1, keepdims=True) + 1e-05  1.81 us
  transfers between devices with their start and end apart: 3, of which 2 were waited for; matrix products, arithmetic and copies ran while one was open for 18% of the time, Pallas kernels for 0%

profile of v7, /device:TPU:9, one launch (start us, length us, event | category | flops | bytes accessed | tf_op | source)
XLA Modules:
  0.0 85.7 jit_solution(447602750208160520)
XLA Ops:
  0.6 2.9 %collective-permute-start.1 = (bf16[128,4096]{1,0:T(8,128)(2,1)}, bf16[128,4096]{1,0:T(8,128)(2,1)S(1)}, u32[]{:S(2)}, u32[]{:S(2)}) collective-permute-start(bf16[128,4096]{1,0:T(8,128)(2,1)} %bitcast.87), channel_id=1, source_target_pairs={{0,15},{1,14},{2,13},{3,12},{4,11},{5,10},{6,9},{7,8},{8,7},{9,6},... | collective-permute-start | bytes 3145736 | tf_op jit(solution)/shard_map/ppermute | solution.py:71
  3.5 0.9 %compare_bitcast_fusion = (pred[127,1]{0,1:T(4,128)(4,1)S(1)}, pred[127,1]{0,1:T(4,128)(4,1)S(1)}) fusion(s32[1,2,128]{2,1,0:T(2,128)} %param.15), kind=kLoop, calls=%fused_computation.131 | loop fusion | flops 254 | bytes 2286 | tf_op jit(solution)/shard_map/jvp()/concatenate | solution.py:17
  4.4 0.8 slice_bitcast_fusion
  5.3 0.1 copy.16
  5.4 0.2 reduce-window.17
  5.6 0.1 reduce.1
  5.7 0.1 copy.14
  5.8 0.2 reduce-window.16
  6.0 0.1 reduce
  6.1 1.5 %fusion.6 = f32[128]{0:T(128)S(1)} fusion(bf16[1,128,4096]{2,1,0:T(8,128)(2,1)} %param.8), kind=kLoop, calls=%fused_computation.16 | loop fusion | flops 1572736 | bytes 1049088 | tf_op jit(solution)/shard_map/reduce_sum | solution.py:39
  7.6 2.5 %fusion.25 = f32[128,256]{1,0:T(8,128)S(1)} fusion(bf16[1,4096,256]{2,1,0:T(8,128)(2,1)} %param.12, bf16[1,128,4096]{2,1,0:T(8,128)(2,1)} %param.8, f32[4096]{0:T(1024)} %bitcast.82, f32[128]{0:T(128)S(1)} %add_rsqrt_fusion), kind=kOutput, calls=%fused_computation.35 | convolution fusion | flops 270532608 | bytes 3293696 | tf_op jit(solution)/shard_map/dot_general | solution.py:41
  10.2 0.5 multiply_cosine_fusion
  10.7 0.1 pad_maximum_fusion.2
  10.9 0.5 fusion.20
  11.5 0.1 fusion.73
  11.7 0.1 copy.15
  11.8 0.1 fusion.47
  11.9 0.1 fusion.51
  12.0 0.3 fusion.95
  12.3 0.2 convolution_convert_fusion.3
  12.5 0.5 copy-done.1
  13.0 0.5 fusion.4
  13.5 1.9 %collective-permute-start = (bf16[1,128,4096]{2,1,0:T(8,128)(2,1)S(1)}, bf16[1,128,4096]{2,1,0:T(8,128)(2,1)S(1)}, u32[]{:S(2)}, u32[]{:S(2)}) collective-permute-start(bf16[1,128,4096]{2,1,0:T(8,128)(2,1)S(1)} %fusion.4), channel_id=1, source_target_pairs={{0,1},{1,2},{2,3},{3,4},{4,5},{5,6},{6,7},{7,8},{8,9},{9,10},{10,1... | collective-permute-start | bytes 3145736 | tf_op jit(solution)/shard_map/ppermute | solution.py:12
  15.5 0.1 copy.17
  15.6 0.8 fusion.30
  16.4 44.6 %collective-permute-done.1 = bf16[128,4096]{1,0:T(8,128)(2,1)S(1)} collective-permute-done((bf16[128,4096]{1,0:T(8,128)(2,1)}, bf16[128,4096]{1,0:T(8,128)(2,1)S(1)}, u32[]{:S(2)}, u32[]{:S(2)}) %collective-permute-start.1) | collective-permute-done | bytes 1048608 | tf_op jit(solution)/shard_map/ppermute | solution.py:71
  61.0 0.3 fusion.10
  61.3 0.5 fusion.18
  61.9 1.0 %copy-done.4 = bf16[1,4096,256]{2,1,0:T(8,128)(2,1)S(1)} copy-done((bf16[1,4096,256]{2,1,0:T(8,128)(2,1)S(1)}, bf16[1,4096,256]{2,1,0:T(8,128)(2,1)}, u32[]{:S(2)}) %copy-start.4) | copy-done | bytes 2097176
  62.9 0.5 fusion.23
  63.5 0.1 fusion.44
  63.6 0.1 pad_maximum_fusion.4
  63.7 0.1 fusion.53
  63.8 0.2 fusion.72
  64.0 0.2 convolution_convert_fusion.6
  64.2 0.2 multiply_reduce_fusion
  64.4 0.2 fusion.87
  64.5 0.2 bitcast_multiply_fusion
  64.8 0.1 fusion.89
  65.0 0.1 fusion.55
  65.1 0.8 convolution_convert_fusion
  65.9 0.1 pad_add_fusion
  66.0 1.0 %fusion.13 = (f32[128]{0:T(128)S(1)}, f32[128,4096]{1,0:T(8,128)S(1)}) fusion(bf16[128,4096]{1,0:T(8,128)(2,1)S(1)} %collective-permute-done.1, f32[4096]{0:T(1024)S(1)} %bitcast.86, bf16[128,4096]{1,0:T(8,128)(2,1)S(1)} %convolution_convert_fusion, bf16[1,4096,256]{2,1,0:T(8,128)(2,1)S(1)} %copy-done, f32[128,128]{1,0:T(8,128)S(1)} %pad_add_fusion, ...), kind=kOutput, calls=%fused_computation.23 | convolution fusion | flops 272170880 | bytes 6406656 | tf_op jit(solution)/shard_map/transpose(jvp())/dot_general | solution.py:42
  67.0 0.7 fusion.36
  67.7 2.4 %collective-permute-start.2 = (bf16[1,128,4096]{2,1,0:T(8,128)(2,1)S(1)}, bf16[1,128,4096]{2,1,0:T(8,128)(2,1)S(1)}, u32[]{:S(2)}, u32[]{:S(2)}) collective-permute-start(bf16[1,128,4096]{2,1,0:T(8,128)(2,1)S(1)} %fusion.36), channel_id=1, source_target_pairs={{1,0},{2,1},{3,2},{4,3},{5,4},{6,5},{7,6},{8,7},{9,8},{10,9},{11,1... | collective-permute-start | bytes 3145736 | tf_op jit(solution)/shard_map/ppermute | solution.py:12
  70.1 13.7 %collective-permute-done.2 = bf16[1,128,4096]{2,1,0:T(8,128)(2,1)S(1)} collective-permute-done((bf16[1,128,4096]{2,1,0:T(8,128)(2,1)S(1)}, bf16[1,128,4096]{2,1,0:T(8,128)(2,1)S(1)}, u32[]{:S(2)}, u32[]{:S(2)}) %collective-permute-start.2) | collective-permute-done | bytes 1048608 | tf_op jit(solution)/shard_map/ppermute | solution.py:12
  83.8 1.0 %copy.31 = bf16[1,128,4096]{2,1,0:T(8,128)(2,1)} copy(bf16[1,128,4096]{2,1,0:T(8,128)(2,1)S(1)} %collective-permute-done) | data formatting | bytes 2097152
  84.8 1.0 %copy.32 = bf16[1,128,4096]{2,1,0:T(8,128)(2,1)} copy(bf16[1,128,4096]{2,1,0:T(8,128)(2,1)S(1)} %collective-permute-done.2) | data formatting | bytes 2097152
  (31 shorter events, 0.6 us)
Async XLA Ops:
  0.6 10.3 %copy-start = (bf16[1,4096,256]{2,1,0:T(8,128)(2,1)S(1)}, bf16[1,4096,256]{2,1,0:T(8,128)(2,1)}, u32[]{:S(2)}) copy-start(bf16[1,4096,256]{2,1,0:T(8,128)(2,1)} %param.13) | copy-start | bytes 6291460
  0.6 60.4 %collective-permute-start.1 = (bf16[128,4096]{1,0:T(8,128)(2,1)}, bf16[128,4096]{1,0:T(8,128)(2,1)S(1)}, u32[]{:S(2)}, u32[]{:S(2)}) collective-permute-start(bf16[128,4096]{1,0:T(8,128)(2,1)} %bitcast.87), channel_id=1, source_target_pairs={{0,15},{1,14},{2,13},{3,12},{4,11},{5,10},{6,9},{7,8},{8,7},{9,6},... | collective-permute-start | bytes 3145736 | tf_op jit(solution)/shard_map/ppermute | solution.py:71
  7.6 3.3 %copy-start.3 = (bf16[1,128,4096]{2,1,0:T(8,128)(2,1)S(1)}, bf16[1,128,4096]{2,1,0:T(8,128)(2,1)}, u32[]{:S(2)}) copy-start(bf16[1,128,4096]{2,1,0:T(8,128)(2,1)} %param.8) | copy-start | bytes 3145732
  7.6 3.3 %copy-start.5 = (f32[1,4096]{1,0:T(1,128)S(1)}, f32[1,4096]{1,0:T(1,128)}, u32[]{:S(2)}) copy-start(f32[1,4096]{1,0:T(1,128)} %param.11) | copy-start | bytes 49156
  11.4 1.6 %copy-start.1 = (bf16[1,256,4096]{2,1,0:T(8,128)(2,1)S(1)}, bf16[1,256,4096]{2,1,0:T(8,128)(2,1)}, u32[]{:S(2)}) copy-start(bf16[1,256,4096]{2,1,0:T(8,128)(2,1)} %param.14) | copy-start | bytes 6291460
  13.0 2.5 %copy-start.2 = (bf16[1,128,4096]{2,1,0:T(8,128)(2,1)S(1)}, bf16[1,128,4096]{2,1,0:T(8,128)(2,1)}, u32[]{:S(2)}) copy-start(bf16[1,128,4096]{2,1,0:T(8,128)(2,1)} %param.10) | copy-start | bytes 3145732
  13.5 56.5 %collective-permute-start = (bf16[1,128,4096]{2,1,0:T(8,128)(2,1)S(1)}, bf16[1,128,4096]{2,1,0:T(8,128)(2,1)S(1)}, u32[]{:S(2)}, u32[]{:S(2)}) collective-permute-start(bf16[1,128,4096]{2,1,0:T(8,128)(2,1)S(1)} %fusion.4), channel_id=1, source_target_pairs={{0,1},{1,2},{2,3},{3,4},{4,5},{5,6},{6,7},{7,8},{8,9},{9,10},{10,1... | collective-permute-start | bytes 3145736 | tf_op jit(solution)/shard_map/ppermute | solution.py:12
  61.3 1.6 %copy-start.4 = (bf16[1,4096,256]{2,1,0:T(8,128)(2,1)S(1)}, bf16[1,4096,256]{2,1,0:T(8,128)(2,1)}, u32[]{:S(2)}) copy-start(bf16[1,4096,256]{2,1,0:T(8,128)(2,1)} %param.12) | copy-start | bytes 6291460
  67.7 16.1 %collective-permute-start.2 = (bf16[1,128,4096]{2,1,0:T(8,128)(2,1)S(1)}, bf16[1,128,4096]{2,1,0:T(8,128)(2,1)S(1)}, u32[]{:S(2)}, u32[]{:S(2)}) collective-permute-start(bf16[1,128,4096]{2,1,0:T(8,128)(2,1)S(1)} %fusion.36), channel_id=1, source_target_pairs={{1,0},{2,1},{3,2},{4,3},{5,4},{6,5},{7,6},{8,7},{9,8},{10,9},{11,1... | collective-permute-start | bytes 3145736 | tf_op jit(solution)/shard_map/ppermute | solution.py:12

commit v8 on v7

--- a/solution.py
+++ b/solution.py
@@ -65,6 +65,21 @@
     )
 
 
+def relay_forward(value, pieces):
+    if pieces < 16:
+        return shifted(value, "section", 1)
+    first = [(source, source + 1) for source in range(pieces - 1) if source not in (5, 11, 14)]
+    first += [(5, 0), (11, 15)]
+    second = [(0, 6), (15, 12), (14, 15)]
+    where = lax.axis_index("section")
+    landed = lax.ppermute(value, "section", first)
+    onward = jnp.where((where == 0) | (where == 15), landed, value)
+    relayed = lax.ppermute(onward, "section", second)
+    late = (where == 6) | (where == 12) | (where == 15)
+    landed = jnp.where(where == 0, jnp.zeros_like(landed), landed)
+    return jnp.where(late, relayed, landed)
+
+
 def shards(section_input, stash, cotangent, norm_gain, w_query, w_kv, w_out, doc_ids):
     pieces = lax.axis_size("section")
     mirror = [(source, pieces - 1 - source) for source in range(pieces)]
@@ -78,7 +93,7 @@
 
     unused, pullback = jax.vjp(replay, fetched)
     gradient = pullback(cotangent[0])[0]
-    forwarded = shifted(outward[None], "section", 1)
+    forwarded = relay_forward(outward[None], pieces)
     returned = shifted(gradient[None], "section", -1)
     return (forwarded, returned)
 

time: 86 us -> 94.9 us (1.10)
  the two profiles are of different devices: /device:TPU:9 before, /device:TPU:14 now
where the time goes in v8:
time: 94.9 us; the launch traced here: 94.5 us
  waiting for transfers between devices  47.2 us (50%)
  starting transfers between devices  19 us (20%)
  other arithmetic  11.8 us (12%)
  matrix products  11.4 us (12%)
  local copies, waits for them, and re-layouts  3.98 us (4%)
  between operations  1.04 us (1%)
    ppermute x1, waiting for transfers between devices, shards(): fetched = lax.ppermute(stash[0], 'section', mirror)  30.6 us
    ppermute x1, starting transfers between devices, shifted(): lax.ppermute(value, axis, [(source, source + steps) for source in range(l...  13.1 us
    ppermute x1, waiting for transfers between devices, shifted(): lax.ppermute(value, axis, [(source, source + steps) for source in range(l...  8.98 us
    ppermute x1, waiting for transfers between devices, relay_forward(): relayed = lax.ppermute(onward, 'section', second)  7.62 us
    dot_general x2, matrix products, section_layer(): jnp.dot(mixed, w_out, preferred_element_type=jnp.float32)  4.2 us
    dot_general x3, matrix products, section_layer(): query = jnp.dot(normed, w_query, preferred_element_type=jnp.float32)  3.83 us
    ppermute x1, starting transfers between devices, relay_forward(): landed = lax.ppermute(value, 'section', first)  3.55 us
    unnamed x13, local copies, waits for them, and re-layouts  2.72 us
  transfers between devices with their start and end apart: 4, of which 3 were waited for; matrix products, arithmetic and copies ran while one was open for 23% of the time, Pallas kernels for 0%

profile of v8, /device:TPU:14, one launch (start us, length us, event | category | flops | bytes accessed | tf_op | source)
XLA Modules:
  0.0 94.5 jit_solution(15590161619892240289)
XLA Ops:
  0.6 1.0 %collective-permute-start.2 = (bf16[128,4096]{1,0:T(8,128)(2,1)}, bf16[128,4096]{1,0:T(8,128)(2,1)S(1)}, u32[]{:S(2)}, u32[]{:S(2)}) collective-permute-start(bf16[128,4096]{1,0:T(8,128)(2,1)} %bitcast.87), channel_id=1, source_target_pairs={{0,15},{1,14},{2,13},{3,12},{4,11},{5,10},{6,9},{7,8},{8,7},{9,6},... | collective-permute-start | bytes 3145736 | tf_op jit(solution)/shard_map/ppermute | solution.py:86
  1.7 0.9 compare_bitcast_fusion
  2.6 0.8 slice_bitcast_fusion
  3.4 0.1 copy.16
  3.5 0.2 reduce-window.17
  3.7 0.1 reduce.1
  3.8 0.1 copy.14
  3.9 0.2 reduce-window.16
  4.1 0.1 reduce
  4.2 1.5 %fusion.6 = f32[128]{0:T(128)S(1)} fusion(bf16[1,128,4096]{2,1,0:T(8,128)(2,1)} %param.8), kind=kLoop, calls=%fused_computation.16 | loop fusion | flops 1572736 | bytes 1049088 | tf_op jit(solution)/shard_map/reduce_sum | solution.py:39
  5.8 2.5 %fusion.25 = f32[128,256]{1,0:T(8,128)S(1)} fusion(bf16[1,4096,256]{2,1,0:T(8,128)(2,1)} %param.12, bf16[1,128,4096]{2,1,0:T(8,128)(2,1)} %param.8, f32[4096]{0:T(1024)} %bitcast.82, f32[128]{0:T(128)S(1)} %add_rsqrt_fusion), kind=kOutput, calls=%fused_computation.35 | convolution fusion | flops 270532608 | bytes 3293696 | tf_op jit(solution)/shard_map/dot_general | solution.py:41
  8.3 0.5 multiply_cosine_fusion
  9.1 0.5 fusion.20
  9.7 0.1 fusion.73
  9.8 0.1 copy.15
  10.0 0.1 fusion.51
  10.1 0.3 fusion.95
  10.4 0.2 convolution_convert_fusion.3
  10.6 0.5 copy-done.1
  11.2 1.4 %fusion.4 = bf16[1,128,4096]{2,1,0:T(8,128)(2,1)} fusion(bf16[1,128,4096]{2,1,0:T(8,128)(2,1)S(1)} %copy-done.3, bf16[1,256,4096]{2,1,0:T(8,128)(2,1)S(1)} %copy-done.1, bf16[128,128]{0,1:T(8,128)(2,1)S(1)} %get-tuple-element.26, bf16[128,128]{0,1:T(8,128)(2,1)S(1)} %get-tuple-element.25), kind=kOutput, calls=%fused_computation.7 | convolution fusion | flops 270139392 | bytes 4259840 | tf_op jit(solution)/shard_map/dot_general | solution.py:63
  12.6 3.5 %collective-permute-start = (bf16[1,128,4096]{2,1,0:T(8,128)(2,1)}, bf16[1,128,4096]{2,1,0:T(8,128)(2,1)}, u32[]{:S(2)}, u32[]{:S(2)}) collective-permute-start(bf16[1,128,4096]{2,1,0:T(8,128)(2,1)} %fusion.4), channel_id=1, source_target_pairs={{0,1},{1,2},{2,3},{3,4},{4,5},{6,7},{7,8},{8,9},{9,10},{10,11},{12... | collective-permute-start | bytes 3145736 | tf_op jit(solution)/shard_map/ppermute | solution.py:75
  16.2 0.1 copy.17
  16.3 2.8 %fusion.30 = bf16[128,256]{1,0:T(8,128)(2,1)S(1)} fusion(bf16[1,256,4096]{2,1,0:T(8,128)(2,1)} %param.14, bf16[1,128,4096]{2,1,0:T(8,128)(2,1)} %param.10), kind=kOutput, calls=%fused_computation.42 | convolution fusion | flops 268468224 | bytes 3211264 | tf_op jit(solution)/shard_map/transpose(jvp())/dot_general | solution.py:63
  19.1 30.6 %collective-permute-done.2 = bf16[128,4096]{1,0:T(8,128)(2,1)S(1)} collective-permute-done((bf16[128,4096]{1,0:T(8,128)(2,1)}, bf16[128,4096]{1,0:T(8,128)(2,1)S(1)}, u32[]{:S(2)}, u32[]{:S(2)}) %collective-permute-start.2) | collective-permute-done | bytes 1048608 | tf_op jit(solution)/shard_map/ppermute | solution.py:86
  49.7 0.3 fusion.10
  50.0 0.5 fusion.18
  50.6 1.0 %copy-done.4 = bf16[1,4096,256]{2,1,0:T(8,128)(2,1)S(1)} copy-done((bf16[1,4096,256]{2,1,0:T(8,128)(2,1)S(1)}, bf16[1,4096,256]{2,1,0:T(8,128)(2,1)}, u32[]{:S(2)}) %copy-start.4) | copy-done | bytes 2097176
  51.6 0.5 fusion.23
  52.3 0.1 pad_maximum_fusion.4
  52.4 0.1 fusion.53
  52.5 0.2 fusion.72
  52.7 0.2 convolution_convert_fusion.6
  52.9 0.2 multiply_reduce_fusion
  53.1 0.2 fusion.87
  53.3 0.2 bitcast_multiply_fusion
  53.6 0.1 fusion.89
  53.7 0.1 fusion.55
  53.8 0.8 convolution_convert_fusion
  54.7 1.0 %fusion.13 = (f32[128]{0:T(128)S(1)}, f32[128,4096]{1,0:T(8,128)S(1)}) fusion(bf16[128,4096]{1,0:T(8,128)(2,1)S(1)} %collective-permute-done.2, f32[4096]{0:T(1024)S(1)} %bitcast.86, bf16[128,4096]{1,0:T(8,128)(2,1)S(1)} %convolution_convert_fusion, bf16[1,4096,256]{2,1,0:T(8,128)(2,1)S(1)} %copy-done, f32[128,128]{1,0:T(8,128)S(1)} %pad_add_fusion, ...), kind=kOutput, calls=%fused_computation.23 | convolution fusion | flops 272170880 | bytes 6406656 | tf_op jit(solution)/shard_map/transpose(jvp())/dot_general | solution.py:42
  55.8 0.2 copy-done.2
  56.0 1.6 %fusion.36 = bf16[1,128,4096]{2,1,0:T(8,128)(2,1)} fusion(bf16[128,4096]{1,0:T(8,128)(2,1)S(1)} %collective-permute-done.2, f32[128,4096]{1,0:T(8,128)S(1)} %get-tuple-element.48, bf16[1,128,4096]{2,1,0:T(8,128)(2,1)S(1)} %copy-done.2, f32[128]{0:T(128)S(1)} %multiply_multiply_fusion.1, f32[128]{0:T(128)S(1)} %fusion.78), kind=kLoop, calls=%fused_computation.51 | loop fusion | flops 4194304 | bytes 5243904 | tf_op jit(solution)/shard_map/broadcast_in_dim | solution.py:97
  57.6 13.1 %collective-permute-start.3 = (bf16[1,128,4096]{2,1,0:T(8,128)(2,1)}, bf16[1,128,4096]{2,1,0:T(8,128)(2,1)S(1)}, u32[]{:S(2)}, u32[]{:S(2)}) collective-permute-start(bf16[1,128,4096]{2,1,0:T(8,128)(2,1)} %fusion.36), channel_id=1, source_target_pairs={{1,0},{2,1},{3,2},{4,3},{5,4},{6,5},{7,6},{8,7},{9,8},{10,9},{11,1... | collective-permute-start | bytes 3145736 | tf_op jit(solution)/shard_map/ppermute | solution.py:12
  70.7 2.3 %broadcast_select_fusion = bf16[1,128,4096]{2,1,0:T(8,128)(2,1)} fusion(bf16[1,128,4096]{2,1,0:T(8,128)(2,1)} %collective-permute-done, bf16[1,128,4096]{2,1,0:T(8,128)(2,1)} %fusion.4, pred[]{:T(512)S(6)} %or.11), kind=kLoop, calls=%fused_computation.55 | loop fusion | flops 524288 | bytes 3145729 | tf_op jit(solution)/shard_map/jit(_where)/select_n | solution.py:76
  73.0 1.3 %collective-permute-start.1 = (bf16[1,128,4096]{2,1,0:T(8,128)(2,1)}, bf16[1,128,4096]{2,1,0:T(8,128)(2,1)}, u32[]{:S(2)}, u32[]{:S(2)}) collective-permute-start(bf16[1,128,4096]{2,1,0:T(8,128)(2,1)} %broadcast_select_fusion), channel_id=1, source_target_pairs={{0,6},{15,12},{14,15},{16,22},{31,28},{30,31}} | collective-permute-start | bytes 3145736 | tf_op jit(solution)/shard_map/ppermute | solution.py:77
  74.3 9.0 %collective-permute-done.3 = bf16[1,128,4096]{2,1,0:T(8,128)(2,1)S(1)} collective-permute-done((bf16[1,128,4096]{2,1,0:T(8,128)(2,1)}, bf16[1,128,4096]{2,1,0:T(8,128)(2,1)S(1)}, u32[]{:S(2)}, u32[]{:S(2)}) %collective-permute-start.3) | collective-permute-done | bytes 1048608 | tf_op jit(solution)/shard_map/ppermute | solution.py:12
  83.3 7.6 %collective-permute-done.1 = bf16[1,128,4096]{2,1,0:T(8,128)(2,1)} collective-permute-done((bf16[1,128,4096]{2,1,0:T(8,128)(2,1)}, bf16[1,128,4096]{2,1,0:T(8,128)(2,1)}, u32[]{:S(2)}, u32[]{:S(2)}) %collective-permute-start.1) | collective-permute-done | bytes 1048608 | tf_op jit(solution)/shard_map/ppermute | solution.py:77
  90.9 2.6 %select_select_fusion = bf16[1,128,4096]{2,1,0:T(8,128)(2,1)} fusion(bf16[1,128,4096]{2,1,0:T(8,128)(2,1)} %collective-permute-done.1, bf16[1,128,4096]{2,1,0:T(8,128)(2,1)} %collective-permute-done, pred[]{:T(512)S(6)} %eq.55, pred[]{:T(512)S(6)} %or.10), kind=kLoop, calls=%fused_computation.54 | loop fusion | flops 1048576 | bytes 3145730 | tf_op jit(solution)/shard_map/jit(_where)/select_n | solution.py:80
  93.6 1.0 %copy.30 = bf16[1,128,4096]{2,1,0:T(8,128)(2,1)} copy(bf16[1,128,4096]{2,1,0:T(8,128)(2,1)S(1)} %collective-permute-done.3) | data formatting | bytes 2097152
  (34 shorter events, 0.9 us)
Async XLA Ops:
  0.6 8.4 %copy-start = (bf16[1,4096,256]{2,1,0:T(8,128)(2,1)S(1)}, bf16[1,4096,256]{2,1,0:T(8,128)(2,1)}, u32[]{:S(2)}) copy-start(bf16[1,4096,256]{2,1,0:T(8,128)(2,1)} %param.13) | copy-start | bytes 6291460
  0.6 49.1 %collective-permute-start.2 = (bf16[128,4096]{1,0:T(8,128)(2,1)}, bf16[128,4096]{1,0:T(8,128)(2,1)S(1)}, u32[]{:S(2)}, u32[]{:S(2)}) collective-permute-start(bf16[128,4096]{1,0:T(8,128)(2,1)} %bitcast.87), channel_id=1, source_target_pairs={{0,15},{1,14},{2,13},{3,12},{4,11},{5,10},{6,9},{7,8},{8,7},{9,6},... | collective-permute-start | bytes 3145736 | tf_op jit(solution)/shard_map/ppermute | solution.py:86
  5.8 3.3 %copy-start.3 = (bf16[1,128,4096]{2,1,0:T(8,128)(2,1)S(1)}, bf16[1,128,4096]{2,1,0:T(8,128)(2,1)}, u32[]{:S(2)}) copy-start(bf16[1,128,4096]{2,1,0:T(8,128)(2,1)} %param.8) | copy-start | bytes 3145732
  5.8 3.3 %copy-start.5 = (f32[1,4096]{1,0:T(1,128)S(1)}, f32[1,4096]{1,0:T(1,128)}, u32[]{:S(2)}) copy-start(f32[1,4096]{1,0:T(1,128)} %param.11) | copy-start | bytes 49156
  9.6 1.6 %copy-start.1 = (bf16[1,256,4096]{2,1,0:T(8,128)(2,1)S(1)}, bf16[1,256,4096]{2,1,0:T(8,128)(2,1)}, u32[]{:S(2)}) copy-start(bf16[1,256,4096]{2,1,0:T(8,128)(2,1)} %param.14) | copy-start | bytes 6291460
  12.6 58.1 %collective-permute-start = (bf16[1,128,4096]{2,1,0:T(8,128)(2,1)}, bf16[1,128,4096]{2,1,0:T(8,128)(2,1)}, u32[]{:S(2)}, u32[]{:S(2)}) collective-permute-start(bf16[1,128,4096]{2,1,0:T(8,128)(2,1)} %fusion.4), channel_id=1, source_target_pairs={{0,1},{1,2},{2,3},{3,4},{4,5},{6,7},{7,8},{8,9},{9,10},{10,11},{12... | collective-permute-start | bytes 3145736 | tf_op jit(solution)/shard_map/ppermute | solution.py:75
  50.0 1.6 %copy-start.4 = (bf16[1,4096,256]{2,1,0:T(8,128)(2,1)S(1)}, bf16[1,4096,256]{2,1,0:T(8,128)(2,1)}, u32[]{:S(2)}) copy-start(bf16[1,4096,256]{2,1,0:T(8,128)(2,1)} %param.12) | copy-start | bytes 6291460
  54.7 1.2 %copy-start.2 = (bf16[1,128,4096]{2,1,0:T(8,128)(2,1)S(1)}, bf16[1,128,4096]{2,1,0:T(8,128)(2,1)}, u32[]{:S(2)}) copy-start(bf16[1,128,4096]{2,1,0:T(8,128)(2,1)} %param.10) | copy-start | bytes 3145732
  57.6 25.7 %collective-permute-start.3 = (bf16[1,128,4096]{2,1,0:T(8,128)(2,1)}, bf16[1,128,4096]{2,1,0:T(8,128)(2,1)S(1)}, u32[]{:S(2)}, u32[]{:S(2)}) collective-permute-start(bf16[1,128,4096]{2,1,0:T(8,128)(2,1)} %fusion.36), channel_id=1, source_target_pairs={{1,0},{2,1},{3,2},{4,3},{5,4},{6,5},{7,6},{8,7},{9,8},{10,9},{11,1... | collective-permute-start | bytes 3145736 | tf_op jit(solution)/shard_map/ppermute | solution.py:12
  73.0 17.9 %collective-permute-start.1 = (bf16[1,128,4096]{2,1,0:T(8,128)(2,1)}, bf16[1,128,4096]{2,1,0:T(8,128)(2,1)}, u32[]{:S(2)}, u32[]{:S(2)}) collective-permute-start(bf16[1,128,4096]{2,1,0:T(8,128)(2,1)} %broadcast_select_fusion), channel_id=1, source_target_pairs={{0,6},{15,12},{14,15},{16,22},{31,28},{30,31}} | collective-permute-start | bytes 3145736 | tf_op jit(solution)/shard_map/ppermute | solution.py:77

commit v9 on v7

--- a/solution.py
+++ b/solution.py
@@ -79,6 +79,7 @@
     unused, pullback = jax.vjp(replay, fetched)
     gradient = pullback(cotangent[0])[0]
     forwarded = shifted(outward[None], "section", 1)
+    forwarded = jnp.where(lax.axis_index("section") == 0, jnp.zeros_like(forwarded), forwarded)
     returned = shifted(gradient[None], "section", -1)
     return (forwarded, returned)
 

time: 86 us -> 86.3 us (level)
  other arithmetic: 5.93 us -> 9.23 us
  waiting for transfers between devices: 58.3 us -> 55.3 us
  local copies, waits for them, and re-layouts: 4.76 us -> 3.79 us
  matrix products: 8.56 us -> 9.53 us
    select_n x0 -> x1, other arithmetic: none -> 2.27 us  [shards(): jnp.where(lax.axis_index('section') == 0, jnp.zeros_like(forwarded), forw...]
    ppermute x2, waiting for transfers between devices: 13.7 us -> 11.7 us  [shifted(): lax.ppermute(value, axis, [(source, source + steps) for source in range(l...]
    broadcast_in_dim x1, other arithmetic: 0.66 us -> 1.68 us  [shards(): returned = shifted(gradient[None], 'section', -1)]
    unnamed x14 -> x13, local copies, waits for them, and re-layouts: 3.49 us -> 2.52 us
    dot_general x2, matrix products: 1.31 us -> 2.28 us  [section_layer(): jnp.dot(mixed, w_out, preferred_element_type=jnp.float32)]
    ppermute x1, waiting for transfers between devices: 44.6 us -> 43.6 us  [shards(): fetched = lax.ppermute(stash[0], 'section', mirror)]
  transfers between devices with their start and end apart: 3 -> 3, of which waited for: 2 -> 2; matrix products, arithmetic and copies ran while one was open for 18% -> 23% of each run, Pallas kernels for 0% -> 0%
where the time goes in v9:
time: 86.3 us; the launch traced here: 86 us
  waiting for transfers between devices  55.3 us (64%)
  matrix products  9.53 us (11%)
  other arithmetic  9.23 us (11%)
  starting transfers between devices  7.14 us (8%)
  local copies, waits for them, and re-layouts  3.79 us (4%)
  between operations  1.03 us (1%)
    ppermute x1, waiting for transfers between devices, shards(): fetched = lax.ppermute(stash[0], 'section', mirror)  43.6 us
    ppermute x2, waiting for transfers between devices, shifted(): lax.ppermute(value, axis, [(source, source + steps) for source in range(l...  11.7 us
    ppermute x2, starting transfers between devices, shifted(): lax.ppermute(value, axis, [(source, source + steps) for source in range(l...  4.26 us
    dot_general x3, matrix products, section_layer(): query = jnp.dot(normed, w_query, preferred_element_type=jnp.float32)  3.83 us
    ppermute x1, starting transfers between devices, shards(): fetched = lax.ppermute(stash[0], 'section', mirror)  2.88 us
    unnamed x13, local copies, waits for them, and re-layouts  2.52 us
    dot_general x2, matrix products, section_layer(): jnp.dot(mixed, w_out, preferred_element_type=jnp.float32)  2.28 us
    select_n x1, other arithmetic, shards(): jnp.where(lax.axis_index('section') == 0, jnp.zeros_like(forwarded), forw...  2.27 us
  transfers between devices with their start and end apart: 3, of which 2 were waited for; matrix products, arithmetic and copies ran while one was open for 23% of the time, Pallas kernels for 0%

profile of v9, /device:TPU:9, one launch (start us, length us, event | category | flops | bytes accessed | tf_op | source)
XLA Modules:
  0.0 86.0 jit_solution(1244580171182226135)
XLA Ops:
  0.6 2.9 %collective-permute-start.1 = (bf16[128,4096]{1,0:T(8,128)(2,1)}, bf16[128,4096]{1,0:T(8,128)(2,1)S(1)}, u32[]{:S(2)}, u32[]{:S(2)}) collective-permute-start(bf16[128,4096]{1,0:T(8,128)(2,1)} %bitcast.87), channel_id=1, source_target_pairs={{0,15},{1,14},{2,13},{3,12},{4,11},{5,10},{6,9},{7,8},{8,7},{9,6},... | collective-permute-start | bytes 3145736 | tf_op jit(solution)/shard_map/ppermute | solution.py:71
  3.5 0.9 %compare_bitcast_fusion = (pred[127,1]{0,1:T(4,128)(4,1)S(1)}, pred[127,1]{0,1:T(4,128)(4,1)S(1)}) fusion(s32[1,2,128]{2,1,0:T(2,128)} %param.15), kind=kLoop, calls=%fused_computation.132 | loop fusion | flops 254 | bytes 2286 | tf_op jit(solution)/shard_map/jvp()/concatenate | solution.py:17
  4.4 0.8 slice_bitcast_fusion
  5.3 0.1 copy.16
  5.4 0.2 reduce-window.17
  5.6 0.1 reduce.1
  5.7 0.1 copy.14
  5.8 0.2 reduce-window.16
  6.0 0.1 reduce
  6.1 1.5 %fusion.6 = f32[128]{0:T(128)S(1)} fusion(bf16[1,128,4096]{2,1,0:T(8,128)(2,1)} %param.8), kind=kLoop, calls=%fused_computation.16 | loop fusion | flops 1572736 | bytes 1049088 | tf_op jit(solution)/shard_map/reduce_sum | solution.py:39
  7.6 2.5 %fusion.25 = f32[128,256]{1,0:T(8,128)S(1)} fusion(bf16[1,4096,256]{2,1,0:T(8,128)(2,1)} %param.12, bf16[1,128,4096]{2,1,0:T(8,128)(2,1)} %param.8, f32[4096]{0:T(1024)} %bitcast.82, f32[128]{0:T(128)S(1)} %add_rsqrt_fusion), kind=kOutput, calls=%fused_computation.35 | convolution fusion | flops 270532608 | bytes 3293696 | tf_op jit(solution)/shard_map/dot_general | solution.py:41
  10.2 0.5 multiply_cosine_fusion
  10.7 0.1 pad_maximum_fusion.2
  10.9 0.5 fusion.20
  11.5 0.1 fusion.73
  11.7 0.1 copy.15
  11.8 0.1 fusion.47
  11.9 0.1 fusion.51
  12.0 0.3 fusion.95
  12.3 0.2 convolution_convert_fusion.3
  12.5 0.5 copy-done.1
  13.0 1.4 %fusion.4 = bf16[1,128,4096]{2,1,0:T(8,128)(2,1)} fusion(bf16[1,128,4096]{2,1,0:T(8,128)(2,1)S(1)} %copy-done.3, bf16[1,256,4096]{2,1,0:T(8,128)(2,1)S(1)} %copy-done.1, bf16[128,128]{0,1:T(8,128)(2,1)S(1)} %get-tuple-element.26, bf16[128,128]{0,1:T(8,128)(2,1)S(1)} %get-tuple-element.25), kind=kOutput, calls=%fused_computation.7 | convolution fusion | flops 270139392 | bytes 4259840 | tf_op jit(solution)/shard_map/dot_general | solution.py:63
  14.5 1.9 %collective-permute-start = (bf16[1,128,4096]{2,1,0:T(8,128)(2,1)}, bf16[1,128,4096]{2,1,0:T(8,128)(2,1)}, u32[]{:S(2)}, u32[]{:S(2)}) collective-permute-start(bf16[1,128,4096]{2,1,0:T(8,128)(2,1)} %fusion.4), channel_id=1, source_target_pairs={{0,1},{1,2},{2,3},{3,4},{4,5},{5,6},{6,7},{7,8},{8,9},{9,10},{10,1... | collective-permute-start | bytes 3145736 | tf_op jit(solution)/shard_map/ppermute | solution.py:12
  16.4 0.1 copy.17
  16.5 0.8 fusion.30
  17.4 43.6 %collective-permute-done.1 = bf16[128,4096]{1,0:T(8,128)(2,1)S(1)} collective-permute-done((bf16[128,4096]{1,0:T(8,128)(2,1)}, bf16[128,4096]{1,0:T(8,128)(2,1)S(1)}, u32[]{:S(2)}, u32[]{:S(2)}) %collective-permute-start.1) | collective-permute-done | bytes 1048608 | tf_op jit(solution)/shard_map/ppermute | solution.py:71
  61.0 0.3 fusion.10
  61.3 0.5 fusion.18
  61.9 1.0 %copy-done.4 = bf16[1,4096,256]{2,1,0:T(8,128)(2,1)S(1)} copy-done((bf16[1,4096,256]{2,1,0:T(8,128)(2,1)S(1)}, bf16[1,4096,256]{2,1,0:T(8,128)(2,1)}, u32[]{:S(2)}) %copy-start.4) | copy-done | bytes 2097176
  62.9 0.5 fusion.23
  63.5 0.1 fusion.44
  63.6 0.1 pad_maximum_fusion.4
  63.7 0.1 fusion.53
  63.8 0.2 fusion.72
  64.0 0.2 convolution_convert_fusion.6
  64.2 0.2 multiply_reduce_fusion
  64.4 0.2 fusion.87
  64.5 0.2 bitcast_multiply_fusion
  64.8 0.1 fusion.89
  65.0 0.1 fusion.55
  65.1 0.8 convolution_convert_fusion
  65.9 0.1 pad_add_fusion
  66.0 1.0 %fusion.13 = (f32[128]{0:T(128)S(1)}, f32[128,4096]{1,0:T(8,128)S(1)}) fusion(bf16[128,4096]{1,0:T(8,128)(2,1)S(1)} %collective-permute-done.1, f32[4096]{0:T(1024)S(1)} %bitcast.86, bf16[128,4096]{1,0:T(8,128)(2,1)S(1)} %convolution_convert_fusion, bf16[1,4096,256]{2,1,0:T(8,128)(2,1)S(1)} %copy-done, f32[128,128]{1,0:T(8,128)S(1)} %pad_add_fusion, ...), kind=kOutput, calls=%fused_computation.23 | convolution fusion | flops 272170880 | bytes 6406656 | tf_op jit(solution)/shard_map/transpose(jvp())/dot_general | solution.py:42
  67.0 1.7 %fusion.36 = bf16[1,128,4096]{2,1,0:T(8,128)(2,1)} fusion(bf16[128,4096]{1,0:T(8,128)(2,1)S(1)} %collective-permute-done.1, f32[128,4096]{1,0:T(8,128)S(1)} %get-tuple-element.48, bf16[1,128,4096]{2,1,0:T(8,128)(2,1)S(1)} %copy-done.2, f32[128]{0:T(128)S(1)} %multiply_multiply_fusion.1, f32[128]{0:T(128)S(1)} %fusion.78), kind=kLoop, calls=%fused_computation.51 | loop fusion | flops 4194304 | bytes 5243904 | tf_op jit(solution)/shard_map/broadcast_in_dim | solution.py:83
  68.7 2.4 %collective-permute-start.2 = (bf16[1,128,4096]{2,1,0:T(8,128)(2,1)}, bf16[1,128,4096]{2,1,0:T(8,128)(2,1)S(1)}, u32[]{:S(2)}, u32[]{:S(2)}) collective-permute-start(bf16[1,128,4096]{2,1,0:T(8,128)(2,1)} %fusion.36), channel_id=1, source_target_pairs={{1,0},{2,1},{3,2},{4,3},{5,4},{6,5},{7,6},{8,7},{9,8},{10,9},{11,1... | collective-permute-start | bytes 3145736 | tf_op jit(solution)/shard_map/ppermute | solution.py:12
  71.1 2.3 %broadcast_select_fusion = bf16[1,128,4096]{2,1,0:T(8,128)(2,1)} fusion(bf16[1,128,4096]{2,1,0:T(8,128)(2,1)} %collective-permute-done, pred[]{:T(512)S(6)} %eq.41), kind=kLoop, calls=%fused_computation.54 | loop fusion | flops 524288 | bytes 2097153 | tf_op jit(solution)/shard_map/jit(_where)/select_n | solution.py:82
  73.4 11.7 %collective-permute-done.2 = bf16[1,128,4096]{2,1,0:T(8,128)(2,1)S(1)} collective-permute-done((bf16[1,128,4096]{2,1,0:T(8,128)(2,1)}, bf16[1,128,4096]{2,1,0:T(8,128)(2,1)S(1)}, u32[]{:S(2)}, u32[]{:S(2)}) %collective-permute-start.2) | collective-permute-done | bytes 1048608 | tf_op jit(solution)/shard_map/ppermute | solution.py:12
  85.0 1.0 %copy.30 = bf16[1,128,4096]{2,1,0:T(8,128)(2,1)} copy(bf16[1,128,4096]{2,1,0:T(8,128)(2,1)S(1)} %collective-permute-done.2) | data formatting | bytes 2097152
  (31 shorter events, 0.6 us)
Async XLA Ops:
  0.6 10.3 %copy-start = (bf16[1,4096,256]{2,1,0:T(8,128)(2,1)S(1)}, bf16[1,4096,256]{2,1,0:T(8,128)(2,1)}, u32[]{:S(2)}) copy-start(bf16[1,4096,256]{2,1,0:T(8,128)(2,1)} %param.13) | copy-start | bytes 6291460
  0.6 60.4 %collective-permute-start.1 = (bf16[128,4096]{1,0:T(8,128)(2,1)}, bf16[128,4096]{1,0:T(8,128)(2,1)S(1)}, u32[]{:S(2)}, u32[]{:S(2)}) collective-permute-start(bf16[128,4096]{1,0:T(8,128)(2,1)} %bitcast.87), channel_id=1, source_target_pairs={{0,15},{1,14},{2,13},{3,12},{4,11},{5,10},{6,9},{7,8},{8,7},{9,6},... | collective-permute-start | bytes 3145736 | tf_op jit(solution)/shard_map/ppermute | solution.py:71
  7.6 3.3 %copy-start.3 = (bf16[1,128,4096]{2,1,0:T(8,128)(2,1)S(1)}, bf16[1,128,4096]{2,1,0:T(8,128)(2,1)}, u32[]{:S(2)}) copy-start(bf16[1,128,4096]{2,1,0:T(8,128)(2,1)} %param.8) | copy-start | bytes 3145732
  7.6 3.3 %copy-start.5 = (f32[1,4096]{1,0:T(1,128)S(1)}, f32[1,4096]{1,0:T(1,128)}, u32[]{:S(2)}) copy-start(f32[1,4096]{1,0:T(1,128)} %param.11) | copy-start | bytes 49156
  11.4 1.6 %copy-start.1 = (bf16[1,256,4096]{2,1,0:T(8,128)(2,1)S(1)}, bf16[1,256,4096]{2,1,0:T(8,128)(2,1)}, u32[]{:S(2)}) copy-start(bf16[1,256,4096]{2,1,0:T(8,128)(2,1)} %param.14) | copy-start | bytes 6291460
  13.0 3.5 %copy-start.2 = (bf16[1,128,4096]{2,1,0:T(8,128)(2,1)S(1)}, bf16[1,128,4096]{2,1,0:T(8,128)(2,1)}, u32[]{:S(2)}) copy-start(bf16[1,128,4096]{2,1,0:T(8,128)(2,1)} %param.10) | copy-start | bytes 3145732
  14.5 56.6 %collective-permute-start = (bf16[1,128,4096]{2,1,0:T(8,128)(2,1)}, bf16[1,128,4096]{2,1,0:T(8,128)(2,1)}, u32[]{:S(2)}, u32[]{:S(2)}) collective-permute-start(bf16[1,128,4096]{2,1,0:T(8,128)(2,1)} %fusion.4), channel_id=1, source_target_pairs={{0,1},{1,2},{2,3},{3,4},{4,5},{5,6},{6,7},{7,8},{8,9},{9,10},{10,1... | collective-permute-start | bytes 3145736 | tf_op jit(solution)/shard_map/ppermute | solution.py:12
  61.3 1.6 %copy-start.4 = (bf16[1,4096,256]{2,1,0:T(8,128)(2,1)S(1)}, bf16[1,4096,256]{2,1,0:T(8,128)(2,1)}, u32[]{:S(2)}) copy-start(bf16[1,4096,256]{2,1,0:T(8,128)(2,1)} %param.12) | copy-start | bytes 6291460
  68.7 16.3 %collective-permute-start.2 = (bf16[1,128,4096]{2,1,0:T(8,128)(2,1)}, bf16[1,128,4096]{2,1,0:T(8,128)(2,1)S(1)}, u32[]{:S(2)}, u32[]{:S(2)}) collective-permute-start(bf16[1,128,4096]{2,1,0:T(8,128)(2,1)} %fusion.36), channel_id=1, source_target_pairs={{1,0},{2,1},{3,2},{4,3},{5,4},{6,5},{7,6},{8,7},{9,8},{10,9},{11,1... | collective-permute-start | bytes 3145736 | tf_op jit(solution)/shard_map/ppermute | solution.py:12

commit v10 on v7

--- a/solution.py
+++ b/solution.py
@@ -3,6 +3,7 @@
 import jax
 import jax.numpy as jnp
 from jax import lax
+from jax.experimental import pallas as pl
 from jax.sharding import PartitionSpec as P
 
 
@@ -65,6 +66,102 @@
     )
 
 
+def flip(block, sign):
+    half = block.shape[-1] // 2
+    return jnp.concatenate([sign * block[:, half:], -sign * block[:, :half]], -1)
+
+
+def attention_gradient_kernel(
+    query_ref, keyval_ref, cosine_ref, sine_ref, allowed_ref, upstream_ref, dquery_ref, dkeyval_ref
+):
+    rows = cosine_ref.shape[0]
+    head_dim = cosine_ref.shape[1]
+    heads = query_ref.shape[1] // head_dim
+    cosine = cosine_ref[...]
+    sine_part = sine_ref[...]
+    keyval = keyval_ref[...]
+    keys = (keyval[:, :head_dim] * cosine + flip(keyval[:, :head_dim], -1.0) * sine_part).astype(
+        jnp.bfloat16
+    )
+    values = keyval[:, head_dim:].astype(jnp.bfloat16)
+    query = query_ref[...]
+    stacked = jnp.concatenate(
+        [query[:, head * head_dim : (head + 1) * head_dim] for head in range(heads)], 0
+    )
+    cosines = jnp.concatenate([cosine] * heads, 0)
+    sines = jnp.concatenate([sine_part] * heads, 0)
+    turned = (stacked * cosines + flip(stacked, -1.0) * sines).astype(jnp.bfloat16)
+    contract = (((1,), (1,)), ((), ()))
+    scores = lax.dot_general(turned, keys, contract, preferred_element_type=jnp.float32)
+    scores = scores / math.sqrt(head_dim)
+    allowed = jnp.concatenate([allowed_ref[...]] * heads, 0) > 0
+    raised = jnp.exp(scores)
+    expd = jnp.where(allowed, raised, 0.0)
+    total = jnp.sum(expd, axis=-1, keepdims=True)
+    probs = (expd / total).astype(jnp.bfloat16)
+    upstream = upstream_ref[...]
+    dmixed = jnp.concatenate(
+        [upstream[:, head * head_dim : (head + 1) * head_dim] for head in range(heads)], 0
+    )
+    dprobs = lax.dot_general(dmixed, values, contract, preferred_element_type=jnp.float32)
+    dprobs = dprobs.astype(jnp.bfloat16).astype(jnp.float32)
+    dvalues = lax.dot_general(
+        probs, dmixed, (((0,), (0,)), ((), ())), preferred_element_type=jnp.float32
+    ).astype(jnp.bfloat16)
+    dtotal = -jnp.sum(dprobs * expd / (total * total), axis=-1, keepdims=True)
+    dexpd = dprobs / total + dtotal
+    dscores = (jnp.where(allowed, dexpd, 0.0) * raised / math.sqrt(head_dim)).astype(jnp.bfloat16)
+    dturned = jnp.dot(dscores, keys, preferred_element_type=jnp.float32)
+    dturned = dturned.astype(jnp.bfloat16).astype(jnp.float32)
+    dkeys = lax.dot_general(
+        dscores, turned, (((0,), (0,)), ((), ())), preferred_element_type=jnp.float32
+    )
+    dkeys = dkeys.astype(jnp.bfloat16).astype(jnp.float32)
+    dstacked = dturned * cosines + flip(dturned * sines, 1.0)
+    dquery_ref[...] = jnp.concatenate(
+        [dstacked[head * rows : (head + 1) * rows] for head in range(heads)], 1
+    )
+    dkeyval_ref[...] = jnp.concatenate(
+        [dkeys * cosine + flip(dkeys * sine_part, 1.0), dvalues.astype(jnp.float32)], 1
+    )
+
+
+def attention_gradient(query, keyval, cosine, sine_part, allowed, dmixed):
+    return pl.pallas_call(
+        attention_gradient_kernel,
+        out_shape=(
+            jax.ShapeDtypeStruct(query.shape, jnp.float32),
+            jax.ShapeDtypeStruct(keyval.shape, jnp.float32),
+        ),
+    )(query, keyval, cosine, sine_part, allowed, dmixed)
+
+
+def input_gradient(acts, cotangent, gain, w_query, w_kv, w_out, segment):
+    rows = acts.shape[0]
+    head_dim = w_kv.shape[1] // 2
+
+    def project(values32):
+        scale = lax.rsqrt(jnp.mean(values32 * values32, axis=-1, keepdims=True) + 1e-05)
+        normed = (values32 * scale * gain).astype(jnp.bfloat16)
+        query = jnp.dot(normed, w_query, preferred_element_type=jnp.float32)
+        keyval = jnp.dot(normed, w_kv, preferred_element_type=jnp.float32)
+        return (query, keyval)
+
+    cosine, sine_part = rotary_tables(segment, head_dim)
+    index = jnp.arange(rows, dtype=jnp.int32)
+    allowed = (segment[:, None] == segment[None, :]) & (index[None, :] <= index[:, None])
+    dmixed = lax.dot_general(
+        cotangent, w_out, (((1,), (1,)), ((), ())), preferred_element_type=jnp.float32
+    ).astype(jnp.bfloat16)
+    values32 = acts.astype(jnp.float32)
+    (query, keyval), pullback = jax.vjp(project, values32)
+    dquery, dkeyval = attention_gradient(
+        query, keyval, cosine, sine_part, allowed.astype(jnp.float32), dmixed
+    )
+    dvalues32 = pullback((dquery, dkeyval))[0]
+    return (cotangent.astype(jnp.float32) + dvalues32).astype(jnp.bfloat16)
+
+
 def shards(section_input, stash, cotangent, norm_gain, w_query, w_kv, w_out, doc_ids):
     pieces = lax.axis_size("section")
     mirror = [(source, pieces - 1 - source) for source in range(pieces)]
@@ -72,12 +169,9 @@
     outward = section_layer(
         section_input[0], norm_gain[0], w_query[0], w_kv[0], w_out[0], doc_ids[0, 0]
     )
-
-    def replay(acts):
-        return section_layer(acts, norm_gain[0], w_query[0], w_kv[0], w_out[0], doc_ids[0, 1])
-
-    unused, pullback = jax.vjp(replay, fetched)
-    gradient = pullback(cotangent[0])[0]
+    gradient = input_gradient(
+        fetched, cotangent[0], norm_gain[0], w_query[0], w_kv[0], w_out[0], doc_ids[0, 1]
+    )
     forwarded = shifted(outward[None], "section", 1)
     returned = shifted(gradient[None], "section", -1)
     return (forwarded, returned)

time: 86 us -> 90.8 us (1.056)
  matrix products: 8.56 us -> 12.2 us
  waiting for transfers between devices: 58.3 us -> 54.8 us
  Pallas kernels: 0 us -> 2.51 us
  other arithmetic: 5.93 us -> 7.22 us
    dot_general x0 -> x5, matrix products: none -> 7.25 us  [the longest x2 3.65 us: project(): query = jnp.dot(normed, w_query, preferred_element_type=jnp.float32)]
    ppermute x1, waiting for transfers between devices: 44.6 us -> 41 us  [shards(): fetched = lax.ppermute(stash[0], 'section', mirror)]
    pallas_call x0 -> x1, Pallas kernels: none -> 2.51 us  [attention_gradient(): pl.pallas_call(attention_gradient_kernel, out_shape=(jax.ShapeDtypeStruct...]
    dot_general x3 -> x1, matrix products: 2.01 us -> 0.52 us  [section_layer(): keyval = jnp.dot(normed, w_kv, preferred_element_type=jnp.float32)]
    dot_general x3 -> x1, matrix products: 3.83 us -> 2.5 us  [section_layer(): query = jnp.dot(normed, w_query, preferred_element_type=jnp.float32)]
    unnamed x14 -> x18, local copies, waits for them, and re-layouts: 3.49 us -> 4.53 us
  transfers between devices with their start and end apart: 3 -> 3, of which waited for: 2 -> 2; matrix products, arithmetic and copies ran while one was open for 18% -> 23% of each run, Pallas kernels for 0% -> 3%
where the time goes in v10:
time: 90.8 us; the launch traced here: 90.4 us
  waiting for transfers between devices  54.8 us (60%)
  matrix products  12.2 us (13%)
  other arithmetic  7.22 us (8%)
  starting transfers between devices  7.14 us (8%)
  local copies, waits for them, and re-layouts  5.65 us (6%)
  Pallas kernels  2.51 us (3%)
    ppermute x1, waiting for transfers between devices, shards(): fetched = lax.ppermute(stash[0], 'section', mirror)  41 us
    ppermute x2, waiting for transfers between devices, shifted(): lax.ppermute(value, axis, [(source, source + steps) for source in range(l...  13.7 us
    unnamed x18, local copies, waits for them, and re-layouts  4.53 us
    ppermute x2, starting transfers between devices, shifted(): lax.ppermute(value, axis, [(source, source + steps) for source in range(l...  4.26 us
    dot_general x2, matrix products, project(): query = jnp.dot(normed, w_query, preferred_element_type=jnp.float32)  3.65 us
    ppermute x1, starting transfers between devices, shards(): fetched = lax.ppermute(stash[0], 'section', mirror)  2.88 us
    pallas_call x1, Pallas kernels, attention_gradient(): pl.pallas_call(attention_gradient_kernel, out_shape=(jax.ShapeDtypeStruct...  2.51 us
    dot_general x1, matrix products, section_layer(): query = jnp.dot(normed, w_query, preferred_element_type=jnp.float32)  2.5 us
  transfers between devices with their start and end apart: 3, of which 2 were waited for; matrix products, arithmetic and copies ran while one was open for 23% of the time, Pallas kernels for 3%

profile of v10, /device:TPU:9, one launch (start us, length us, event | category | flops | bytes accessed | tf_op | source)
XLA Modules:
  0.0 90.4 jit_solution(14155300528251612148)
XLA Ops:
  0.6 0.0 copy-start
  0.6 2.9 %collective-permute-start.1 = (bf16[128,4096]{1,0:T(8,128)(2,1)}, bf16[128,4096]{1,0:T(8,128)(2,1)S(1)}, u32[]{:S(2)}, u32[]{:S(2)}) collective-permute-start(bf16[128,4096]{1,0:T(8,128)(2,1)} %bitcast.67), channel_id=1, source_target_pairs={{0,15},{1,14},{2,13},{3,12},{4,11},{5,10},{6,9},{7,8},{8,7},{9,6},... | collective-permute-start | bytes 3145736 | tf_op jit(solution)/shard_map/ppermute | solution.py:168
  3.5 0.9 %compare_bitcast_fusion = (pred[127,1]{0,1:T(4,128)(4,1)S(1)}, pred[127,1]{0,1:T(4,128)(4,1)S(1)}) fusion(s32[1,2,128]{2,1,0:T(2,128)} %param.15), kind=kLoop, calls=%fused_computation.85 | loop fusion | flops 254 | bytes 2286 | tf_op jit(solution)/shard_map/concatenate | solution.py:18
  4.4 0.8 slice_bitcast_fusion
  5.2 0.1 fusion.56
  5.3 0.1 copy.15
  5.4 0.2 reduce-window.17
  5.6 0.1 reduce.1
  5.7 0.1 copy.13
  5.8 0.2 reduce-window.16
  6.0 0.1 reduce
  6.1 1.5 %fusion.6 = f32[128]{0:T(128)S(1)} fusion(bf16[1,128,4096]{2,1,0:T(8,128)(2,1)} %param.8), kind=kLoop, calls=%fused_computation.16 | loop fusion | flops 1572736 | bytes 1049088 | tf_op jit(solution)/shard_map/reduce_sum | solution.py:40
  7.6 0.0 copy-start.7
  7.6 2.5 %fusion.26 = f32[128,256]{1,0:T(8,128)S(1)} fusion(bf16[1,4096,256]{2,1,0:T(8,128)(2,1)} %param.12, bf16[1,128,4096]{2,1,0:T(8,128)(2,1)} %param.8, f32[4096]{0:T(1024)} %bitcast.62, f32[128]{0:T(128)S(1)} %add_rsqrt_fusion), kind=kOutput, calls=%fused_computation.36 | convolution fusion | flops 270532608 | bytes 3293696 | tf_op jit(solution)/shard_map/dot_general | solution.py:42
  10.2 0.5 multiply_sine_fusion
  10.7 0.1 pad_maximum_fusion.1
  10.8 0.1 pad_maximum_fusion.2
  10.9 0.5 fusion.21
  11.4 0.0 copy-start.1
  11.5 0.1 slice_negate_fusion
  11.5 0.1 fusion.53
  11.6 0.1 copy.14
  11.8 0.1 fusion.41
  11.9 0.1 fusion.45
  12.0 0.3 fusion.63
  12.2 0.2 convolution_convert_fusion.2
  12.5 0.5 copy-done.1
  13.0 1.4 %fusion.4 = bf16[1,128,4096]{2,1,0:T(8,128)(2,1)} fusion(bf16[1,128,4096]{2,1,0:T(8,128)(2,1)S(1)} %copy-done.4, bf16[1,256,4096]{2,1,0:T(8,128)(2,1)S(1)} %copy-done.1, bf16[128,128]{0,1:T(8,128)(2,1)S(1)} %get-tuple-element.13, bf16[128,128]{0,1:T(8,128)(2,1)S(1)} %get-tuple-element.12), kind=kOutput, calls=%fused_computation.7 | convolution fusion | flops 270139392 | bytes 4259840 | tf_op jit(solution)/shard_map/dot_general | solution.py:64
  14.5 1.9 %collective-permute-start = (bf16[1,128,4096]{2,1,0:T(8,128)(2,1)}, bf16[1,128,4096]{2,1,0:T(8,128)(2,1)}, u32[]{:S(2)}, u32[]{:S(2)}) collective-permute-start(bf16[1,128,4096]{2,1,0:T(8,128)(2,1)} %fusion.4), channel_id=1, source_target_pairs={{0,1},{1,2},{2,3},{3,4},{4,5},{5,6},{6,7},{7,8},{8,9},{9,10},{10,1... | collective-permute-start | bytes 3145736 | tf_op jit(solution)/shard_map/ppermute | solution.py:13
  16.4 0.7 pad_maximum_fusion.3.cosine_ref
  17.1 0.7 pad_maximum_fusion.4.sine_ref
  17.8 0.7 fusion.54.allowed_ref
  18.5 1.5 %fusion.30.upstream_ref = bf16[128,256]{1,0:T(8,128)(2,1)} fusion(bf16[1,256,4096]{2,1,0:T(8,128)(2,1)S(1)} %copy-done.1, bf16[1,128,4096]{2,1,0:T(8,128)(2,1)S(1)} %copy-done.2), kind=kOutput, calls=%fused_computation.41 | convolution fusion | flops 268468224 | bytes 3211264 | tf_op jit(solution)/shard_map/dot_general | solution.py:153
  20.0 41.0 %collective-permute-done.1 = bf16[128,4096]{1,0:T(8,128)(2,1)S(1)} collective-permute-done((bf16[128,4096]{1,0:T(8,128)(2,1)}, bf16[128,4096]{1,0:T(8,128)(2,1)S(1)}, u32[]{:S(2)}, u32[]{:S(2)}) %collective-permute-start.1) | collective-permute-done | bytes 1048608 | tf_op jit(solution)/shard_map/ppermute | solution.py:168
  61.0 0.3 fusion.11
  61.3 1.1 %fusion.19.keyval_ref = f32[128,256]{1,0:T(8,128)} fusion(bf16[1,4096,256]{2,1,0:T(8,128)(2,1)S(1)} %copy-done, bf16[128,4096]{1,0:T(8,128)(2,1)S(1)} %collective-permute-done.1, f32[4096]{0:T(1024)S(1)} %bitcast.64, f32[128]{0:T(128)S(1)} %fusion.58), kind=kOutput, calls=%fused_computation.29 | convolution fusion | flops 270532608 | bytes 3293696 | tf_op jit(solution)/shard_map/jvp()/dot_general | solution.py:147
  62.5 0.5 copy-done.5
  62.9 1.1 %fusion.24.query_ref = f32[128,256]{1,0:T(8,128)} fusion(bf16[1,4096,256]{2,1,0:T(8,128)(2,1)S(1)} %copy-done.5, bf16[128,4096]{1,0:T(8,128)(2,1)S(1)} %collective-permute-done.1, f32[4096]{0:T(1024)S(1)} %bitcast.65, f32[128]{0:T(128)S(1)} %fusion.58), kind=kOutput, calls=%fused_computation.34 | convolution fusion | flops 270532608 | bytes 3293696 | tf_op jit(solution)/shard_map/jvp()/dot_general | solution.py:146
  64.1 2.5 %shard_map.95 = (f32[128,256]{1,0:T(8,128)}, f32[128,256]{1,0:T(8,128)}) custom-call(f32[128,256]{1,0:T(8,128)} %fusion.24.query_ref, f32[128,256]{1,0:T(8,128)} %fusion.19.keyval_ref, f32[128,128]{1,0:T(8,128)} %pad_maximum_fusion.3.cosine_ref, f32[128,128]{1,0:T(8,128)} %pad_maximum_fusion.4.sine_ref, f32[128,128]{1,0:T(8,128)} %fusion.54.allowed_ref, ...), custom_call_target="tpu_custom_call" | custom-call | tf_op jit(solution)/shard_map/pallas_call | solution.py:130
  66.6 2.5 %convolution_convert_fusion = bf16[128,4096]{1,0:T(8,128)(2,1)S(1)} fusion(f32[128,256]{1,0:T(8,128)} %get-tuple-element.5, bf16[1,4096,256]{2,1,0:T(8,128)(2,1)} %param.12), kind=kOutput, calls=%fused_computation.2 | convolution fusion | flops 268435456 | bytes 3276800 | tf_op jit(solution)/shard_map/transpose(jvp())/dot_general | solution.py:146
  69.1 0.0 copy-start.3
  69.1 1.0 %fusion.14 = (f32[128]{0:T(128)S(1)}, f32[128,4096]{1,0:T(8,128)S(1)}) fusion(bf16[128,4096]{1,0:T(8,128)(2,1)S(1)} %collective-permute-done.1, f32[4096]{0:T(1024)S(1)} %bitcast.66, bf16[128,4096]{1,0:T(8,128)(2,1)S(1)} %convolution_convert_fusion, f32[128,256]{1,0:T(8,128)S(1)} %copy-done.6, bf16[1,4096,256]{2,1,0:T(8,128)(2,1)S(1)} %copy-done), kind=kOutput, calls=%fused_computation.24 | convolution fusion | flops 271581056 | bytes 6439424 | tf_op jit(solution)/shard_map/transpose(jvp())/dot_general | solution.py:147
  70.2 0.2 copy-done.3
  70.4 0.7 fusion.33
  71.0 2.4 %collective-permute-start.2 = (bf16[1,128,4096]{2,1,0:T(8,128)(2,1)S(1)}, bf16[1,128,4096]{2,1,0:T(8,128)(2,1)S(1)}, u32[]{:S(2)}, u32[]{:S(2)}) collective-permute-start(bf16[1,128,4096]{2,1,0:T(8,128)(2,1)S(1)} %fusion.33), channel_id=1, source_target_pairs={{1,0},{2,1},{3,2},{4,3},{5,4},{6,5},{7,6},{8,7},{9,8},{10,9},{11,1... | collective-permute-start | bytes 3145736 | tf_op jit(solution)/shard_map/ppermute | solution.py:13
  73.4 13.7 %collective-permute-done.2 = bf16[1,128,4096]{2,1,0:T(8,128)(2,1)S(1)} collective-permute-done((bf16[1,128,4096]{2,1,0:T(8,128)(2,1)S(1)}, bf16[1,128,4096]{2,1,0:T(8,128)(2,1)S(1)}, u32[]{:S(2)}, u32[]{:S(2)}) %collective-permute-start.2) | collective-permute-done | bytes 1048608 | tf_op jit(solution)/shard_map/ppermute | solution.py:13
  87.1 2.3 %copy.19 = bf16[1,128,4096]{2,1,0:T(8,128)(2,1)} copy(bf16[1,128,4096]{2,1,0:T(8,128)(2,1)} %collective-permute-done) | data formatting | bytes 2097152
  89.4 1.0 %copy.20 = bf16[1,128,4096]{2,1,0:T(8,128)(2,1)} copy(bf16[1,128,4096]{2,1,0:T(8,128)(2,1)S(1)} %collective-permute-done.2) | data formatting | bytes 2097152
  (19 shorter events, 0.1 us)
Async XLA Ops:
  0.6 10.3 %copy-start = (bf16[1,4096,256]{2,1,0:T(8,128)(2,1)S(1)}, bf16[1,4096,256]{2,1,0:T(8,128)(2,1)}, u32[]{:S(2)}) copy-start(bf16[1,4096,256]{2,1,0:T(8,128)(2,1)} %param.13) | copy-start | bytes 6291460
  0.6 60.4 %collective-permute-start.1 = (bf16[128,4096]{1,0:T(8,128)(2,1)}, bf16[128,4096]{1,0:T(8,128)(2,1)S(1)}, u32[]{:S(2)}, u32[]{:S(2)}) collective-permute-start(bf16[128,4096]{1,0:T(8,128)(2,1)} %bitcast.67), channel_id=1, source_target_pairs={{0,15},{1,14},{2,13},{3,12},{4,11},{5,10},{6,9},{7,8},{8,7},{9,6},... | collective-permute-start | bytes 3145736 | tf_op jit(solution)/shard_map/ppermute | solution.py:168
  7.6 3.3 %copy-start.4 = (bf16[1,128,4096]{2,1,0:T(8,128)(2,1)S(1)}, bf16[1,128,4096]{2,1,0:T(8,128)(2,1)}, u32[]{:S(2)}) copy-start(bf16[1,128,4096]{2,1,0:T(8,128)(2,1)} %param.8) | copy-start | bytes 3145732
  7.6 3.3 %copy-start.7 = (f32[1,4096]{1,0:T(1,128)S(1)}, f32[1,4096]{1,0:T(1,128)}, u32[]{:S(2)}) copy-start(f32[1,4096]{1,0:T(1,128)} %param.11) | copy-start | bytes 49156
  11.4 1.6 %copy-start.1 = (bf16[1,256,4096]{2,1,0:T(8,128)(2,1)S(1)}, bf16[1,256,4096]{2,1,0:T(8,128)(2,1)}, u32[]{:S(2)}) copy-start(bf16[1,256,4096]{2,1,0:T(8,128)(2,1)} %param.14) | copy-start | bytes 6291460
  13.0 5.5 %copy-start.2 = (bf16[1,128,4096]{2,1,0:T(8,128)(2,1)S(1)}, bf16[1,128,4096]{2,1,0:T(8,128)(2,1)}, u32[]{:S(2)}) copy-start(bf16[1,128,4096]{2,1,0:T(8,128)(2,1)} %param.10) | copy-start | bytes 3145732
  14.5 58.9 %collective-permute-start = (bf16[1,128,4096]{2,1,0:T(8,128)(2,1)}, bf16[1,128,4096]{2,1,0:T(8,128)(2,1)}, u32[]{:S(2)}, u32[]{:S(2)}) collective-permute-start(bf16[1,128,4096]{2,1,0:T(8,128)(2,1)} %fusion.4), channel_id=1, source_target_pairs={{0,1},{1,2},{2,3},{3,4},{4,5},{5,6},{6,7},{7,8},{8,9},{9,10},{10,1... | collective-permute-start | bytes 3145736 | tf_op jit(solution)/shard_map/ppermute | solution.py:13
  61.3 1.6 %copy-start.5 = (bf16[1,4096,256]{2,1,0:T(8,128)(2,1)S(1)}, bf16[1,4096,256]{2,1,0:T(8,128)(2,1)}, u32[]{:S(2)}) copy-start(bf16[1,4096,256]{2,1,0:T(8,128)(2,1)} %param.12) | copy-start | bytes 6291460
  66.6 2.5 %copy-start.6 = (f32[128,256]{1,0:T(8,128)S(1)}, f32[128,256]{1,0:T(8,128)}, u32[]{:S(2)}) copy-start(f32[128,256]{1,0:T(8,128)} %get-tuple-element.4) | copy-start | bytes 393220
  69.1 1.2 %copy-start.3 = (bf16[1,128,4096]{2,1,0:T(8,128)(2,1)S(1)}, bf16[1,128,4096]{2,1,0:T(8,128)(2,1)}, u32[]{:S(2)}) copy-start(bf16[1,128,4096]{2,1,0:T(8,128)(2,1)} %param.10) | copy-start | bytes 3145732
  71.0 16.1 %collective-permute-start.2 = (bf16[1,128,4096]{2,1,0:T(8,128)(2,1)S(1)}, bf16[1,128,4096]{2,1,0:T(8,128)(2,1)S(1)}, u32[]{:S(2)}, u32[]{:S(2)}) collective-permute-start(bf16[1,128,4096]{2,1,0:T(8,128)(2,1)S(1)} %fusion.33), channel_id=1, source_target_pairs={{1,0},{2,1},{3,2},{4,3},{5,4},{6,5},{7,6},{8,7},{9,8},{10,9},{11,1... | collective-permute-start | bytes 3145736 | tf_op jit(solution)/shard_map/ppermute | solution.py:13

commit v11 on v10

--- a/solution.py
+++ b/solution.py
@@ -71,20 +71,14 @@
     return jnp.concatenate([sign * block[:, half:], -sign * block[:, :half]], -1)
 
 
-def attention_gradient_kernel(
-    query_ref, keyval_ref, cosine_ref, sine_ref, allowed_ref, upstream_ref, dquery_ref, dkeyval_ref
-):
-    rows = cosine_ref.shape[0]
-    head_dim = cosine_ref.shape[1]
-    heads = query_ref.shape[1] // head_dim
-    cosine = cosine_ref[...]
-    sine_part = sine_ref[...]
-    keyval = keyval_ref[...]
+def attention_gradient_body(query, keyval, cosine, sine_part, allowed, upstream):
+    rows = cosine.shape[0]
+    head_dim = cosine.shape[1]
+    heads = query.shape[1] // head_dim
     keys = (keyval[:, :head_dim] * cosine + flip(keyval[:, :head_dim], -1.0) * sine_part).astype(
         jnp.bfloat16
     )
     values = keyval[:, head_dim:].astype(jnp.bfloat16)
-    query = query_ref[...]
     stacked = jnp.concatenate(
         [query[:, head * head_dim : (head + 1) * head_dim] for head in range(heads)], 0
     )
@@ -94,12 +88,11 @@
     contract = (((1,), (1,)), ((), ()))
     scores = lax.dot_general(turned, keys, contract, preferred_element_type=jnp.float32)
     scores = scores / math.sqrt(head_dim)
-    allowed = jnp.concatenate([allowed_ref[...]] * heads, 0) > 0
+    allowed = jnp.concatenate([allowed] * heads, 0) > 0
     raised = jnp.exp(scores)
     expd = jnp.where(allowed, raised, 0.0)
     total = jnp.sum(expd, axis=-1, keepdims=True)
     probs = (expd / total).astype(jnp.bfloat16)
-    upstream = upstream_ref[...]
     dmixed = jnp.concatenate(
         [upstream[:, head * head_dim : (head + 1) * head_dim] for head in range(heads)], 0
     )
@@ -118,48 +111,62 @@
     )
     dkeys = dkeys.astype(jnp.bfloat16).astype(jnp.float32)
     dstacked = dturned * cosines + flip(dturned * sines, 1.0)
-    dquery_ref[...] = jnp.concatenate(
+    dquery = jnp.concatenate(
         [dstacked[head * rows : (head + 1) * rows] for head in range(heads)], 1
     )
-    dkeyval_ref[...] = jnp.concatenate(
+    dkeyval = jnp.concatenate(
         [dkeys * cosine + flip(dkeys * sine_part, 1.0), dvalues.astype(jnp.float32)], 1
     )
-
-
-def attention_gradient(query, keyval, cosine, sine_part, allowed, dmixed):
-    return pl.pallas_call(
-        attention_gradient_kernel,
-        out_shape=(
-            jax.ShapeDtypeStruct(query.shape, jnp.float32),
-            jax.ShapeDtypeStruct(keyval.shape, jnp.float32),
-        ),
-    )(query, keyval, cosine, sine_part, allowed, dmixed)
+    return (dquery, dkeyval)
+
+
+def input_gradient_kernel(
+    acts_ref, cotangent_ref, gain_ref, wq_ref, wkv_ref, cosine_ref, sine_ref, allowed_ref,
+    upstream_ref, out_ref,
+):
+    values32 = acts_ref[...].astype(jnp.float32)
+    gain = gain_ref[...]
+    width = values32.shape[1]
+    scale = lax.rsqrt(jnp.sum(values32 * values32, axis=-1, keepdims=True) / width + 1e-05)
+    normed = (values32 * scale * gain).astype(jnp.bfloat16)
+    w_query = wq_ref[...]
+    w_kv = wkv_ref[...]
+    query = jnp.dot(normed, w_query, preferred_element_type=jnp.float32)
+    keyval = jnp.dot(normed, w_kv, preferred_element_type=jnp.float32)
+    dquery, dkeyval = attention_gradient_body(
+        query, keyval, cosine_ref[...], sine_ref[...], allowed_ref[...], upstream_ref[...]
+    )
+    contract = (((1,), (1,)), ((), ()))
+    from_query = lax.dot_general(
+        dquery.astype(jnp.bfloat16), w_query, contract, preferred_element_type=jnp.float32
+    ).astype(jnp.bfloat16)
+    from_keyval = lax.dot_general(
+        dkeyval.astype(jnp.bfloat16), w_kv, contract, preferred_element_type=jnp.float32
+    ).astype(jnp.bfloat16)
+    dnormed = (from_query.astype(jnp.float32) + from_keyval.astype(jnp.float32)).astype(
+        jnp.bfloat16
+    ).astype(jnp.float32)
+    weighted = dnormed * gain
+    spread = jnp.sum(weighted * values32, axis=-1, keepdims=True) * (scale * scale * scale) / width
+    dvalues32 = weighted * scale - values32 * spread
+    out_ref[...] = (cotangent_ref[...].astype(jnp.float32) + dvalues32).astype(out_ref.dtype)
 
 
 def input_gradient(acts, cotangent, gain, w_query, w_kv, w_out, segment):
     rows = acts.shape[0]
     head_dim = w_kv.shape[1] // 2
-
-    def project(values32):
-        scale = lax.rsqrt(jnp.mean(values32 * values32, axis=-1, keepdims=True) + 1e-05)
-        normed = (values32 * scale * gain).astype(jnp.bfloat16)
-        query = jnp.dot(normed, w_query, preferred_element_type=jnp.float32)
-        keyval = jnp.dot(normed, w_kv, preferred_element_type=jnp.float32)
-        return (query, keyval)
-
     cosine, sine_part = rotary_tables(segment, head_dim)
     index = jnp.arange(rows, dtype=jnp.int32)
     allowed = (segment[:, None] == segment[None, :]) & (index[None, :] <= index[:, None])
     dmixed = lax.dot_general(
         cotangent, w_out, (((1,), (1,)), ((), ())), preferred_element_type=jnp.float32
     ).astype(jnp.bfloat16)
-    values32 = acts.astype(jnp.float32)
-    (query, keyval), pullback = jax.vjp(project, values32)
-    dquery, dkeyval = attention_gradient(
-        query, keyval, cosine, sine_part, allowed.astype(jnp.float32), dmixed
-    )
-    dvalues32 = pullback((dquery, dkeyval))[0]
-    return (cotangent.astype(jnp.float32) + dvalues32).astype(jnp.bfloat16)
+    return pl.pallas_call(
+        input_gradient_kernel, out_shape=jax.ShapeDtypeStruct(acts.shape, acts.dtype)
+    )(
+        acts, cotangent, gain.reshape(1, -1), w_query, w_kv, cosine, sine_part,
+        allowed.astype(jnp.float32), dmixed,
+    )
 
 
 def shards(section_input, stash, cotangent, norm_gain, w_query, w_kv, w_out, doc_ids):

time: 90.8 us -> 87.3 us (0.961)
  matrix products: 12.2 us -> 6.42 us
  Pallas kernels: 2.51 us -> 7.71 us
  local copies, waits for them, and re-layouts: 5.65 us -> 3.13 us
  other arithmetic: 7.22 us -> 6.26 us
    dot_general x4 -> x0, matrix products: 5.79 us -> none  [the longest x2 3.65 us: project(): query = jnp.dot(normed, w_query, preferred_element_type=jnp.float32)]
    pallas_call x1, Pallas kernels: 2.51 us -> 7.71 us  [input_gradient(): pl.pallas_call(input_gradient_kernel, out_shape=jax.ShapeDtypeStruct(acts...]
    unnamed x18 -> x12, local copies, waits for them, and re-layouts: 4.53 us -> 2 us
    dot_general x1, matrix products: 0.52 us -> 2.56 us  [section_layer(): keyval = jnp.dot(normed, w_kv, preferred_element_type=jnp.float32)]
    dot_general x1, matrix products: 2.5 us -> 0.48 us  [section_layer(): query = jnp.dot(normed, w_query, preferred_element_type=jnp.float32)]
  transfers between devices with their start and end apart: 3 -> 3, of which waited for: 2 -> 2; matrix products, arithmetic and copies ran while one was open for 23% -> 16% of each run, Pallas kernels for 3% -> 9%
where the time goes in v11:
time: 87.3 us; the launch traced here: 87.1 us
  waiting for transfers between devices  55.6 us (64%)
  Pallas kernels  7.71 us (9%)
  starting transfers between devices  7.14 us (8%)
  matrix products  6.42 us (7%)
  other arithmetic  6.26 us (7%)
  local copies, waits for them, and re-layouts  3.13 us (4%)
    ppermute x1, waiting for transfers between devices, shards(): fetched = lax.ppermute(stash[0], 'section', mirror)  41.6 us
    ppermute x2, waiting for transfers between devices, shifted(): lax.ppermute(value, axis, [(source, source + steps) for source in range(l...  13.9 us
    pallas_call x1, Pallas kernels, input_gradient(): pl.pallas_call(input_gradient_kernel, out_shape=jax.ShapeDtypeStruct(acts...  7.71 us
    ppermute x2, starting transfers between devices, shifted(): lax.ppermute(value, axis, [(source, source + steps) for source in range(l...  4.26 us
    ppermute x1, starting transfers between devices, shards(): fetched = lax.ppermute(stash[0], 'section', mirror)  2.88 us
    dot_general x1, matrix products, section_layer(): keyval = jnp.dot(normed, w_kv, preferred_element_type=jnp.float32)  2.56 us
    unnamed x12, local copies, waits for them, and re-layouts  2 us
  transfers between devices with their start and end apart: 3, of which 2 were waited for; matrix products, arithmetic and copies ran while one was open for 16% of the time, Pallas kernels for 9%

profile of v11, /device:TPU:9, one launch (start us, length us, event | category | flops | bytes accessed | tf_op | source)
XLA Modules:
  0.0 87.1 jit_solution(5767574846397345797)
XLA Ops:
  0.6 0.0 copy-start
  0.6 2.9 %collective-permute-start.1 = (bf16[128,4096]{1,0:T(8,128)(2,1)}, bf16[128,4096]{1,0:T(8,128)(2,1)}, u32[]{:S(2)}, u32[]{:S(2)}) collective-permute-start(bf16[128,4096]{1,0:T(8,128)(2,1)} %bitcast.54), channel_id=1, source_target_pairs={{0,15},{1,14},{2,13},{3,12},{4,11},{5,10},{6,9},{7,8},{8,7},{9,6},... | collective-permute-start | bytes 3145736 | tf_op jit(solution)/shard_map/ppermute | solution.py:175
  3.5 0.8 slice_bitcast_fusion
  4.3 0.9 %compare_bitcast_fusion = (pred[127,1]{0,1:T(4,128)(4,1)S(1)}, pred[127,1]{0,1:T(4,128)(4,1)S(1)}) fusion(s32[1,2,128]{2,1,0:T(2,128)} %param.15), kind=kLoop, calls=%fused_computation.59 | loop fusion | flops 254 | bytes 2286 | tf_op jit(solution)/shard_map/concatenate | solution.py:18
  5.2 1.5 %fusion.3 = f32[128]{0:T(128)S(1)} fusion(bf16[1,128,4096]{2,1,0:T(8,128)(2,1)} %param.8), kind=kLoop, calls=%fused_computation.6 | loop fusion | flops 1572736 | bytes 1049088 | tf_op jit(solution)/shard_map/reduce_sum | solution.py:40
  6.7 0.1 fusion.32
  6.8 0.1 copy.14
  7.0 0.1 fusion.35
  7.0 0.1 copy.13
  7.1 0.0 copy-start.1
  7.2 0.0 copy-start.4
  7.2 0.2 reduce-window.16
  7.3 0.1 reduce
  7.5 0.1 copy.15
  7.6 0.2 reduce-window.17
  7.7 0.1 reduce.1
  7.9 0.0 copy-start.3
  7.9 2.6 %fusion.15 = f32[128,256]{1,0:T(8,128)S(1)} fusion(bf16[1,128,4096]{2,1,0:T(8,128)(2,1)} %param.8, f32[4096]{0:T(1024)} %bitcast.52, f32[128]{0:T(128)S(1)} %add_rsqrt_fusion, bf16[1,4096,256]{2,1,0:T(8,128)(2,1)} %param.13), kind=kOutput, calls=%fused_computation.18 | convolution fusion | flops 270532608 | bytes 3293696 | tf_op jit(solution)/shard_map/dot_general | solution.py:43
  10.4 0.0 copy-done.1
  10.5 0.0 copy-done.4
  10.5 0.0 copy-done.3
  10.5 0.5 fusion.17
  11.0 0.1 slice_negate_fusion
  11.1 0.5 multiply_sine_fusion
  11.6 0.1 pad_maximum_fusion.2
  11.7 0.1 pad_maximum_fusion.1
  11.8 0.1 fusion.20
  11.9 0.1 fusion.24
  12.0 0.3 fusion.44
  12.3 0.2 convolution_convert_fusion
  12.5 0.0 copy-done
  12.5 0.0 copy-start.2
  12.6 1.4 %fusion.1 = bf16[1,128,4096]{2,1,0:T(8,128)(2,1)} fusion(bf16[1,128,4096]{2,1,0:T(8,128)(2,1)S(1)} %copy-done.1, bf16[1,256,4096]{2,1,0:T(8,128)(2,1)S(1)} %copy-done, bf16[128,128]{0,1:T(8,128)(2,1)S(1)} %get-tuple-element.9, bf16[128,128]{0,1:T(8,128)(2,1)S(1)} %get-tuple-element.8), kind=kOutput, calls=%fused_computation.2 | convolution fusion | flops 270139392 | bytes 4259840 | tf_op jit(solution)/shard_map/dot_general | solution.py:64
  14.0 1.9 %collective-permute-start = (bf16[1,128,4096]{2,1,0:T(8,128)(2,1)}, bf16[1,128,4096]{2,1,0:T(8,128)(2,1)S(1)}, u32[]{:S(2)}, u32[]{:S(2)}) collective-permute-start(bf16[1,128,4096]{2,1,0:T(8,128)(2,1)} %fusion.1), channel_id=1, source_target_pairs={{0,1},{1,2},{2,3},{3,4},{4,5},{5,6},{6,7},{7,8},{8,9},{9,10},{10,1... | collective-permute-start | bytes 3145736 | tf_op jit(solution)/shard_map/ppermute | solution.py:13
  15.9 0.7 pad_maximum_fusion.4.sine_ref
  16.6 0.7 pad_maximum_fusion.3.cosine_ref
  17.3 0.7 fusion.33.allowed_ref
  18.0 0.0 copy-done.2
  18.0 1.5 %fusion.11.upstream_ref = bf16[128,256]{1,0:T(8,128)(2,1)} fusion(bf16[1,256,4096]{2,1,0:T(8,128)(2,1)S(1)} %copy-done, bf16[1,128,4096]{2,1,0:T(8,128)(2,1)S(1)} %copy-done.2), kind=kOutput, calls=%fused_computation.15 | convolution fusion | flops 268468224 | bytes 3211264 | tf_op jit(solution)/shard_map/dot_general | solution.py:161
  19.5 41.6 %collective-permute-done.1.acts_ref = bf16[128,4096]{1,0:T(8,128)(2,1)} collective-permute-done((bf16[128,4096]{1,0:T(8,128)(2,1)}, bf16[128,4096]{1,0:T(8,128)(2,1)}, u32[]{:S(2)}, u32[]{:S(2)}) %collective-permute-start.1) | collective-permute-done | bytes 1048608 | tf_op jit(solution)/shard_map/ppermute | solution.py:175
  61.1 7.7 %shard_map.95 = bf16[128,4096]{1,0:T(8,128)(2,1)} custom-call(bf16[128,4096]{1,0:T(8,128)(2,1)} %collective-permute-done.1.acts_ref, bf16[128,4096]{1,0:T(8,128)(2,1)} %bitcast.47, f32[1,4096]{1,0:T(1,128)} %gain_ref.1, bf16[4096,256]{1,0:T(8,128)(2,1)} %bitcast.48, bf16[4096,256]{1,0:T(8,128)(2,1)} %bitcast.49, f32[128,128]{1,0:T(8,128)} %pad_maximum_fusion.3.cosine_ref, ...), custom_call_target="tpu_custom_call" | custom-call | tf_op jit(solution)/shard_map/pallas_call | solution.py:164
  68.8 2.4 %collective-permute-start.2 = (bf16[1,128,4096]{2,1,0:T(8,128)(2,1)}, bf16[1,128,4096]{2,1,0:T(8,128)(2,1)S(1)}, u32[]{:S(2)}, u32[]{:S(2)}) collective-permute-start(bf16[1,128,4096]{2,1,0:T(8,128)(2,1)} %bitcast.50), channel_id=1, source_target_pairs={{1,0},{2,1},{3,2},{4,3},{5,4},{6,5},{7,6},{8,7},{9,8},{10,9},{11,1... | collective-permute-start | bytes 3145736 | tf_op jit(solution)/shard_map/ppermute | solution.py:13
  71.2 0.0 collective-permute-done
  71.2 13.9 %collective-permute-done.2 = bf16[1,128,4096]{2,1,0:T(8,128)(2,1)S(1)} collective-permute-done((bf16[1,128,4096]{2,1,0:T(8,128)(2,1)}, bf16[1,128,4096]{2,1,0:T(8,128)(2,1)S(1)}, u32[]{:S(2)}, u32[]{:S(2)}) %collective-permute-start.2) | collective-permute-done | bytes 1048608 | tf_op jit(solution)/shard_map/ppermute | solution.py:13
  85.2 1.0 %copy.19 = bf16[1,128,4096]{2,1,0:T(8,128)(2,1)} copy(bf16[1,128,4096]{2,1,0:T(8,128)(2,1)S(1)} %collective-permute-done) | data formatting | bytes 2097152
  86.1 1.0 %copy.20 = bf16[1,128,4096]{2,1,0:T(8,128)(2,1)} copy(bf16[1,128,4096]{2,1,0:T(8,128)(2,1)S(1)} %collective-permute-done.2) | data formatting | bytes 2097152
  (7 shorter events, 0.1 us)
Async XLA Ops:
  0.6 11.9 %copy-start = (bf16[1,256,4096]{2,1,0:T(8,128)(2,1)S(1)}, bf16[1,256,4096]{2,1,0:T(8,128)(2,1)}, u32[]{:S(2)}) copy-start(bf16[1,256,4096]{2,1,0:T(8,128)(2,1)} %param.14) | copy-start | bytes 6291460
  0.6 60.5 %collective-permute-start.1 = (bf16[128,4096]{1,0:T(8,128)(2,1)}, bf16[128,4096]{1,0:T(8,128)(2,1)}, u32[]{:S(2)}, u32[]{:S(2)}) collective-permute-start(bf16[128,4096]{1,0:T(8,128)(2,1)} %bitcast.54), channel_id=1, source_target_pairs={{0,15},{1,14},{2,13},{3,12},{4,11},{5,10},{6,9},{7,8},{8,7},{9,6},... | collective-permute-start | bytes 3145736 | tf_op jit(solution)/shard_map/ppermute | solution.py:175
  7.1 3.3 %copy-start.1 = (bf16[1,128,4096]{2,1,0:T(8,128)(2,1)S(1)}, bf16[1,128,4096]{2,1,0:T(8,128)(2,1)}, u32[]{:S(2)}) copy-start(bf16[1,128,4096]{2,1,0:T(8,128)(2,1)} %param.8) | copy-start | bytes 3145732
  7.2 3.3 %copy-start.4 = (f32[1,4096]{1,0:T(1,128)S(1)}, f32[1,4096]{1,0:T(1,128)}, u32[]{:S(2)}) copy-start(f32[1,4096]{1,0:T(1,128)} %gain_ref.1) | copy-start | bytes 49156
  7.9 2.6 %copy-start.3 = (bf16[1,4096,256]{2,1,0:T(8,128)(2,1)S(1)}, bf16[1,4096,256]{2,1,0:T(8,128)(2,1)}, u32[]{:S(2)}) copy-start(bf16[1,4096,256]{2,1,0:T(8,128)(2,1)} %param.12) | copy-start | bytes 6291460
  12.5 5.5 %copy-start.2 = (bf16[1,128,4096]{2,1,0:T(8,128)(2,1)S(1)}, bf16[1,128,4096]{2,1,0:T(8,128)(2,1)}, u32[]{:S(2)}) copy-start(bf16[1,128,4096]{2,1,0:T(8,128)(2,1)} %param.10) | copy-start | bytes 3145732
  14.0 57.2 %collective-permute-start = (bf16[1,128,4096]{2,1,0:T(8,128)(2,1)}, bf16[1,128,4096]{2,1,0:T(8,128)(2,1)S(1)}, u32[]{:S(2)}, u32[]{:S(2)}) collective-permute-start(bf16[1,128,4096]{2,1,0:T(8,128)(2,1)} %fusion.1), channel_id=1, source_target_pairs={{0,1},{1,2},{2,3},{3,4},{4,5},{5,6},{6,7},{7,8},{8,9},{9,10},{10,1... | collective-permute-start | bytes 3145736 | tf_op jit(solution)/shard_map/ppermute | solution.py:13
  68.8 16.3 %collective-permute-start.2 = (bf16[1,128,4096]{2,1,0:T(8,128)(2,1)}, bf16[1,128,4096]{2,1,0:T(8,128)(2,1)S(1)}, u32[]{:S(2)}, u32[]{:S(2)}) collective-permute-start(bf16[1,128,4096]{2,1,0:T(8,128)(2,1)} %bitcast.50), channel_id=1, source_target_pairs={{1,0},{2,1},{3,2},{4,3},{5,4},{6,5},{7,6},{8,7},{9,8},{10,9},{11,1... | collective-permute-start | bytes 3145736 | tf_op jit(solution)/shard_map/ppermute | solution.py:13

commit v12 on v11

--- a/solution.py
+++ b/solution.py
@@ -121,35 +121,31 @@
 
 
 def input_gradient_kernel(
-    acts_ref, cotangent_ref, gain_ref, wq_ref, wkv_ref, cosine_ref, sine_ref, allowed_ref,
+    acts_ref, cotangent_ref, gain_ref, weight_ref, cosine_ref, sine_ref, allowed_ref,
     upstream_ref, out_ref,
 ):
     values32 = acts_ref[...].astype(jnp.float32)
     gain = gain_ref[...]
     width = values32.shape[1]
+    split = upstream_ref.shape[1]
     scale = lax.rsqrt(jnp.sum(values32 * values32, axis=-1, keepdims=True) / width + 1e-05)
-    normed = (values32 * scale * gain).astype(jnp.bfloat16)
-    w_query = wq_ref[...]
-    w_kv = wkv_ref[...]
-    query = jnp.dot(normed, w_query, preferred_element_type=jnp.float32)
-    keyval = jnp.dot(normed, w_kv, preferred_element_type=jnp.float32)
+    weight = weight_ref[...]
+    projected = jnp.dot(
+        (values32 * (scale * gain)).astype(jnp.bfloat16), weight, preferred_element_type=jnp.float32
+    )
     dquery, dkeyval = attention_gradient_body(
-        query, keyval, cosine_ref[...], sine_ref[...], allowed_ref[...], upstream_ref[...]
+        projected[:, :split], projected[:, split:], cosine_ref[...], sine_ref[...],
+        allowed_ref[...], upstream_ref[...],
     )
-    contract = (((1,), (1,)), ((), ()))
-    from_query = lax.dot_general(
-        dquery.astype(jnp.bfloat16), w_query, contract, preferred_element_type=jnp.float32
-    ).astype(jnp.bfloat16)
-    from_keyval = lax.dot_general(
-        dkeyval.astype(jnp.bfloat16), w_kv, contract, preferred_element_type=jnp.float32
-    ).astype(jnp.bfloat16)
-    dnormed = (from_query.astype(jnp.float32) + from_keyval.astype(jnp.float32)).astype(
-        jnp.bfloat16
-    ).astype(jnp.float32)
+    both = jnp.concatenate([dquery, dkeyval], 1).astype(jnp.bfloat16)
+    dnormed = lax.dot_general(
+        both, weight, (((1,), (1,)), ((), ())), preferred_element_type=jnp.float32
+    ).astype(jnp.bfloat16).astype(jnp.float32)
     weighted = dnormed * gain
     spread = jnp.sum(weighted * values32, axis=-1, keepdims=True) * (scale * scale * scale) / width
-    dvalues32 = weighted * scale - values32 * spread
-    out_ref[...] = (cotangent_ref[...].astype(jnp.float32) + dvalues32).astype(out_ref.dtype)
+    out_ref[...] = (
+        cotangent_ref[...].astype(jnp.float32) + weighted * scale - values32 * spread
+    ).astype(out_ref.dtype)
 
 
 def input_gradient(acts, cotangent, gain, w_query, w_kv, w_out, segment):
@@ -164,7 +160,7 @@
     return pl.pallas_call(
         input_gradient_kernel, out_shape=jax.ShapeDtypeStruct(acts.shape, acts.dtype)
     )(
-        acts, cotangent, gain.reshape(1, -1), w_query, w_kv, cosine, sine_part,
+        acts, cotangent, gain.reshape(1, -1), jnp.concatenate([w_query, w_kv], 1), cosine, sine_part,
         allowed.astype(jnp.float32), dmixed,
     )
 

time: 87.3 us -> 99.5 us (1.14)
  the two profiles are of different devices: /device:TPU:9 before, /device:TPU:15 now
where the time goes in v12:
time: 99.5 us; the launch traced here: 99.2 us
  waiting for transfers between devices  67.1 us (67%)
  other arithmetic  8.53 us (9%)
  Pallas kernels  7.3 us (7%)
  matrix products  6.42 us (6%)
  starting transfers between devices  5.81 us (6%)
  local copies, waits for them, and re-layouts  3.22 us (3%)
    ppermute x1, waiting for transfers between devices, shards(): fetched = lax.ppermute(stash[0], 'section', mirror)  50.9 us
    ppermute x2, waiting for transfers between devices, shifted(): lax.ppermute(value, axis, [(source, source + steps) for source in range(l...  16.1 us
    pallas_call x1, Pallas kernels, input_gradient(): pl.pallas_call(input_gradient_kernel, out_shape=jax.ShapeDtypeStruct(acts...  7.3 us
    ppermute x2, starting transfers between devices, shifted(): lax.ppermute(value, axis, [(source, source + steps) for source in range(l...  5.73 us
    dot_general x1, matrix products, section_layer(): keyval = jnp.dot(normed, w_kv, preferred_element_type=jnp.float32)  2.56 us
    concatenate x1, other arithmetic, input_gradient(): jnp.concatenate([w_query, w_kv], 1)  2.27 us
    unnamed x16, local copies, waits for them, and re-layouts  2.01 us
  transfers between devices with their start and end apart: 3, of which 2 were waited for; matrix products, arithmetic and copies ran while one was open for 6% of the time, Pallas kernels for 7%

profile of v12, /device:TPU:15, one launch (start us, length us, event | category | flops | bytes accessed | tf_op | source)
XLA Modules:
  0.0 99.2 jit_solution(13450013228382748275)
XLA Ops:
  0.6 0.0 copy-start
  0.7 0.8 slice_bitcast_fusion
  1.5 0.9 compare_bitcast_fusion
  2.4 1.5 %fusion.3 = f32[128]{0:T(128)S(1)} fusion(bf16[1,128,4096]{2,1,0:T(8,128)(2,1)} %param.8), kind=kLoop, calls=%fused_computation.7 | loop fusion | flops 1572736 | bytes 1049088 | tf_op jit(solution)/shard_map/reduce_sum | solution.py:40
  3.9 0.1 fusion.32
  4.0 0.1 copy.14
  4.2 0.1 fusion.35
  4.2 0.1 copy.13
  4.4 0.0 copy-start.5
  4.4 0.2 reduce-window.16
  4.5 0.1 reduce
  4.7 0.1 copy.15
  4.8 0.2 reduce-window.17
  5.0 0.1 reduce.1
  5.1 0.0 copy-start.3
  5.1 2.6 %fusion.15 = f32[128,256]{1,0:T(8,128)S(1)} fusion(bf16[1,128,4096]{2,1,0:T(8,128)(2,1)} %param.8, f32[4096]{0:T(1024)} %bitcast.52, f32[128]{0:T(128)S(1)} %add_rsqrt_fusion, bf16[1,4096,256]{2,1,0:T(8,128)(2,1)} %param.13), kind=kOutput, calls=%fused_computation.19 | convolution fusion | flops 270532608 | bytes 3293696 | tf_op jit(solution)/shard_map/dot_general | solution.py:43
  7.7 0.0 copy-done.1
  7.7 0.0 copy-done.5
  7.7 0.0 copy-done.3
  7.7 0.5 fusion.17
  8.2 0.1 slice_negate_fusion
  8.3 0.5 multiply_sine_fusion
  8.8 0.1 pad_maximum_fusion.3
  8.9 0.1 pad_maximum_fusion.2
  9.0 0.1 fusion.20
  9.1 0.1 fusion.24
  9.2 0.3 fusion.44
  9.5 0.2 convolution_convert_fusion
  9.7 0.0 copy-done
  9.8 0.0 copy-start.6
  9.8 0.0 copy-start.2
  9.8 1.4 %fusion.1 = bf16[1,128,4096]{2,1,0:T(8,128)(2,1)} fusion(bf16[1,128,4096]{2,1,0:T(8,128)(2,1)S(1)} %copy-done.1, bf16[1,256,4096]{2,1,0:T(8,128)(2,1)S(1)} %copy-done, bf16[128,128]{0,1:T(8,128)(2,1)S(1)} %get-tuple-element.9, bf16[128,128]{0,1:T(8,128)(2,1)S(1)} %get-tuple-element.8), kind=kOutput, calls=%fused_computation.2 | convolution fusion | flops 270139392 | bytes 4259840 | tf_op jit(solution)/shard_map/dot_general | solution.py:64
  11.2 3.8 %collective-permute-start = (bf16[1,128,4096]{2,1,0:T(8,128)(2,1)}, bf16[1,128,4096]{2,1,0:T(8,128)(2,1)S(1)}, u32[]{:S(2)}, u32[]{:S(2)}) collective-permute-start(bf16[1,128,4096]{2,1,0:T(8,128)(2,1)} %fusion.1), channel_id=1, source_target_pairs={{0,1},{1,2},{2,3},{3,4},{4,5},{5,6},{6,7},{7,8},{8,9},{9,10},{10,1... | collective-permute-start | bytes 3145736 | tf_op jit(solution)/shard_map/ppermute | solution.py:13
  15.1 0.0 copy-done.6
  15.1 0.1 collective-permute-start.1
  15.1 0.7 pad_maximum_fusion.5.sine_ref
  15.9 0.7 pad_maximum_fusion.4.cosine_ref
  16.6 0.7 fusion.33.allowed_ref
  17.3 1.5 %fusion.11.upstream_ref = bf16[128,256]{1,0:T(8,128)(2,1)} fusion(bf16[1,256,4096]{2,1,0:T(8,128)(2,1)S(1)} %copy-done, bf16[1,128,4096]{2,1,0:T(8,128)(2,1)S(1)} %copy-done.2), kind=kOutput, calls=%fused_computation.16 | convolution fusion | flops 268468224 | bytes 3211264 | tf_op jit(solution)/shard_map/dot_general | solution.py:157
  18.7 0.0 copy-done.4
  18.7 2.3 %pad_maximum_fusion.weight_ref = bf16[4096,512]{1,0:T(8,128)(2,1)} fusion(bf16[4096,256]{1,0:T(8,128)(2,1)S(1)} %bitcast.49, bf16[4096,256]{1,0:T(8,128)(2,1)S(1)} %bitcast.48), kind=kLoop, calls=%fused_computation.3 | loop fusion | flops 8388608 | bytes 8388608 | tf_op jit(solution)/shard_map/concatenate | solution.py:163
  21.0 50.9 %collective-permute-done.1.acts_ref = bf16[128,4096]{1,0:T(8,128)(2,1)} collective-permute-done((bf16[128,4096]{1,0:T(8,128)(2,1)S(1)}, bf16[128,4096]{1,0:T(8,128)(2,1)}, u32[]{:S(2)}, u32[]{:S(2)}) %collective-permute-start.1) | collective-permute-done | bytes 1048608 | tf_op jit(solution)/shard_map/ppermute | solution.py:171
  71.9 7.3 %shard_map.95 = bf16[128,4096]{1,0:T(8,128)(2,1)} custom-call(bf16[128,4096]{1,0:T(8,128)(2,1)} %collective-permute-done.1.acts_ref, bf16[128,4096]{1,0:T(8,128)(2,1)} %bitcast.47, f32[1,4096]{1,0:T(1,128)} %gain_ref.1, bf16[4096,512]{1,0:T(8,128)(2,1)} %pad_maximum_fusion.weight_ref, f32[128,128]{1,0:T(8,128)} %pad_maximum_fusion.4.cosine_ref, ...), custom_call_target="tpu_custom_call" | custom-call | tf_op jit(solution)/shard_map/pallas_call | solution.py:160
  79.2 1.9 %collective-permute-start.2 = (bf16[1,128,4096]{2,1,0:T(8,128)(2,1)}, bf16[1,128,4096]{2,1,0:T(8,128)(2,1)S(1)}, u32[]{:S(2)}, u32[]{:S(2)}) collective-permute-start(bf16[1,128,4096]{2,1,0:T(8,128)(2,1)} %bitcast.50), channel_id=1, source_target_pairs={{1,0},{2,1},{3,2},{4,3},{5,4},{6,5},{7,6},{8,7},{9,8},{10,9},{11,1... | collective-permute-start | bytes 3145736 | tf_op jit(solution)/shard_map/ppermute | solution.py:13
  81.2 0.0 collective-permute-done
  81.2 16.1 %collective-permute-done.2 = bf16[1,128,4096]{2,1,0:T(8,128)(2,1)S(1)} collective-permute-done((bf16[1,128,4096]{2,1,0:T(8,128)(2,1)}, bf16[1,128,4096]{2,1,0:T(8,128)(2,1)S(1)}, u32[]{:S(2)}, u32[]{:S(2)}) %collective-permute-start.2) | collective-permute-done | bytes 1048608 | tf_op jit(solution)/shard_map/ppermute | solution.py:13
  97.3 1.0 copy.19
  98.3 1.0 copy.20
  (10 shorter events, 0.1 us)
Async XLA Ops:
  0.6 9.1 %copy-start = (bf16[1,256,4096]{2,1,0:T(8,128)(2,1)S(1)}, bf16[1,256,4096]{2,1,0:T(8,128)(2,1)}, u32[]{:S(2)}) copy-start(bf16[1,256,4096]{2,1,0:T(8,128)(2,1)} %param.14) | copy-start | bytes 6291460
  4.4 3.3 %copy-start.1 = (bf16[1,128,4096]{2,1,0:T(8,128)(2,1)S(1)}, bf16[1,128,4096]{2,1,0:T(8,128)(2,1)}, u32[]{:S(2)}) copy-start(bf16[1,128,4096]{2,1,0:T(8,128)(2,1)} %param.8) | copy-start | bytes 3145732
  4.4 3.3 %copy-start.5 = (f32[1,4096]{1,0:T(1,128)S(1)}, f32[1,4096]{1,0:T(1,128)}, u32[]{:S(2)}) copy-start(f32[1,4096]{1,0:T(1,128)} %gain_ref.1) | copy-start | bytes 49156
  5.1 2.6 %copy-start.3 = (bf16[1,4096,256]{2,1,0:T(8,128)(2,1)S(1)}, bf16[1,4096,256]{2,1,0:T(8,128)(2,1)}, u32[]{:S(2)}) copy-start(bf16[1,4096,256]{2,1,0:T(8,128)(2,1)} %param.12) | copy-start | bytes 6291460
  9.8 5.3 %copy-start.6 = (bf16[1,128,4096]{2,1,0:T(8,128)(2,1)S(1)}, bf16[1,128,4096]{2,1,0:T(8,128)(2,1)}, u32[]{:S(2)}) copy-start(bf16[1,128,4096]{2,1,0:T(8,128)(2,1)} %param.9) | copy-start | bytes 3145732
  9.8 7.5 %copy-start.2 = (bf16[1,128,4096]{2,1,0:T(8,128)(2,1)S(1)}, bf16[1,128,4096]{2,1,0:T(8,128)(2,1)}, u32[]{:S(2)}) copy-start(bf16[1,128,4096]{2,1,0:T(8,128)(2,1)} %param.10) | copy-start | bytes 3145732
  11.2 7.5 %copy-start.4 = (bf16[1,4096,256]{2,1,0:T(8,128)(2,1)S(1)}, bf16[1,4096,256]{2,1,0:T(8,128)(2,1)}, u32[]{:S(2)}) copy-start(bf16[1,4096,256]{2,1,0:T(8,128)(2,1)} %param.13) | copy-start | bytes 6291460
  11.2 69.9 %collective-permute-start = (bf16[1,128,4096]{2,1,0:T(8,128)(2,1)}, bf16[1,128,4096]{2,1,0:T(8,128)(2,1)S(1)}, u32[]{:S(2)}, u32[]{:S(2)}) collective-permute-start(bf16[1,128,4096]{2,1,0:T(8,128)(2,1)} %fusion.1), channel_id=1, source_target_pairs={{0,1},{1,2},{2,3},{3,4},{4,5},{5,6},{6,7},{7,8},{8,9},{9,10},{10,1... | collective-permute-start | bytes 3145736 | tf_op jit(solution)/shard_map/ppermute | solution.py:13
  15.1 56.9 %collective-permute-start.1 = (bf16[128,4096]{1,0:T(8,128)(2,1)S(1)}, bf16[128,4096]{1,0:T(8,128)(2,1)}, u32[]{:S(2)}, u32[]{:S(2)}) collective-permute-start(bf16[128,4096]{1,0:T(8,128)(2,1)S(1)} %bitcast.54), channel_id=1, source_target_pairs={{0,15},{1,14},{2,13},{3,12},{4,11},{5,10},{6,9},{7,8},{8,7},{9,6},... | collective-permute-start | bytes 3145736 | tf_op jit(solution)/shard_map/ppermute | solution.py:171
  79.2 18.1 %collective-permute-start.2 = (bf16[1,128,4096]{2,1,0:T(8,128)(2,1)}, bf16[1,128,4096]{2,1,0:T(8,128)(2,1)S(1)}, u32[]{:S(2)}, u32[]{:S(2)}) collective-permute-start(bf16[1,128,4096]{2,1,0:T(8,128)(2,1)} %bitcast.50), channel_id=1, source_target_pairs={{1,0},{2,1},{3,2},{4,3},{5,4},{6,5},{7,6},{8,7},{9,8},{10,9},{11,1... | collective-permute-start | bytes 3145736 | tf_op jit(solution)/shard_map/ppermute | solution.py:13

commit v13 on v7

--- a/solution.py
+++ b/solution.py
@@ -65,6 +65,63 @@
     )
 
 
+def attention_part(query, keyval, segment, head_dim):
+    rows = query.shape[0]
+    heads = query.shape[1] // head_dim
+    cosine, sine_part = rotary_tables(segment, head_dim)
+    keys = rotary(keyval[:, :head_dim], cosine, sine_part).astype(jnp.bfloat16)
+    values = keyval[:, head_dim:].astype(jnp.bfloat16)
+    index = jnp.arange(rows, dtype=jnp.int32)
+    allowed = (segment[:, None] == segment[None, :]) & (index[None, :] <= index[:, None])
+    stacked = jnp.concatenate(
+        [query[:, head * head_dim : (head + 1) * head_dim] for head in range(heads)], 0
+    )
+    stacked = rotary(
+        stacked, jnp.tile(cosine, (heads, 1)), jnp.tile(sine_part, (heads, 1))
+    ).astype(jnp.bfloat16)
+    scores = lax.dot_general(
+        stacked, keys, (((1,), (1,)), ((), ())), preferred_element_type=jnp.float32
+    ) / math.sqrt(head_dim)
+    expd = jnp.where(jnp.tile(allowed, (heads, 1)), jnp.exp(scores), jnp.zeros_like(scores))
+    probs = (expd / jnp.sum(expd, axis=-1, keepdims=True)).astype(jnp.bfloat16)
+    mixed = jnp.dot(probs, values, preferred_element_type=jnp.float32).astype(jnp.bfloat16)
+    return jnp.concatenate([mixed[head * rows : (head + 1) * rows] for head in range(heads)], -1)
+
+
+def gradient_halves(acts, cotangent, gain, w_query, w_kv, w_out, segment):
+    rows = acts.shape[0]
+    width = acts.shape[1]
+    head_dim = w_kv.shape[1] // 2
+    values32 = acts.astype(jnp.float32)
+    scale = lax.rsqrt(jnp.mean(values32 * values32, axis=-1, keepdims=True) + 1e-05)
+    normed = (values32 * scale * gain).astype(jnp.bfloat16)
+    query = jnp.dot(normed, w_query, preferred_element_type=jnp.float32)
+    keyval = jnp.dot(normed, w_kv, preferred_element_type=jnp.float32)
+    dmixed = lax.dot_general(
+        cotangent, w_out, (((1,), (1,)), ((), ())), preferred_element_type=jnp.float32
+    ).astype(jnp.bfloat16)
+    unused, pullback = jax.vjp(
+        lambda q, kv: attention_part(q, kv, segment, head_dim), query, keyval
+    )
+    dquery, dkeyval = pullback(dmixed)
+    contract = (((1,), (1,)), ((), ()))
+    halves = []
+    for low in (0, rows // 2):
+        part = slice(low, low + rows // 2)
+        from_query = lax.dot_general(
+            dquery[part], w_query, contract, preferred_element_type=jnp.bfloat16
+        )
+        from_keyval = lax.dot_general(
+            dkeyval[part], w_kv, contract, preferred_element_type=jnp.bfloat16
+        )
+        weighted = (from_query + from_keyval).astype(jnp.float32) * gain
+        own = values32[part]
+        spread = jnp.sum(weighted * own, axis=-1, keepdims=True) * scale[part] ** 3 / width
+        grad = weighted * scale[part] - own * spread
+        halves.append((cotangent[part].astype(jnp.float32) + grad).astype(jnp.bfloat16))
+    return halves
+
+
 def shards(section_input, stash, cotangent, norm_gain, w_query, w_kv, w_out, doc_ids):
     pieces = lax.axis_size("section")
     mirror = [(source, pieces - 1 - source) for source in range(pieces)]
@@ -72,14 +129,11 @@
     outward = section_layer(
         section_input[0], norm_gain[0], w_query[0], w_kv[0], w_out[0], doc_ids[0, 0]
     )
-
-    def replay(acts):
-        return section_layer(acts, norm_gain[0], w_query[0], w_kv[0], w_out[0], doc_ids[0, 1])
-
-    unused, pullback = jax.vjp(replay, fetched)
-    gradient = pullback(cotangent[0])[0]
+    halves = gradient_halves(
+        fetched, cotangent[0], norm_gain[0], w_query[0], w_kv[0], w_out[0], doc_ids[0, 1]
+    )
     forwarded = shifted(outward[None], "section", 1)
-    returned = shifted(gradient[None], "section", -1)
+    returned = jnp.concatenate([shifted(half[None], "section", -1) for half in halves], 1)
     return (forwarded, returned)
 
 

time: 86 us -> 87.8 us (1.021)
  starting transfers between devices: 7.16 us -> 9.08 us
  waiting for transfers between devices: 58.3 us -> 56.4 us
  matrix products: 8.56 us -> 9.89 us
  other arithmetic: 5.93 us -> 7.24 us
  local copies, waits for them, and re-layouts: 4.76 us -> 3.86 us
    dot_general x0 -> x12, matrix products: none -> 5.93 us  [the longest x2 1.67 us: gradient_halves(): lax.dot_general(dkeyval[part], w_kv, contract, preferred_element_type=jnp...]
    ppermute x2 -> x3, waiting for transfers between devices: 13.7 us -> 11.8 us  [shifted(): lax.ppermute(value, axis, [(source, source + steps) for source in range(l...]
    ppermute x2 -> x3, starting transfers between devices: 4.28 us -> 6.2 us  [shifted(): lax.ppermute(value, axis, [(source, source + steps) for source in range(l...]
    dot_general x3 -> x1, matrix products: 2.01 us -> 0.52 us  [section_layer(): keyval = jnp.dot(normed, w_kv, preferred_element_type=jnp.float32)]
    dot_general x3 -> x1, matrix products: 3.83 us -> 2.5 us  [section_layer(): query = jnp.dot(normed, w_query, preferred_element_type=jnp.float32)]
    concatenate x0 -> x1, other arithmetic: none -> 1.06 us  [shards(): jnp.concatenate([shifted(half[None], 'section', -1) for half in halves], 1)]
    unnamed x14 -> x13, local copies, waits for them, and re-layouts: 3.49 us -> 2.52 us
    reduce_sum x2 -> x1, other arithmetic: 1.81 us -> 1.52 us  [section_layer(): jnp.mean(values32 * values32, axis=-1, keepdims=True) + 1e-05]
  transfers between devices with their start and end apart: 3 -> 4, of which waited for: 2 -> 3; matrix products, arithmetic and copies ran while one was open for 18% -> 20% of each run, Pallas kernels for 0% -> 0%
where the time goes in v13:
time: 87.8 us; the launch traced here: 87.5 us
  waiting for transfers between devices  56.4 us (64%)
  matrix products  9.89 us (11%)
  starting transfers between devices  9.08 us (10%)
  other arithmetic  7.24 us (8%)
  local copies, waits for them, and re-layouts  3.86 us (4%)
  between operations  1.05 us (1%)
    ppermute x1, waiting for transfers between devices, shards(): fetched = lax.ppermute(stash[0], 'section', mirror)  44.6 us
    ppermute x3, waiting for transfers between devices, shifted(): lax.ppermute(value, axis, [(source, source + steps) for source in range(l...  11.8 us
    ppermute x3, starting transfers between devices, shifted(): lax.ppermute(value, axis, [(source, source + steps) for source in range(l...  6.2 us
    ppermute x1, starting transfers between devices, shards(): fetched = lax.ppermute(stash[0], 'section', mirror)  2.88 us
    unnamed x13, local copies, waits for them, and re-layouts  2.52 us
    dot_general x1, matrix products, section_layer(): query = jnp.dot(normed, w_query, preferred_element_type=jnp.float32)  2.5 us
  transfers between devices with their start and end apart: 4, of which 3 were waited for; matrix products, arithmetic and copies ran while one was open for 20% of the time, Pallas kernels for 0%

profile of v13, /device:TPU:9, one launch (start us, length us, event | category | flops | bytes accessed | tf_op | source)
XLA Modules:
  0.0 87.5 jit_solution(2814946522638615559)
XLA Ops:
  0.6 2.9 %collective-permute-start.1 = (bf16[128,4096]{1,0:T(8,128)(2,1)}, bf16[128,4096]{1,0:T(8,128)(2,1)S(1)}, u32[]{:S(2)}, u32[]{:S(2)}) collective-permute-start(bf16[128,4096]{1,0:T(8,128)(2,1)} %bitcast.119), channel_id=1, source_target_pairs={{0,15},{1,14},{2,13},{3,12},{4,11},{5,10},{6,9},{7,8},{8,7},{9,6},... | collective-permute-start | bytes 3145736 | tf_op jit(solution)/shard_map/ppermute | solution.py:128
  3.5 0.9 %compare_bitcast_fusion = (pred[127,1]{0,1:T(4,128)(4,1)S(1)}, pred[127,1]{0,1:T(4,128)(4,1)S(1)}) fusion(s32[1,2,128]{2,1,0:T(2,128)} %param.15), kind=kLoop, calls=%fused_computation.137 | loop fusion | flops 254 | bytes 2286 | tf_op jit(solution)/shard_map/jvp()/concatenate | solution.py:17
  4.4 0.8 slice_bitcast_fusion
  5.3 0.1 copy.14
  5.4 0.2 reduce-window.17
  5.6 0.1 reduce.1
  5.7 0.1 copy.12
  5.8 0.2 reduce-window.16
  6.0 0.1 reduce
  6.1 1.5 %fusion.7 = f32[128]{0:T(128)S(1)} fusion(bf16[1,128,4096]{2,1,0:T(8,128)(2,1)} %param.8), kind=kLoop, calls=%fused_computation.12 | loop fusion | flops 1572736 | bytes 1049088 | tf_op jit(solution)/shard_map/reduce_sum | solution.py:39
  7.6 2.5 %fusion.25 = f32[128,256]{1,0:T(8,128)S(1)} fusion(bf16[1,4096,256]{2,1,0:T(8,128)(2,1)} %param.12, bf16[1,128,4096]{2,1,0:T(8,128)(2,1)} %param.8, f32[4096]{0:T(1024)} %bitcast.113, f32[128]{0:T(128)S(1)} %add_rsqrt_fusion.1), kind=kOutput, calls=%fused_computation.30 | convolution fusion | flops 270532608 | bytes 3293696 | tf_op jit(solution)/shard_map/dot_general | solution.py:41
  10.2 0.5 multiply_cosine_fusion
  10.9 0.5 fusion.17
  11.7 0.1 copy.13
  11.9 0.1 fusion.52
  12.0 0.3 fusion.95
  12.3 0.2 convolution_convert_fusion.1
  12.5 0.5 copy-done.1
  13.0 0.5 fusion.1
  13.5 1.9 %collective-permute-start = (bf16[1,128,4096]{2,1,0:T(8,128)(2,1)S(1)}, bf16[1,128,4096]{2,1,0:T(8,128)(2,1)S(1)}, u32[]{:S(2)}, u32[]{:S(2)}) collective-permute-start(bf16[1,128,4096]{2,1,0:T(8,128)(2,1)S(1)} %fusion.1), channel_id=1, source_target_pairs={{0,1},{1,2},{2,3},{3,4},{4,5},{5,6},{6,7},{7,8},{8,9},{9,10},{10,1... | collective-permute-start | bytes 3145736 | tf_op jit(solution)/shard_map/ppermute | solution.py:12
  15.5 0.1 copy.16
  15.6 0.8 fusion.30
  16.4 44.6 %collective-permute-done.1 = bf16[128,4096]{1,0:T(8,128)(2,1)S(1)} collective-permute-done((bf16[128,4096]{1,0:T(8,128)(2,1)}, bf16[128,4096]{1,0:T(8,128)(2,1)S(1)}, u32[]{:S(2)}, u32[]{:S(2)}) %collective-permute-start.1) | collective-permute-done | bytes 1048608 | tf_op jit(solution)/shard_map/ppermute | solution.py:128
  61.0 0.3 multiply_reduce_fusion
  61.3 0.5 fusion.15
  61.9 1.0 %copy-done.2 = bf16[1,4096,256]{2,1,0:T(8,128)(2,1)S(1)} copy-done((bf16[1,4096,256]{2,1,0:T(8,128)(2,1)S(1)}, bf16[1,4096,256]{2,1,0:T(8,128)(2,1)}, u32[]{:S(2)}) %copy-start.2) | copy-done | bytes 2097176
  62.9 0.5 fusion.23
  63.5 0.1 pad_maximum_fusion.5
  63.7 0.1 fusion.54
  63.8 0.2 fusion.71
  64.0 0.2 convolution_convert_fusion.4
  64.1 0.2 multiply_reduce_fusion.3
  64.3 0.2 bitcast_multiply_fusion
  64.6 0.2 fusion.86
  64.8 0.1 fusion.56
  65.0 0.8 fusion.21
  65.7 0.8 fusion.19
  66.6 0.1 pad_add_fusion.3
  66.8 0.8 fusion.3
  67.6 0.2 convert_element_type.127
  67.8 0.9 %multiply_reduce_fusion.2 = (f32[64]{0:T(128)S(1)}, f32[64]{0:T(128)S(1)}, f32[64,4096]{1,0:T(8,128)S(1)}) fusion(f32[128,4096]{1,0:T(8,128)S(1)} %convert_element_type.127, f32[64,4096]{1,0:T(8,128)S(1)} %fusion.3, f32[4096]{0:T(1024)S(1)} %bitcast.118, bf16[64,4096]{1,0:T(8,128)(2,1)S(1)} %fusion.21, bf16[1,4096,256]{2,1,0:T(8,128)(2,1)S(1)} %copy-done, ...), kind=kOutput, calls=%fused_computation.56 | convolution fusion | flops 136052608 | bytes 6865408 | tf_op jit(solution)/shard_map/dot_general | solution.py:114
  68.7 0.6 fusion.40
  69.4 2.4 %collective-permute-start.2 = (bf16[1,64,4096]{2,1,0:T(8,128)(2,1)S(1)}, bf16[1,64,4096]{2,1,0:T(8,128)(2,1)S(1)}, u32[]{:S(2)}, u32[]{:S(2)}) collective-permute-start(bf16[1,64,4096]{2,1,0:T(8,128)(2,1)S(1)} %get-tuple-element.4), channel_id=1, source_target_pairs={{1,0},{2,1},{3,2},{4,3},{5,4},{6,5},{7,6},{8,7},{9,8},{10,9},{11,1... | collective-permute-start | bytes 1572872 | tf_op jit(solution)/shard_map/ppermute | solution.py:12
  71.7 1.9 %collective-permute-start.3 = (bf16[1,64,4096]{2,1,0:T(8,128)(2,1)S(1)}, bf16[1,64,4096]{2,1,0:T(8,128)(2,1)S(1)}, u32[]{:S(2)}, u32[]{:S(2)}) collective-permute-start(bf16[1,64,4096]{2,1,0:T(8,128)(2,1)S(1)} %get-tuple-element.5), channel_id=1, source_target_pairs={{1,0},{2,1},{3,2},{4,3},{5,4},{6,5},{7,6},{8,7},{9,8},{10,9},{11,1... | collective-permute-start | bytes 1572872 | tf_op jit(solution)/shard_map/ppermute | solution.py:12
  73.7 6.2 %collective-permute-done.2 = bf16[1,64,4096]{2,1,0:T(8,128)(2,1)S(1)} collective-permute-done((bf16[1,64,4096]{2,1,0:T(8,128)(2,1)S(1)}, bf16[1,64,4096]{2,1,0:T(8,128)(2,1)S(1)}, u32[]{:S(2)}, u32[]{:S(2)}) %collective-permute-start.2) | collective-permute-done | bytes 524320 | tf_op jit(solution)/shard_map/ppermute | solution.py:12
  79.9 5.6 %collective-permute-done.3 = bf16[1,64,4096]{2,1,0:T(8,128)(2,1)S(1)} collective-permute-done((bf16[1,64,4096]{2,1,0:T(8,128)(2,1)S(1)}, bf16[1,64,4096]{2,1,0:T(8,128)(2,1)S(1)}, u32[]{:S(2)}, u32[]{:S(2)}) %collective-permute-start.3) | collective-permute-done | bytes 524320 | tf_op jit(solution)/shard_map/ppermute | solution.py:12
  85.5 1.1 %pad_maximum_fusion = bf16[1,128,4096]{2,1,0:T(8,128)(2,1)} fusion(bf16[1,64,4096]{2,1,0:T(8,128)(2,1)S(1)} %collective-permute-done.3, bf16[1,64,4096]{2,1,0:T(8,128)(2,1)S(1)} %collective-permute-done.2), kind=kLoop, calls=%fused_computation.49 | loop fusion | flops 2097152 | bytes 2097152 | tf_op jit(solution)/shard_map/concatenate | solution.py:136
  86.5 1.0 %copy.24 = bf16[1,128,4096]{2,1,0:T(8,128)(2,1)} copy(bf16[1,128,4096]{2,1,0:T(8,128)(2,1)S(1)} %collective-permute-done) | data formatting | bytes 2097152
  (38 shorter events, 1.2 us)
Async XLA Ops:
  0.6 10.3 %copy-start = (bf16[1,4096,256]{2,1,0:T(8,128)(2,1)S(1)}, bf16[1,4096,256]{2,1,0:T(8,128)(2,1)}, u32[]{:S(2)}) copy-start(bf16[1,4096,256]{2,1,0:T(8,128)(2,1)} %param.13) | copy-start | bytes 6291460
  0.6 60.4 %collective-permute-start.1 = (bf16[128,4096]{1,0:T(8,128)(2,1)}, bf16[128,4096]{1,0:T(8,128)(2,1)S(1)}, u32[]{:S(2)}, u32[]{:S(2)}) collective-permute-start(bf16[128,4096]{1,0:T(8,128)(2,1)} %bitcast.119), channel_id=1, source_target_pairs={{0,15},{1,14},{2,13},{3,12},{4,11},{5,10},{6,9},{7,8},{8,7},{9,6},... | collective-permute-start | bytes 3145736 | tf_op jit(solution)/shard_map/ppermute | solution.py:128
  7.6 3.3 %copy-start.4 = (bf16[1,128,4096]{2,1,0:T(8,128)(2,1)S(1)}, bf16[1,128,4096]{2,1,0:T(8,128)(2,1)}, u32[]{:S(2)}) copy-start(bf16[1,128,4096]{2,1,0:T(8,128)(2,1)} %param.8) | copy-start | bytes 3145732
  7.6 3.3 %copy-start.5 = (f32[1,4096]{1,0:T(1,128)S(1)}, f32[1,4096]{1,0:T(1,128)}, u32[]{:S(2)}) copy-start(f32[1,4096]{1,0:T(1,128)} %param.11) | copy-start | bytes 49156
  11.4 1.6 %copy-start.1 = (bf16[1,256,4096]{2,1,0:T(8,128)(2,1)S(1)}, bf16[1,256,4096]{2,1,0:T(8,128)(2,1)}, u32[]{:S(2)}) copy-start(bf16[1,256,4096]{2,1,0:T(8,128)(2,1)} %param.14) | copy-start | bytes 6291460
  13.0 2.5 %copy-start.3 = (bf16[1,128,4096]{2,1,0:T(8,128)(2,1)S(1)}, bf16[1,128,4096]{2,1,0:T(8,128)(2,1)}, u32[]{:S(2)}) copy-start(bf16[1,128,4096]{2,1,0:T(8,128)(2,1)} %param.10) | copy-start | bytes 3145732
  13.5 60.1 %collective-permute-start = (bf16[1,128,4096]{2,1,0:T(8,128)(2,1)S(1)}, bf16[1,128,4096]{2,1,0:T(8,128)(2,1)S(1)}, u32[]{:S(2)}, u32[]{:S(2)}) collective-permute-start(bf16[1,128,4096]{2,1,0:T(8,128)(2,1)S(1)} %fusion.1), channel_id=1, source_target_pairs={{0,1},{1,2},{2,3},{3,4},{4,5},{5,6},{6,7},{7,8},{8,9},{9,10},{10,1... | collective-permute-start | bytes 3145736 | tf_op jit(solution)/shard_map/ppermute | solution.py:12
  61.3 1.6 %copy-start.2 = (bf16[1,4096,256]{2,1,0:T(8,128)(2,1)S(1)}, bf16[1,4096,256]{2,1,0:T(8,128)(2,1)}, u32[]{:S(2)}) copy-start(bf16[1,4096,256]{2,1,0:T(8,128)(2,1)} %param.12) | copy-start | bytes 6291460
  69.4 10.5 %collective-permute-start.2 = (bf16[1,64,4096]{2,1,0:T(8,128)(2,1)S(1)}, bf16[1,64,4096]{2,1,0:T(8,128)(2,1)S(1)}, u32[]{:S(2)}, u32[]{:S(2)}) collective-permute-start(bf16[1,64,4096]{2,1,0:T(8,128)(2,1)S(1)} %get-tuple-element.4), channel_id=1, source_target_pairs={{1,0},{2,1},{3,2},{4,3},{5,4},{6,5},{7,6},{8,7},{9,8},{10,9},{11,1... | collective-permute-start | bytes 1572872 | tf_op jit(solution)/shard_map/ppermute | solution.py:12
  71.7 13.7 %collective-permute-start.3 = (bf16[1,64,4096]{2,1,0:T(8,128)(2,1)S(1)}, bf16[1,64,4096]{2,1,0:T(8,128)(2,1)S(1)}, u32[]{:S(2)}, u32[]{:S(2)}) collective-permute-start(bf16[1,64,4096]{2,1,0:T(8,128)(2,1)S(1)} %get-tuple-element.5), channel_id=1, source_target_pairs={{1,0},{2,1},{3,2},{4,3},{5,4},{6,5},{7,6},{8,7},{9,8},{10,9},{11,1... | collective-permute-start | bytes 1572872 | tf_op jit(solution)/shard_map/ppermute | solution.py:12

commit v14 on v8

--- a/solution.py
+++ b/solution.py
@@ -69,15 +69,14 @@
     if pieces < 16:
         return shifted(value, "section", 1)
     first = [(source, source + 1) for source in range(pieces - 1) if source not in (5, 11, 14)]
-    first += [(5, 0), (11, 15)]
-    second = [(0, 6), (15, 12), (14, 15)]
+    first += [(11, 15)]
+    second = [(5, 6), (15, 12), (14, 15)]
     where = lax.axis_index("section")
     landed = lax.ppermute(value, "section", first)
-    onward = jnp.where((where == 0) | (where == 15), landed, value)
-    relayed = lax.ppermute(onward, "section", second)
-    late = (where == 6) | (where == 12) | (where == 15)
-    landed = jnp.where(where == 0, jnp.zeros_like(landed), landed)
-    return jnp.where(late, relayed, landed)
+    onward = jnp.where(where == 15, landed, value)
+    late = lax.ppermute(onward, "section", second)
+    tail = (where == 6) | (where == 12) | (where == 15)
+    return jnp.where(tail, late, landed)
 
 
 def shards(section_input, stash, cotangent, norm_gain, w_query, w_kv, w_out, doc_ids):

time: 94.9 us -> 93.2 us (0.982)
  the two profiles are of different devices: /device:TPU:14 before, /device:TPU:9 now
where the time goes in v14:
time: 93.2 us; the launch traced here: 92.1 us
  waiting for transfers between devices  53.4 us (57%)
  other arithmetic  11.5 us (12%)
  matrix products  11.4 us (12%)
  starting transfers between devices  10.7 us (11%)
  local copies, waits for them, and re-layouts  3.99 us (4%)
  between operations  1.03 us (1%)
    ppermute x1, waiting for transfers between devices, shards(): fetched = lax.ppermute(stash[0], 'section', mirror)  42.3 us
    ppermute x1, waiting for transfers between devices, shifted(): lax.ppermute(value, axis, [(source, source + steps) for source in range(l...  7.42 us
    ppermute x1, starting transfers between devices, relay_forward(): late = lax.ppermute(onward, 'section', second)  4.21 us
    dot_general x2, matrix products, section_layer(): jnp.dot(mixed, w_out, preferred_element_type=jnp.float32)  4.2 us
    dot_general x3, matrix products, section_layer(): query = jnp.dot(normed, w_query, preferred_element_type=jnp.float32)  3.83 us
    ppermute x1, waiting for transfers between devices, relay_forward(): late = lax.ppermute(onward, 'section', second)  3.61 us
    ppermute x1, starting transfers between devices, shards(): fetched = lax.ppermute(stash[0], 'section', mirror)  2.88 us
    unnamed x13, local copies, waits for them, and re-layouts  2.72 us
  transfers between devices with their start and end apart: 4, of which 3 were waited for; matrix products, arithmetic and copies ran while one was open for 24% of the time, Pallas kernels for 0%

profile of v14, /device:TPU:9, one launch (start us, length us, event | category | flops | bytes accessed | tf_op | source)
XLA Modules:
  0.0 92.1 jit_solution(7694784991929805808)
XLA Ops:
  0.6 2.9 %collective-permute-start.2 = (bf16[128,4096]{1,0:T(8,128)(2,1)}, bf16[128,4096]{1,0:T(8,128)(2,1)S(1)}, u32[]{:S(2)}, u32[]{:S(2)}) collective-permute-start(bf16[128,4096]{1,0:T(8,128)(2,1)} %bitcast.87), channel_id=1, source_target_pairs={{0,15},{1,14},{2,13},{3,12},{4,11},{5,10},{6,9},{7,8},{8,7},{9,6},... | collective-permute-start | bytes 3145736 | tf_op jit(solution)/shard_map/ppermute | solution.py:85
  3.5 0.9 compare_bitcast_fusion
  4.4 0.8 slice_bitcast_fusion
  5.3 0.1 copy.16
  5.4 0.2 reduce-window.17
  5.6 0.1 reduce.1
  5.7 0.1 copy.14
  5.8 0.2 reduce-window.16
  6.0 0.1 reduce
  6.1 1.5 %fusion.6 = f32[128]{0:T(128)S(1)} fusion(bf16[1,128,4096]{2,1,0:T(8,128)(2,1)} %param.8), kind=kLoop, calls=%fused_computation.16 | loop fusion | flops 1572736 | bytes 1049088 | tf_op jit(solution)/shard_map/reduce_sum | solution.py:39
  7.6 2.5 %fusion.25 = f32[128,256]{1,0:T(8,128)S(1)} fusion(bf16[1,4096,256]{2,1,0:T(8,128)(2,1)} %param.12, bf16[1,128,4096]{2,1,0:T(8,128)(2,1)} %param.8, f32[4096]{0:T(1024)} %bitcast.82, f32[128]{0:T(128)S(1)} %add_rsqrt_fusion), kind=kOutput, calls=%fused_computation.35 | convolution fusion | flops 270532608 | bytes 3293696 | tf_op jit(solution)/shard_map/dot_general | solution.py:41
  10.2 0.5 multiply_cosine_fusion
  10.9 0.5 fusion.20
  11.5 0.1 fusion.73
  11.7 0.1 copy.15
  11.9 0.1 fusion.51
  12.0 0.3 fusion.95
  12.3 0.2 convolution_convert_fusion.3
  12.5 0.5 copy-done.1
  13.0 1.4 %fusion.4 = bf16[1,128,4096]{2,1,0:T(8,128)(2,1)} fusion(bf16[1,128,4096]{2,1,0:T(8,128)(2,1)S(1)} %copy-done.3, bf16[1,256,4096]{2,1,0:T(8,128)(2,1)S(1)} %copy-done.1, bf16[128,128]{0,1:T(8,128)(2,1)S(1)} %get-tuple-element.26, bf16[128,128]{0,1:T(8,128)(2,1)S(1)} %get-tuple-element.25), kind=kOutput, calls=%fused_computation.7 | convolution fusion | flops 270139392 | bytes 4259840 | tf_op jit(solution)/shard_map/dot_general | solution.py:63
  14.5 1.3 %collective-permute-start = (bf16[1,128,4096]{2,1,0:T(8,128)(2,1)}, bf16[1,128,4096]{2,1,0:T(8,128)(2,1)}, u32[]{:S(2)}, u32[]{:S(2)}) collective-permute-start(bf16[1,128,4096]{2,1,0:T(8,128)(2,1)} %fusion.4), channel_id=1, source_target_pairs={{0,1},{1,2},{2,3},{3,4},{4,5},{6,7},{7,8},{8,9},{9,10},{10,11},{12... | collective-permute-start | bytes 3145736 | tf_op jit(solution)/shard_map/ppermute | solution.py:75
  15.8 0.1 copy.17
  15.9 2.8 %fusion.30 = bf16[128,256]{1,0:T(8,128)(2,1)S(1)} fusion(bf16[1,256,4096]{2,1,0:T(8,128)(2,1)} %param.14, bf16[1,128,4096]{2,1,0:T(8,128)(2,1)} %param.10), kind=kOutput, calls=%fused_computation.42 | convolution fusion | flops 268468224 | bytes 3211264 | tf_op jit(solution)/shard_map/transpose(jvp())/dot_general | solution.py:63
  18.7 42.3 %collective-permute-done.2 = bf16[128,4096]{1,0:T(8,128)(2,1)S(1)} collective-permute-done((bf16[128,4096]{1,0:T(8,128)(2,1)}, bf16[128,4096]{1,0:T(8,128)(2,1)S(1)}, u32[]{:S(2)}, u32[]{:S(2)}) %collective-permute-start.2) | collective-permute-done | bytes 1048608 | tf_op jit(solution)/shard_map/ppermute | solution.py:85
  61.0 0.3 fusion.10
  61.3 0.5 fusion.18
  61.9 1.0 %copy-done.4 = bf16[1,4096,256]{2,1,0:T(8,128)(2,1)S(1)} copy-done((bf16[1,4096,256]{2,1,0:T(8,128)(2,1)S(1)}, bf16[1,4096,256]{2,1,0:T(8,128)(2,1)}, u32[]{:S(2)}) %copy-start.4) | copy-done | bytes 2097176
  62.9 0.5 fusion.23
  63.6 0.1 pad_maximum_fusion.4
  63.7 0.1 fusion.53
  63.8 0.2 fusion.72
  64.0 0.2 convolution_convert_fusion.6
  64.2 0.2 multiply_reduce_fusion
  64.4 0.2 fusion.87
  64.5 0.2 bitcast_multiply_fusion
  64.8 0.1 fusion.89
  65.0 0.1 fusion.55
  65.1 0.8 convolution_convert_fusion
  66.0 1.0 %fusion.13 = (f32[128]{0:T(128)S(1)}, f32[128,4096]{1,0:T(8,128)S(1)}) fusion(bf16[128,4096]{1,0:T(8,128)(2,1)S(1)} %collective-permute-done.2, f32[4096]{0:T(1024)S(1)} %bitcast.86, bf16[128,4096]{1,0:T(8,128)(2,1)S(1)} %convolution_convert_fusion, bf16[1,4096,256]{2,1,0:T(8,128)(2,1)S(1)} %copy-done, f32[128,128]{1,0:T(8,128)S(1)} %pad_add_fusion, ...), kind=kOutput, calls=%fused_computation.23 | convolution fusion | flops 272170880 | bytes 6406656 | tf_op jit(solution)/shard_map/transpose(jvp())/dot_general | solution.py:42
  67.0 0.2 copy-done.2
  67.2 1.6 %fusion.36 = bf16[1,128,4096]{2,1,0:T(8,128)(2,1)} fusion(bf16[128,4096]{1,0:T(8,128)(2,1)S(1)} %collective-permute-done.2, f32[128,4096]{1,0:T(8,128)S(1)} %get-tuple-element.48, bf16[1,128,4096]{2,1,0:T(8,128)(2,1)S(1)} %copy-done.2, f32[128]{0:T(128)S(1)} %multiply_multiply_fusion.1, f32[128]{0:T(128)S(1)} %fusion.78), kind=kLoop, calls=%fused_computation.51 | loop fusion | flops 4194304 | bytes 5243904 | tf_op jit(solution)/shard_map/broadcast_in_dim | solution.py:96
  68.9 2.4 %collective-permute-start.3 = (bf16[1,128,4096]{2,1,0:T(8,128)(2,1)}, bf16[1,128,4096]{2,1,0:T(8,128)(2,1)S(1)}, u32[]{:S(2)}, u32[]{:S(2)}) collective-permute-start(bf16[1,128,4096]{2,1,0:T(8,128)(2,1)} %fusion.36), channel_id=1, source_target_pairs={{1,0},{2,1},{3,2},{4,3},{5,4},{6,5},{7,6},{8,7},{9,8},{10,9},{11,1... | collective-permute-start | bytes 3145736 | tf_op jit(solution)/shard_map/ppermute | solution.py:12
  71.2 2.3 %broadcast_select_fusion = bf16[1,128,4096]{2,1,0:T(8,128)(2,1)} fusion(bf16[1,128,4096]{2,1,0:T(8,128)(2,1)} %collective-permute-done, bf16[1,128,4096]{2,1,0:T(8,128)(2,1)} %fusion.4, pred[]{:T(512)S(6)} %eq.50), kind=kLoop, calls=%fused_computation.54 | loop fusion | flops 524288 | bytes 3145729 | tf_op jit(solution)/shard_map/jit(_where)/select_n | solution.py:76
  73.5 4.2 %collective-permute-start.1 = (bf16[1,128,4096]{2,1,0:T(8,128)(2,1)}, bf16[1,128,4096]{2,1,0:T(8,128)(2,1)}, u32[]{:S(2)}, u32[]{:S(2)}) collective-permute-start(bf16[1,128,4096]{2,1,0:T(8,128)(2,1)} %broadcast_select_fusion), channel_id=1, source_target_pairs={{5,6},{15,12},{14,15},{21,22},{31,28},{30,31}} | collective-permute-start | bytes 3145736 | tf_op jit(solution)/shard_map/ppermute | solution.py:77
  77.7 7.4 %collective-permute-done.3 = bf16[1,128,4096]{2,1,0:T(8,128)(2,1)S(1)} collective-permute-done((bf16[1,128,4096]{2,1,0:T(8,128)(2,1)}, bf16[1,128,4096]{2,1,0:T(8,128)(2,1)S(1)}, u32[]{:S(2)}, u32[]{:S(2)}) %collective-permute-start.3) | collective-permute-done | bytes 1048608 | tf_op jit(solution)/shard_map/ppermute | solution.py:12
  85.2 3.6 %collective-permute-done.1 = bf16[1,128,4096]{2,1,0:T(8,128)(2,1)} collective-permute-done((bf16[1,128,4096]{2,1,0:T(8,128)(2,1)}, bf16[1,128,4096]{2,1,0:T(8,128)(2,1)}, u32[]{:S(2)}, u32[]{:S(2)}) %collective-permute-start.1) | collective-permute-done | bytes 1048608 | tf_op jit(solution)/shard_map/ppermute | solution.py:77
  88.8 2.3 %broadcast_select_fusion.1 = bf16[1,128,4096]{2,1,0:T(8,128)(2,1)} fusion(bf16[1,128,4096]{2,1,0:T(8,128)(2,1)} %collective-permute-done.1, bf16[1,128,4096]{2,1,0:T(8,128)(2,1)} %collective-permute-done, pred[]{:T(512)S(6)} %or.7), kind=kLoop, calls=%fused_computation.55 | loop fusion | flops 524288 | bytes 3145729 | tf_op jit(solution)/shard_map/jit(_where)/select_n | solution.py:79
  91.1 1.0 %copy.30 = bf16[1,128,4096]{2,1,0:T(8,128)(2,1)} copy(bf16[1,128,4096]{2,1,0:T(8,128)(2,1)S(1)} %collective-permute-done.3) | data formatting | bytes 2097152
  (34 shorter events, 0.9 us)
Async XLA Ops:
  0.6 10.3 %copy-start = (bf16[1,4096,256]{2,1,0:T(8,128)(2,1)S(1)}, bf16[1,4096,256]{2,1,0:T(8,128)(2,1)}, u32[]{:S(2)}) copy-start(bf16[1,4096,256]{2,1,0:T(8,128)(2,1)} %param.13) | copy-start | bytes 6291460
  0.6 60.4 %collective-permute-start.2 = (bf16[128,4096]{1,0:T(8,128)(2,1)}, bf16[128,4096]{1,0:T(8,128)(2,1)S(1)}, u32[]{:S(2)}, u32[]{:S(2)}) collective-permute-start(bf16[128,4096]{1,0:T(8,128)(2,1)} %bitcast.87), channel_id=1, source_target_pairs={{0,15},{1,14},{2,13},{3,12},{4,11},{5,10},{6,9},{7,8},{8,7},{9,6},... | collective-permute-start | bytes 3145736 | tf_op jit(solution)/shard_map/ppermute | solution.py:85
  7.6 3.3 %copy-start.3 = (bf16[1,128,4096]{2,1,0:T(8,128)(2,1)S(1)}, bf16[1,128,4096]{2,1,0:T(8,128)(2,1)}, u32[]{:S(2)}) copy-start(bf16[1,128,4096]{2,1,0:T(8,128)(2,1)} %param.8) | copy-start | bytes 3145732
  7.6 3.3 %copy-start.5 = (f32[1,4096]{1,0:T(1,128)S(1)}, f32[1,4096]{1,0:T(1,128)}, u32[]{:S(2)}) copy-start(f32[1,4096]{1,0:T(1,128)} %param.11) | copy-start | bytes 49156
  11.4 1.6 %copy-start.1 = (bf16[1,256,4096]{2,1,0:T(8,128)(2,1)S(1)}, bf16[1,256,4096]{2,1,0:T(8,128)(2,1)}, u32[]{:S(2)}) copy-start(bf16[1,256,4096]{2,1,0:T(8,128)(2,1)} %param.14) | copy-start | bytes 6291460
  14.5 56.7 %collective-permute-start = (bf16[1,128,4096]{2,1,0:T(8,128)(2,1)}, bf16[1,128,4096]{2,1,0:T(8,128)(2,1)}, u32[]{:S(2)}, u32[]{:S(2)}) collective-permute-start(bf16[1,128,4096]{2,1,0:T(8,128)(2,1)} %fusion.4), channel_id=1, source_target_pairs={{0,1},{1,2},{2,3},{3,4},{4,5},{6,7},{7,8},{8,9},{9,10},{10,11},{12... | collective-permute-start | bytes 3145736 | tf_op jit(solution)/shard_map/ppermute | solution.py:75
  61.3 1.6 %copy-start.4 = (bf16[1,4096,256]{2,1,0:T(8,128)(2,1)S(1)}, bf16[1,4096,256]{2,1,0:T(8,128)(2,1)}, u32[]{:S(2)}) copy-start(bf16[1,4096,256]{2,1,0:T(8,128)(2,1)} %param.12) | copy-start | bytes 6291460
  66.0 1.2 %copy-start.2 = (bf16[1,128,4096]{2,1,0:T(8,128)(2,1)S(1)}, bf16[1,128,4096]{2,1,0:T(8,128)(2,1)}, u32[]{:S(2)}) copy-start(bf16[1,128,4096]{2,1,0:T(8,128)(2,1)} %param.10) | copy-start | bytes 3145732
  68.9 16.3 %collective-permute-start.3 = (bf16[1,128,4096]{2,1,0:T(8,128)(2,1)}, bf16[1,128,4096]{2,1,0:T(8,128)(2,1)S(1)}, u32[]{:S(2)}, u32[]{:S(2)}) collective-permute-start(bf16[1,128,4096]{2,1,0:T(8,128)(2,1)} %fusion.36), channel_id=1, source_target_pairs={{1,0},{2,1},{3,2},{4,3},{5,4},{6,5},{7,6},{8,7},{9,8},{10,9},{11,1... | collective-permute-start | bytes 3145736 | tf_op jit(solution)/shard_map/ppermute | solution.py:12
  73.5 15.2 %collective-permute-start.1 = (bf16[1,128,4096]{2,1,0:T(8,128)(2,1)}, bf16[1,128,4096]{2,1,0:T(8,128)(2,1)}, u32[]{:S(2)}, u32[]{:S(2)}) collective-permute-start(bf16[1,128,4096]{2,1,0:T(8,128)(2,1)} %broadcast_select_fusion), channel_id=1, source_target_pairs={{5,6},{15,12},{14,15},{21,22},{31,28},{30,31}} | collective-permute-start | bytes 3145736 | tf_op jit(solution)/shard_map/ppermute | solution.py:77
